TPU v7x, 256 devices: a whole 4x4x8 slice. The times are simulated.
256 devices in a mesh: seq: 16 (over y_lo, z), tm: 8 (over x, core), dp: 2 (over y_hi).
Axes of the slice: x: 4, y: 4 (y_hi: 2, y_lo: 2; y = y_hi * 2 + y_lo), z: 8, core: 2. Of those that a mesh axis runs over, the one named last changes fastest.
Arguments:
- queries: bfloat16 [16384, 8, 128], P(('dp', 'seq'), 'tm'), parts along dimension 0, may hold values from -6 to 6
- keys: bfloat16 [16384, 8, 128], P(('dp', 'seq'), 'tm'), parts along dimension 0, may hold values from -6 to 6
- values: bfloat16 [16384, 8, 128], P(('dp', 'seq'), 'tm'), parts along dimension 0, may hold values from -6 to 6
- token_cell: int32 [512], P('seq'), may hold values from 0 to 511, each once
- head_weight: bfloat16 [8, 128, 384], P('tm'), may hold values from -2 to 2
- norm_gain: float32 [384], replicated, may hold values from 0.1 to 1.9
- time_weight: bfloat16 [3, 384, 768], replicated, may hold values from -0.1875 to 0.1875
- frame_clip: int32 [32], P('dp'), parts along dimension 0, may hold values from 0 to 2, never falling along the last dimension, each value on 1 to 8 neighbouring positions
- cotangent: bfloat16 [32, 512, 768], P(('dp', 'tm'), 'seq'), parts along dimension 0, may hold values from -6 to 6
Outputs:
- grad_queries: bfloat16 [16384, 8, 128], P(('dp', 'seq'), 'tm'), parts along dimension 0
- grad_keys: bfloat16 [16384, 8, 128], P(('dp', 'seq'), 'tm'), parts along dimension 0
- grad_values: bfloat16 [16384, 8, 128], P(('dp', 'seq'), 'tm'), parts along dimension 0
There are 2 independent parts, one for each index of `dp`. A program takes and returns all parts, laid end to end along the dimension named above; an argument that names none is the same for every part. Nothing has to cross between parts.
Inputs may be any that keep to these rules, and one draw needn't show every extreme that they name: `token_cell`: a permutation of the 512 cells. `frame_clip`: never falls along the frames.
All inputs are finite; a program needn't handle non-finite values.
Results may differ from a plain program's by a relative error of at most 0.023.
Values may be sent and summed in bfloat16 or wider, within the bound.
No kernel may reach another device: no remote copies, remote signals or barrier semaphores. Data moves between devices by JAX's collectives and lax.ppermute only.
A program may use at most 64 MiB of HBM per device.

v0:
```python
import math

import jax
import jax.numpy as jnp
from jax import lax
from jax.sharding import PartitionSpec as P

HD = 128
GRID_W = 32


def shifted(value, axis, steps):
    count = lax.axis_size(axis)
    initial, last = (max(0, -steps), min(count, count - steps))
    return lax.ppermute(value, axis, [(source, source + steps) for source in range(initial, last)])


def frequencies(pair_count):
    return 1.0 / 10000.0 ** (jnp.arange(pair_count, dtype=jnp.float32) / pair_count)


def rope_tables(frame_pos, cell_ids):
    pair_count = HD // 2
    part_side = pair_count // 3
    part_time = pair_count - 2 * part_side
    grid_row = (cell_ids // GRID_W).astype(jnp.float32)
    grid_col = (cell_ids % GRID_W).astype(jnp.float32)
    angles = jnp.concatenate(
        [
            frame_pos.astype(jnp.float32)[:, None] * frequencies(part_time)[None, :],
            grid_row[:, None] * frequencies(part_side)[None, :],
            grid_col[:, None] * frequencies(part_side)[None, :],
        ],
        axis=1,
    )
    return (jnp.cos(angles), jnp.sin(angles))


def rotate(vectors, cos_table, sin_table, direction):
    layout = vectors.shape
    paired = vectors.reshape(layout[:-1] + (layout[-1] // 2, 2))
    former = paired[..., 0]
    latter = paired[..., 1]
    out_former = former * cos_table - direction * latter * sin_table
    out_latter = direction * former * sin_table + latter * cos_table
    return jnp.stack([out_former, out_latter], axis=-1).reshape(layout)


def tap_mask(frame_clip):
    frame_total = frame_clip.shape[0]
    frame_ids = jnp.arange(frame_total, dtype=jnp.int32)
    columns = []
    for offset in range(3):
        target = frame_ids + offset
        inside = target < frame_total
        same_clip = frame_clip[jnp.minimum(target, frame_total - 1)] == frame_clip
        columns.append(jnp.logical_and(inside, same_clip).astype(jnp.float32))
    return jnp.stack(columns, axis=1)


def cross(left, right):
    return lax.dot_general(
        left, right, (((1,), (1,)), ((), ())), preferred_element_type=jnp.float32
    )


def inner(left, right):
    return lax.dot_general(
        left, right, (((0,), (0,)), ((), ())), preferred_element_type=jnp.float32
    )


def on_device(
    queries, keys, values, token_cell, head_weight, norm_gain, time_weight, frame_clip, cotangent
):
    score_scale = HD ** (-0.5)
    tok_local = queries.shape[0]
    slab_cells = token_cell.shape[0]
    span_frames = cotangent.shape[0]
    channels = head_weight.shape[2]
    frame_pos = jnp.arange(tok_local, dtype=jnp.int32) // slab_cells
    cell_ids = jnp.tile(token_cell, tok_local // slab_cells)
    cos_table, sin_table = rope_tables(frame_pos, cell_ids)
    rot_q = rotate(queries[:, 0, :].astype(jnp.float32), cos_table, sin_table, 1.0).astype(
        jnp.bfloat16
    )
    rot_k = rotate(keys[:, 0, :].astype(jnp.float32), cos_table, sin_table, 1.0).astype(
        jnp.bfloat16
    )
    plain_v = values[:, 0, :]
    keys_all, values_all = (
        lax.all_gather(rot_k, "seq", axis=0, tiled=True),
        lax.all_gather(plain_v, "seq", axis=0, tiled=True),
    )
    total_tokens = keys_all.shape[0]
    key_block = math.gcd(total_tokens, 1024)
    block_count = total_tokens // key_block

    def forward_step(block_id, state):
        running_top, running_total, running_sum = state
        key_piece = lax.dynamic_slice_in_dim(keys_all, block_id * key_block, key_block, 0)
        value_piece = lax.dynamic_slice_in_dim(values_all, block_id * key_block, key_block, 0)
        scores = cross(rot_q, key_piece) * score_scale
        new_top = jnp.maximum(running_top, jnp.max(scores, axis=1))
        factor = jnp.exp(running_top - new_top)
        weights = jnp.exp(scores - new_top[:, None])
        running_total = running_total * factor + jnp.sum(weights, axis=1)
        running_sum = running_sum * factor[:, None] + jnp.dot(
            weights.astype(jnp.bfloat16), value_piece, preferred_element_type=jnp.float32
        )
        return (new_top, running_total, running_sum)

    start_state = (
        jnp.full((tok_local,), -1e30, jnp.float32),
        jnp.zeros((tok_local,), jnp.float32),
        jnp.zeros((tok_local, HD), jnp.float32),
    )
    row_top, row_total, summed = lax.fori_loop(0, block_count, forward_step, start_state)
    attended = (summed / row_total[:, None]).astype(jnp.bfloat16)
    log_total = row_top + jnp.log(row_total)
    span_rows = span_frames * slab_cells
    mixed = (
        lax.psum_scatter(
            jnp.dot(attended, head_weight[0], preferred_element_type=jnp.float32).astype(
                jnp.bfloat16
            ),
            "tm",
            scatter_dimension=0,
            tiled=True,
        )
        .astype(jnp.float32)
        .reshape(span_frames, slab_cells, channels)
    )
    inverse = lax.rsqrt(jnp.mean(mixed * mixed, axis=2, keepdims=True) + 1e-06)
    normed = mixed * inverse * norm_gain
    mask_table = tap_mask(frame_clip)
    first_frame = lax.axis_index("tm") * span_frames
    local_mask = lax.dynamic_slice_in_dim(mask_table, first_frame, span_frames, 0)
    following = shifted(cotangent, "tm", -1)
    extended = jnp.concatenate([cotangent, following], axis=0)
    grad_act = jnp.zeros((span_frames, slab_cells, channels), jnp.float32)
    for offset in range(3):
        term = jnp.einsum(
            "fco,io->fci",
            extended[offset : offset + span_frames],
            time_weight[offset],
            preferred_element_type=jnp.float32,
        )
        grad_act = grad_act + local_mask[:, offset][:, None, None] * term
    sigmoid_n = jax.nn.sigmoid(normed)
    grad_normed = grad_act * sigmoid_n * (1.0 + normed * (1.0 - sigmoid_n))
    gained = grad_normed * norm_gain
    grad_mixed = (
        inverse * gained
        - inverse * inverse * inverse * mixed * jnp.mean(gained * mixed, axis=2, keepdims=True)
    ).astype(jnp.bfloat16)
    grad_mixed = grad_mixed.reshape(span_rows, channels)
    grad_out = cross(lax.all_gather(grad_mixed, "tm", axis=0, tiled=True), head_weight[0]).astype(
        jnp.bfloat16
    )
    row_delta = jnp.sum(grad_out.astype(jnp.float32) * attended.astype(jnp.float32), axis=1)

    def score_block(block_id):
        key_piece = lax.dynamic_slice_in_dim(keys_all, block_id * key_block, key_block, 0)
        value_piece = lax.dynamic_slice_in_dim(values_all, block_id * key_block, key_block, 0)
        scores = cross(rot_q, key_piece) * score_scale
        weights = jnp.exp(scores - log_total[:, None])
        grad_w = cross(grad_out, value_piece)
        grad_s = (weights * (grad_w - row_delta[:, None])).astype(jnp.bfloat16)
        return (key_piece, weights, grad_s)

    def query_step(block_id, grad_q):
        key_piece, weights, grad_s = score_block(block_id)
        return grad_q + jnp.dot(grad_s, key_piece, preferred_element_type=jnp.float32) * score_scale

    grad_q = lax.fori_loop(0, block_count, query_step, jnp.zeros((tok_local, HD), jnp.float32))
    fold_start = (jnp.zeros((tok_local, HD), jnp.float32), jnp.zeros((tok_local, HD), jnp.float32))
    wide_q = rot_q.astype(jnp.float32)
    wide_grad = grad_out.astype(jnp.float32)
    piece_q = lax.all_gather(wide_q, "seq", axis=0, tiled=True)
    piece_grad = lax.all_gather(wide_grad, "seq", axis=0, tiled=True)
    piece_log = lax.all_gather(log_total, "seq", axis=0, tiled=True)
    piece_delta = lax.all_gather(row_delta, "seq", axis=0, tiled=True)
    piece_count = piece_q.shape[0]
    sub_rows = math.gcd(piece_count, 1024)

    def sub_step(sub_id, inner_carry):
        grad_k, grad_v = inner_carry
        offset = sub_id * sub_rows
        query_block = lax.dynamic_slice_in_dim(piece_q, offset, sub_rows, 0).astype(jnp.bfloat16)
        grad_rows = lax.dynamic_slice_in_dim(piece_grad, offset, sub_rows, 0).astype(jnp.bfloat16)
        log_block = lax.dynamic_slice_in_dim(piece_log, offset, sub_rows, 0)
        delta_block = lax.dynamic_slice_in_dim(piece_delta, offset, sub_rows, 0)
        scores = cross(query_block, rot_k) * score_scale
        weights = jnp.exp(scores - log_block[:, None])
        grad_w = cross(grad_rows, plain_v)
        grad_s = (weights * (grad_w - delta_block[:, None])).astype(jnp.bfloat16)
        grad_k = grad_k + inner(grad_s, query_block) * score_scale
        grad_v = grad_v + inner(weights.astype(jnp.bfloat16), grad_rows)
        return (grad_k, grad_v)

    grad_k, grad_v = lax.fori_loop(0, piece_count // sub_rows, sub_step, fold_start)
    grad_queries = rotate(grad_q, cos_table, sin_table, -1.0).astype(jnp.bfloat16)[:, None, :]
    grad_keys = rotate(grad_k, cos_table, sin_table, -1.0).astype(jnp.bfloat16)[:, None, :]
    grad_values = grad_v.astype(jnp.bfloat16)[:, None, :]
    return (grad_queries, grad_keys, grad_values)


def solution(mesh):
    in_specs = (
        P(("dp", "seq"), "tm", None),
        P(("dp", "seq"), "tm", None),
        P(("dp", "seq"), "tm", None),
        P("seq"),
        P("tm", None, None),
        P(),
        P(),
        P("dp"),
        P(("dp", "tm"), "seq", None),
    )
    out_specs = (
        P(("dp", "seq"), "tm", None),
        P(("dp", "seq"), "tm", None),
        P(("dp", "seq"), "tm", None),
    )
    return jax.shard_map(
        on_device, mesh=mesh, in_specs=in_specs, out_specs=out_specs, check_vma=False
    )
```

profile of v0, /device:TPU:2, one launch (start us, length us, event | category | flops | bytes accessed | tf_op | source)
XLA Modules:
  0.0 426.3 jit_solution(6514035259708986628)
XLA Ops:
  9.4 1.0 copy.50
  13.6 73.2 %all-gather.8.cloned.1.call-done = bf16[8192,128]{0,1:T(8,128)(2,1)} async-done(((bf16[512,128]{0,1:T(8,128)(2,1)}), bf16[8192,128]{0,1:T(8,128)(2,1)}) %all-gather.8.cloned.1.call-update) | async-done | bytes 2097168 | tf_op jit(solution)/shard_map/all_gather | solution.py:92
  86.8 4.1 copy.61
  90.9 66.2 %all-gather.14.cloned.1.call-done = bf16[8192,1,128]{2,0,1:T(8,128)(2,1)} async-done(((bf16[512,1,128]{2,0,1:T(8,128)(2,1)}), bf16[8192,1,128]{2,0,1:T(8,128)(2,1)}) %all-gather.14.cloned.1.call-update) | async-done | bytes 2097168 | tf_op jit(solution)/shard_map/all_gather | solution.py:93
  157.2 26.8 %while.48 = (s32[]{:T(128)}, f32[512]{0:T(512)S(1)}, f32[512]{0:T(512)S(1)}, f32[512,128]{1,0:T(8,128)S(1)}, bf16[8192,128]{1,0:T(8,128)(2,1)}, /*index=5*/bf16[...) while((s32[]{:T(128)}, f32[512]{0:T(512)S(1)}, ...), condition=%wide.region_3.4_spmd.clone, body=%wide.region_0.3_spmd.clone.sunk | while | flops 272828928 | bytes 7504047 | solution.py:118
  157.2 1.4 multiply_reduce_fusion.5
  159.0 1.5 convolution_add_fusion.4
  160.5 1.4 multiply_reduce_fusion.5
  162.4 1.5 convolution_add_fusion.4
  163.9 1.4 multiply_reduce_fusion.5
  165.7 1.5 convolution_add_fusion.4
  167.2 1.4 multiply_reduce_fusion.5
  169.1 1.5 convolution_add_fusion.4
  170.6 1.4 multiply_reduce_fusion.5
  172.4 1.5 convolution_add_fusion.4
  173.9 1.4 multiply_reduce_fusion.5
  175.8 1.5 convolution_add_fusion.4
  177.3 1.4 multiply_reduce_fusion.5
  179.1 1.5 convolution_add_fusion.4
  180.6 1.4 multiply_reduce_fusion.5
  182.5 1.5 convolution_add_fusion.4
  184.2 1.1 convolution_convert_fusion
  185.9 1.9 collective-permute-start
  190.8 34.3 %all-gather.1 = f32[16,1,512]{2,1,0:T(1,128)} all-gather(f32[1,1,512]{2,1,0:T(1,128)S(1)} %bitcast.108), channel_id=1, replica_groups=mesh['seq'=16,'tm'=8,'dp'=2] {'seq'}, dimensions={0}, use_global_device_ids=true | all-gather | bytes 34816 | tf_op jit(solution)/shard_map/all_gather | solution.py:182
  228.3 13.0 %all_gather.23 = bf16[512,384]{1,0:T(8,128)(2,1)S(1)} all-gather(bf16[64,384]{1,0:T(8,128)(2,1)S(1)} %bitcast.103), channel_id=1, replica_groups=mesh['seq'=16,'tm'=8,'dp'=2] {'tm'}, dimensions={0}, use_global_device_ids=true | all-gather | bytes 442368 | tf_op jit(solution)/shard_map/all_gather | solution.py:158
  242.9 35.1 %while.49 = (s32[]{:T(128)}, f32[512,128]{1,0:T(8,128)}, bf16[8192,128]{1,0:T(8,128)(2,1)}, bf16[512,128]{1,0:T(8,128)(2,1)S(1)}, f32[512]{0:T(512)}, /*index=5*...) while((s32[]{:T(128)}, f32[512,128]{1,0:T(8,128)}, ...), condition=%wide.region_9.10_spmd.clone, body=%wide.region_8.9_spmd.clone.sunk | while | flops 405471232 | bytes 7886624 | solution.py:176
  242.9 1.4 fusion.121
  244.4 2.2 fusion.122
  247.3 1.4 fusion.121
  248.8 2.2 fusion.122
  251.7 1.4 fusion.121
  253.1 2.2 fusion.122
  256.0 1.4 fusion.121
  257.5 2.2 fusion.122
  260.4 1.4 fusion.121
  261.9 2.2 fusion.122
  264.8 1.4 fusion.121
  266.3 2.2 fusion.122
  269.2 1.4 fusion.121
  270.6 2.2 fusion.122
  273.6 1.4 fusion.121
  275.0 2.2 fusion.122
  277.9 1.1 copy.64
  279.2 32.2 %all-gather.2 = f32[16,1,512]{2,1,0:T(1,128)} all-gather(f32[1,1,512]{2,1,0:T(1,128)} %bitcast.109), channel_id=1, replica_groups=mesh['seq'=16,'tm'=8,'dp'=2] {'seq'}, dimensions={0}, use_global_device_ids=true | all-gather | bytes 34816 | tf_op jit(solution)/shard_map/all_gather | solution.py:183
  312.2 47.2 %all-gather.12.cloned.1.call-done = bf16[8192,128]{0,1:T(8,128)(2,1)} async-done(((bf16[512,128]{0,1:T(8,128)(2,1)}), bf16[8192,128]{0,1:T(8,128)(2,1)}) %all-gather.12.cloned.1.call-update) | async-done | bytes 2097168 | tf_op jit(solution)/shard_map/all_gather | solution.py:181
  359.4 54.8 %while.50 = (s32[]{:T(128)}, f32[512,128]{1,0:T(8,128)}, f32[512,128]{1,0:T(8,128)S(1)}, bf16[8192,128]{0,1:T(8,128)(2,1)}, bf16[512,128]{1,0:T(8,128)(2,1)S(1)}...) while((s32[]{:T(128)}, f32[512,128]{1,0:T(8,128)}, ...), condition=%wide.region_11.12_spmd.clone, body=%wide.region_10.11_spmd.clone.sunk | while | flops 541392896 | bytes 11301086 | solution.py:202
  359.4 1.1 constant_dynamic-slice_fusion.4
  363.5 2.0 fusion.131
  365.4 1.1 constant_dynamic-slice_fusion.4
  369.5 2.9 fusion.131
  372.4 1.1 constant_dynamic-slice_fusion.4
  376.4 2.9 fusion.131
  379.3 1.1 constant_dynamic-slice_fusion.4
  383.4 2.9 fusion.131
  386.3 1.1 constant_dynamic-slice_fusion.4
  390.4 2.9 fusion.131
  393.3 1.1 constant_dynamic-slice_fusion.4
  397.3 2.9 fusion.131
  400.2 1.1 constant_dynamic-slice_fusion.4
  404.3 2.9 fusion.131
  407.2 1.1 constant_dynamic-slice_fusion.4
  411.3 2.9 fusion.131
  414.2 1.1 copy.71
  415.6 1.5 subtract_convert_fusion
  (266 shorter events, 50.4 us)
Async XLA Ops:
  7.2 177.0 %copy-start = (bf16[1,128,384]{2,1,0:T(8,128)(2,1)S(1)}, bf16[1,128,384]{2,1,0:T(8,128)(2,1)}, u32[]{:S(2)}) copy-start(bf16[1,128,384]{2,1,0:T(8,128)(2,1)} %param.19) | copy-start | bytes 294916
  7.2 79.6 %all-gather.8.cloned.1.call-start = ((), (), s32[]{:S(2)}) async-start(), calls=%async_computation.1 | async-start | bytes 2228224 | tf_op jit(solution)/shard_map/all_gather | solution.py:92
  10.9 80.0 %copy-start.6 = (f32[512,21,1]{0,1,2:T(8,128)}, f32[512,21,1]{0,1,2:T(8,128)S(1)}, u32[]{:S(2)}) copy-start(f32[512,21,1]{0,1,2:T(8,128)S(1)} %get-tuple-element.690) | copy-start | bytes 129028
  10.9 80.0 %copy-start.7 = (f32[512,21,1]{0,1,2:T(8,128)}, f32[512,21,1]{0,1,2:T(8,128)S(1)}, u32[]{:S(2)}) copy-start(f32[512,21,1]{0,1,2:T(8,128)S(1)} %get-tuple-element.691) | copy-start | bytes 129028
  12.4 144.8 %all-gather.14.cloned.1.call-start = ((), (), s32[]{:S(2)}) async-start(), calls=%async_computation.5 | async-start | bytes 2228224 | tf_op jit(solution)/shard_map/all_gather | solution.py:93
  13.2 212.0 %reduce-scatter.2.cloned.1.call-start = ((), (), s32[]{:S(2)}) async-start(), calls=%async_computation.2 | async-start | bytes 442368 | tf_op jit(solution)/shard_map/reduce_scatter | solution.py:123
  13.4 77.5 %copy-start.2 = (bf16[512,128]{0,1:T(8,128)(2,1)}, bf16[512,128]{0,1:T(8,128)(2,1)S(1)}, u32[]{:S(2)}) copy-start(bf16[512,128]{0,1:T(8,128)(2,1)S(1)} %convert_element_type.145) | copy-start | bytes 393220
  184.0 6.8 %copy-start.12 = (f32[512]{0:T(512)}, f32[512]{0:T(512)S(1)}, u32[]{:S(2)}) copy-start(f32[512]{0:T(512)S(1)} %get-tuple-element.424) | copy-start | bytes 6148
  184.0 1.9 copy-start.11
  184.0 3.9 copy-start.1
  184.0 6.0 %copy-start.4 = (bf16[3,384,768]{2,1,0:T(8,128)(2,1)S(1)}, bf16[3,384,768]{2,1,0:T(8,128)(2,1)}, u32[]{:S(2)}) copy-start(bf16[3,384,768]{2,1,0:T(8,128)(2,1)} %param.21) | copy-start | bytes 5308420
  184.2 6.2 %copy-start.3 = (bf16[512,128]{0,1:T(8,128)(2,1)S(1)}, bf16[512,128]{0,1:T(8,128)(2,1)}, u32[]{:S(2)}) copy-start(bf16[512,128]{0,1:T(8,128)(2,1)} %convert_element_type.142) | copy-start | bytes 393220
  185.2 41.8 %copy-start.17 = (f32[384]{0:T(512)S(1)}, f32[384]{0:T(512)}, u32[]{:S(2)}) copy-start(f32[384]{0:T(512)} %param.20) | copy-start | bytes 4612
  185.3 127.0 %all-gather.10.cloned.1.call-start = ((), (), s32[]{:S(2)}) async-start(), calls=%async_computation.3 | async-start | bytes 2228224 | tf_op jit(solution)/shard_map/all_gather | solution.py:180
  185.9 173.5 %all-gather.12.cloned.1.call-start = ((), (), s32[]{:S(2)}) async-start(), calls=%async_computation.4 | async-start | bytes 2228224 | tf_op jit(solution)/shard_map/all_gather | solution.py:181
  185.9 4.6 %collective-permute-start = (bf16[2,32,768]{2,1,0:T(8,128)(2,1)S(1)}, bf16[2,32,768]{2,1,0:T(8,128)(2,1)S(1)}, u32[]{:S(2)}, u32[]{:S(2)}) collective-permute-start(bf16[2,32,768]{2,1,0:T(8,128)(2,1)S(1)} %copy-done.11), channel_id=1, source_target_pairs={{2,0},{4,2},{6,4},{8,6},{10,8},{12,10},{14,12},{3,1},{5,3},{7,5},{... | collective-permute-start | bytes 294920 | tf_op jit(solution)/shard_map/ppermute | solution.py:15
  190.8 36.2 %copy-start.14 = (f32[512]{0:T(512)}, f32[512]{0:T(512)S(1)}, u32[]{:S(2)}) copy-start(f32[512]{0:T(512)S(1)} %log_add_fusion) | copy-start | bytes 6148
  190.8 50.5 %copy-start.13 = (f32[512]{0:T(512)S(1)}, f32[512]{0:T(512)}, u32[]{:S(2)}) copy-start(f32[512]{0:T(512)} %copy-done.12) | copy-start | bytes 6148
  242.2 0.7 copy-start.5
  242.9 1.5 copy-start.8
  242.9 1.5 copy-start.15
  242.9 1.5 copy-start.16
  246.6 0.7 copy-start.9
  247.3 1.4 copy-start.8
  247.3 1.4 copy-start.15
  247.3 1.5 copy-start.16
  250.9 0.7 copy-start.9
  251.7 1.4 copy-start.8
  251.7 1.4 copy-start.15
  251.7 1.5 copy-start.16
  255.3 0.7 copy-start.9
  256.0 1.4 copy-start.8
  256.0 1.4 copy-start.15
  256.0 1.5 copy-start.16
  259.7 0.7 copy-start.9
  260.4 1.4 copy-start.8
  260.4 1.4 copy-start.15
  260.4 1.5 copy-start.16
  264.1 0.7 copy-start.9
  264.8 1.4 copy-start.8
  264.8 1.4 copy-start.15
  264.8 1.5 copy-start.16
  268.5 0.7 copy-start.9
  269.2 1.4 copy-start.8
  269.2 1.4 copy-start.15
  269.2 1.5 copy-start.16
  272.8 0.7 copy-start.9
  273.6 1.4 copy-start.8
  273.6 1.4 copy-start.15
  273.6 1.5 copy-start.16
  277.2 0.7 copy-start.9
  361.3 2.2 copy-start.10
  367.3 2.2 copy-start.10
  374.2 2.2 copy-start.10
  381.2 2.2 copy-start.10
  388.2 2.2 copy-start.10
  395.1 2.2 copy-start.10
  402.1 2.2 copy-start.10
  409.1 2.2 copy-start.10
Sparse Core Ops, SparseCore 0:
  12.5 74.2 all-gather.7
  88.6 68.5 all-gather.13
  185.4 28.1 reduce-scatter.1
  215.8 72.9 all-gather.9
  291.1 68.2 all-gather.11
where the time goes:
time: 429 us; the launch traced here: 426 us
  waiting for transfers between devices  188 us (44%)
  matrix products  86.7 us (20%)
  blocking collectives  79.5 us (19%)
  local copies, waits for them, and re-layouts  45.6 us (11%)
  between operations  14.3 us (3%)
  other arithmetic  9.06 us (2%)
    all_gather x1, waiting for transfers between devices, on_device(): lax.all_gather(rot_k, 'seq', axis=0, tiled=True)  73.2 us
    all_gather x1, waiting for transfers between devices, on_device(): lax.all_gather(plain_v, 'seq', axis=0, tiled=True)  66.2 us
    all_gather x1, waiting for transfers between devices, on_device(): piece_grad = lax.all_gather(wide_grad, 'seq', axis=0, tiled=True)  47.2 us
    all_gather x1, blocking collectives, on_device(): piece_log = lax.all_gather(log_total, 'seq', axis=0, tiled=True)  34.3 us
    all_gather x1, blocking collectives, on_device(): piece_delta = lax.all_gather(row_delta, 'seq', axis=0, tiled=True)  32.2 us
    dot_general x16, matrix products, inner(): lax.dot_general(left, right, (((0,), (0,)), ((), ())), preferred_element_...  28.5 us
    dot_general x25, matrix products, cross(): lax.dot_general(left, right, (((1,), (1,)), ((), ())), preferred_element_...  26.9 us
    dot_general x8, matrix products, query_step(): jnp.dot(grad_s, key_piece, preferred_element_type=jnp.float32) * score_scale  17.4 us
  transfers between devices with their start and end apart: 6, of which 3 were waited for; matrix products, arithmetic and copies ran while one was open for 10% of the time, Pallas kernels for 0%

commit v1 on v0

--- a/solution.py
+++ b/solution.py
@@ -58,6 +58,14 @@
     return jnp.stack(columns, axis=1)
 
 
+def split_exact(values):
+    high = lax.reduce_precision(values, exponent_bits=8, mantissa_bits=7)
+    rest = values - high
+    middle = lax.reduce_precision(rest, exponent_bits=8, mantissa_bits=7)
+    low = rest - middle
+    return jnp.stack([high, middle, low]).astype(jnp.bfloat16)
+
+
 def cross(left, right):
     return lax.dot_general(
         left, right, (((1,), (1,)), ((), ())), preferred_element_type=jnp.float32
@@ -88,10 +96,8 @@
         jnp.bfloat16
     )
     plain_v = values[:, 0, :]
-    keys_all, values_all = (
-        lax.all_gather(rot_k, "seq", axis=0, tiled=True),
-        lax.all_gather(plain_v, "seq", axis=0, tiled=True),
-    )
+    pair_all = lax.all_gather(jnp.concatenate([rot_k, plain_v], axis=1), "seq", axis=0, tiled=True)
+    keys_all, values_all = pair_all[:, :HD], pair_all[:, HD:]
     total_tokens = keys_all.shape[0]
     key_block = math.gcd(total_tokens, 1024)
     block_count = total_tokens // key_block
@@ -175,12 +181,24 @@
 
     grad_q = lax.fori_loop(0, block_count, query_step, jnp.zeros((tok_local, HD), jnp.float32))
     fold_start = (jnp.zeros((tok_local, HD), jnp.float32), jnp.zeros((tok_local, HD), jnp.float32))
-    wide_q = rot_q.astype(jnp.float32)
-    wide_grad = grad_out.astype(jnp.float32)
-    piece_q = lax.all_gather(wide_q, "seq", axis=0, tiled=True)
-    piece_grad = lax.all_gather(wide_grad, "seq", axis=0, tiled=True)
-    piece_log = lax.all_gather(log_total, "seq", axis=0, tiled=True)
-    piece_delta = lax.all_gather(row_delta, "seq", axis=0, tiled=True)
+    stat_rows = split_exact(jnp.stack([log_total, row_delta]))
+    stat_rows = stat_rows.reshape(-1, 2 * HD)
+    stat_pad = (-stat_rows.shape[0]) % 16
+    stat_rows = jnp.pad(stat_rows, ((0, stat_pad), (0, 0)))
+    packed = jnp.concatenate([jnp.concatenate([rot_q, grad_out], axis=1), stat_rows], axis=0)
+    block_rows = packed.shape[0]
+    seq_count = lax.axis_size("seq")
+    gathered = lax.all_gather(packed, "seq", axis=0, tiled=True).reshape(
+        seq_count, block_rows, 2 * HD
+    )
+    body_rows = gathered[:, :tok_local, :].reshape(seq_count * tok_local, 2 * HD)
+    piece_q = body_rows[:, :HD]
+    piece_grad = body_rows[:, HD:]
+    stat_all = gathered[:, tok_local:, :].reshape(seq_count, -1)[:, : 6 * tok_local]
+    stat_all = stat_all.reshape(seq_count, 3, 2, tok_local).astype(jnp.float32)
+    stat_all = (stat_all[:, 0] + stat_all[:, 1]) + stat_all[:, 2]
+    piece_log = stat_all[:, 0, :].reshape(-1)
+    piece_delta = stat_all[:, 1, :].reshape(-1)
     piece_count = piece_q.shape[0]
     sub_rows = math.gcd(piece_count, 1024)
 

time: 429 us -> 319 us (0.74)
  blocking collectives: 79.5 us -> 13.6 us
  waiting for transfers between devices: 188 us -> 151 us
  local copies, waits for them, and re-layouts: 45.6 us -> 28.1 us
  matrix products: 86.7 us -> 97.2 us
    all_gather x2 -> x0, blocking collectives: 66.5 us -> none  [the longest x1 34.3 us: on_device(): piece_log = lax.all_gather(log_total, 'seq', axis=0, tiled=True)]
    all_gather x4 -> x2, waiting for transfers between devices: 187 us -> 124 us  [the longest x1 74.7 us: on_device(): lax.all_gather(jnp.concatenate([rot_k, plain_v], axis=1), 'seq', axis=0,...]
    reduce_scatter x1, waiting for transfers between devices: 0.01 us -> 27.6 us  [on_device(): lax.psum_scatter(jnp.dot(attended, head_weight[0], preferred_element_type...]
    dynamic_slice x24 -> x0, local copies, waits for them, and re-layouts: 11.2 us -> none  [the longest x16 9.87 us: sub_step(): lax.dynamic_slice_in_dim(piece_grad, offset, sub_rows, 0)]
    slice x0 -> x5, local copies, waits for them, and re-layouts: none -> 9.64 us  [the longest x1 3.99 us: on_device(): keys_all, values_all = (pair_all[:, :HD], pair_all[:, HD:])]
    dot_general x25, matrix products: 26.9 us -> 33.8 us  [cross(): lax.dot_general(left, right, (((1,), (1,)), ((), ())), preferred_element_...]
    while x88 -> x8, local copies, waits for them, and re-layouts: 5.89 us -> 0.02 us
    dynamic_slice x8, local copies, waits for them, and re-layouts: 5.75 us -> 0.07 us  [sub_step(): log_block = lax.dynamic_slice_in_dim(piece_log, offset, sub_rows, 0)]
  transfers between devices with their start and end apart: 6 -> 4, of which waited for: 3 -> 3; matrix products, arithmetic and copies ran while one was open for 10% -> 22% of each run, Pallas kernels for 0% -> 0%
where the time goes in v1:
time: 319 us; the launch traced here: 316 us
  waiting for transfers between devices  151 us (47%)
  matrix products  97.2 us (30%)
  local copies, waits for them, and re-layouts  28.1 us (9%)
  between operations  14.3 us (4%)
  blocking collectives  13.6 us (4%)
  other arithmetic  8.98 us (3%)
    all_gather x1, waiting for transfers between devices, on_device(): lax.all_gather(jnp.concatenate([rot_k, plain_v], axis=1), 'seq', axis=0,...  74.7 us
    all_gather x1, waiting for transfers between devices, on_device(): lax.all_gather(packed, 'seq', axis=0, tiled=True)  48.8 us
    dot_general x25, matrix products, cross(): lax.dot_general(left, right, (((1,), (1,)), ((), ())), preferred_element_...  33.8 us
    dot_general x16, matrix products, inner(): lax.dot_general(left, right, (((0,), (0,)), ((), ())), preferred_element_...  32.1 us
    reduce_scatter x1, waiting for transfers between devices, on_device(): lax.psum_scatter(jnp.dot(attended, head_weight[0], preferred_element_type...  27.6 us
    dot_general x8, matrix products, query_step(): jnp.dot(grad_s, key_piece, preferred_element_type=jnp.float32) * score_scale  17.4 us
    all_gather x1, blocking collectives, on_device(): lax.all_gather(grad_mixed, 'tm', axis=0, tiled=True)  13.6 us
    dot_general x8, matrix products, forward_step(): jnp.dot(weights.astype(jnp.bfloat16), value_piece, preferred_element_type...  11.9 us
  transfers between devices with their start and end apart: 4, of which 3 were waited for; matrix products, arithmetic and copies ran while one was open for 22% of the time, Pallas kernels for 0%

profile of v1, /device:TPU:2, one launch (start us, length us, event | category | flops | bytes accessed | tf_op | source)
XLA Modules:
  0.0 316.5 jit_solution(8375542764352756657)
XLA Ops:
  13.6 1.9 collective-permute-start
  18.1 74.7 %all-gather.3.cloned.1.call-done = bf16[8192,256]{0,1:T(8,128)(2,1)} async-done(((bf16[512,256]{0,1:T(8,128)(2,1)}), bf16[8192,256]{0,1:T(8,128)(2,1)}) %all-gather.3.cloned.1.call-update) | async-done | bytes 4194320 | tf_op jit(solution)/shard_map/all_gather | solution.py:99
  92.8 4.0 %fusion.82 = (bf16[8192,128]{0,1:T(8,128)(2,1)}, bf16[8192,128]{0,1:T(8,128)(2,1)S(1)}) fusion(bf16[8192,256]{0,1:T(8,128)(2,1)} %all-gather.3.cloned.1.call-done), kind=kLoop, calls=%fused_computation.159 | loop fusion | bytes 8388608 | tf_op jit(solution)/shard_map/slice | solution.py:100
  96.8 4.1 %copy.110 = bf16[8192,128]{1,0:T(8,128)(2,1)} copy(bf16[8192,128]{0,1:T(8,128)(2,1)} %get-tuple-element.687) | data formatting | bytes 4194304
  100.8 2.5 copy.112
  103.4 26.9 %while.48 = (s32[]{:T(128)}, f32[512]{0:T(512)S(1)}, f32[512]{0:T(512)S(1)}, f32[512,128]{1,0:T(8,128)S(1)}, bf16[8192,128]{1,0:T(8,128)(2,1)}, /*index=5*/bf16[...) while((s32[]{:T(128)}, f32[512]{0:T(512)S(1)}, ...), condition=%wide.region_3.4_spmd.clone, body=%wide.region_0.3_spmd.clone.sunk | while | flops 272828928 | bytes 7504055 | solution.py:124
  103.4 1.5 multiply_reduce_fusion.5
  105.3 1.5 convolution_add_fusion.4
  106.8 1.4 multiply_reduce_fusion.5
  108.7 1.5 convolution_add_fusion.4
  110.2 1.4 multiply_reduce_fusion.5
  112.0 1.5 convolution_add_fusion.4
  113.5 1.4 multiply_reduce_fusion.5
  115.4 1.5 convolution_add_fusion.4
  116.9 1.4 multiply_reduce_fusion.5
  118.7 1.5 convolution_add_fusion.4
  120.3 1.4 multiply_reduce_fusion.5
  122.1 1.5 convolution_add_fusion.4
  123.6 1.4 multiply_reduce_fusion.5
  125.4 1.5 convolution_add_fusion.4
  127.0 1.4 multiply_reduce_fusion.5
  128.8 1.5 convolution_add_fusion.4
  132.2 27.6 %reduce-scatter.2.cloned.1.call-done = bf16[64,384]{1,0:T(8,128)(2,1)} async-done(((bf16[512,384]{1,0:T(8,128)(2,1)}), bf16[64,384]{1,0:T(8,128)(2,1)}) %reduce-scatter.2.cloned.1.call-update) | async-done | bytes 49168 | tf_op jit(solution)/shard_map/reduce_scatter | solution.py:129
  163.0 13.6 %all_gather.10 = bf16[512,384]{1,0:T(8,128)(2,1)S(1)} all-gather(bf16[64,384]{1,0:T(8,128)(2,1)S(1)} %bitcast.102), channel_id=1, replica_groups=mesh['seq'=16,'tm'=8,'dp'=2] {'tm'}, dimensions={0}, use_global_device_ids=true | all-gather | bytes 442368 | tf_op jit(solution)/shard_map/all_gather | solution.py:164
  178.3 28.8 %while.49 = (s32[]{:T(128)}, f32[512,128]{1,0:T(8,128)S(1)}, bf16[8192,128]{1,0:T(8,128)(2,1)}, bf16[512,128]{1,0:T(8,128)(2,1)S(1)}, f32[512]{0:T(512)S(1)}, /*...) while((s32[]{:T(128)}, f32[512,128]{1,0:T(8,128)S(1)}, ...), condition=%wide.region_9.10_spmd.clone, body=%wide.region_8.9_spmd.clone.sunk | while | flops 405471232 | bytes 5772984 | solution.py:182
  179.8 2.2 fusion.128
  183.3 2.2 fusion.128
  185.6 1.4 fusion.127
  186.9 2.2 fusion.128
  189.1 1.4 fusion.127
  190.5 2.2 fusion.128
  194.1 2.2 fusion.128
  197.7 2.2 fusion.128
  201.3 2.2 fusion.128
  203.5 1.4 fusion.127
  204.9 2.2 fusion.128
  207.6 48.8 %all-gather.5.cloned.1.call-done = bf16[8448,256]{1,0:T(8,128)(2,1)} async-done(((bf16[528,256]{1,0:T(8,128)(2,1)}), bf16[8448,256]{1,0:T(8,128)(2,1)}) %all-gather.5.cloned.1.call-update) | async-done | bytes 4325392 | tf_op jit(solution)/shard_map/all_gather | solution.py:191
  257.4 2.5 slice.122
  259.9 2.2 fusion.81
  262.4 43.8 %while.50 = (s32[]{:T(128)}, f32[512,128]{1,0:T(8,128)S(1)}, f32[512,128]{1,0:T(8,128)S(1)}, bf16[8192,128]{1,0:T(8,128)(2,1)}, bf16[512,128]{1,0:T(8,128)(2,1)S...) while((s32[]{:T(128)}, f32[512,128]{1,0:T(8,128)S(1)}, ...), condition=%wide.region_11.12_spmd.clone, body=%wide.region_10.11_spmd.clone.sunk | while | flops 541392896 | bytes 8681165 | solution.py:220
  262.5 1.4 fusion.136
  263.9 2.3 fusion.137
  266.2 1.7 convolution_add_fusion.5
  268.0 1.4 fusion.136
  269.4 2.3 fusion.137
  271.6 1.7 convolution_add_fusion.5
  273.4 1.4 fusion.136
  274.8 2.3 fusion.137
  277.1 1.7 convolution_add_fusion.5
  278.9 1.4 fusion.136
  280.3 2.3 fusion.137
  282.6 1.7 convolution_add_fusion.5
  284.4 1.4 fusion.136
  285.8 2.3 fusion.137
  288.1 1.7 convolution_add_fusion.5
  289.9 1.4 fusion.136
  291.3 2.3 fusion.137
  293.5 1.7 convolution_add_fusion.5
  295.3 1.4 fusion.136
  296.7 2.3 fusion.137
  299.0 1.7 convolution_add_fusion.5
  300.8 1.4 fusion.136
  302.2 2.3 fusion.137
  304.5 1.7 convolution_add_fusion.5
  (158 shorter events, 31.2 us)
Async XLA Ops:
  7.2 123.3 %copy-start = (bf16[1,128,384]{2,1,0:T(8,128)(2,1)S(1)}, bf16[1,128,384]{2,1,0:T(8,128)(2,1)}, u32[]{:S(2)}) copy-start(bf16[1,128,384]{2,1,0:T(8,128)(2,1)} %param.19) | copy-start | bytes 294916
  7.2 85.6 %all-gather.3.cloned.1.call-start = ((), (), s32[]{:S(2)}) async-start(), calls=%async_computation.1 | async-start | bytes 4456448 | tf_op jit(solution)/shard_map/all_gather | solution.py:99
  11.4 2.1 copy-start.4
  11.4 4.1 %copy-start.1 = (s32[16]{0:T(128)S(1)}, s32[16]{0:T(128)}, u32[]{:S(2)}) copy-start(s32[16]{0:T(128)} %param.22) | copy-start | bytes 196
  13.5 146.4 %reduce-scatter.2.cloned.1.call-start = ((), (), s32[]{:S(2)}) async-start(), calls=%async_computation.2 | async-start | bytes 442368 | tf_op jit(solution)/shard_map/reduce_scatter | solution.py:129
  13.6 118.3 %collective-permute-start = (bf16[2,32,768]{2,1,0:T(8,128)(2,1)S(1)}, bf16[2,32,768]{2,1,0:T(8,128)(2,1)S(1)}, u32[]{:S(2)}, u32[]{:S(2)}) collective-permute-start(bf16[2,32,768]{2,1,0:T(8,128)(2,1)S(1)} %copy-done.4), channel_id=1, source_target_pairs={{2,0},{4,2},{6,4},{8,6},{10,8},{12,10},{14,12},{3,1},{5,3},{7,5},{... | collective-permute-start | bytes 294920 | tf_op jit(solution)/shard_map/ppermute | solution.py:15
  103.4 28.2 %copy-start.2 = (bf16[3,384,768]{2,1,0:T(8,128)(2,1)S(1)}, bf16[3,384,768]{2,1,0:T(8,128)(2,1)}, u32[]{:S(2)}) copy-start(bf16[3,384,768]{2,1,0:T(8,128)(2,1)} %param.21) | copy-start | bytes 5308420
  130.3 31.4 %copy-start.5 = (f32[384]{0:T(512)S(1)}, f32[384]{0:T(512)}, u32[]{:S(2)}) copy-start(f32[384]{0:T(512)} %param.20) | copy-start | bytes 4612
  131.5 124.9 %all-gather.5.cloned.1.call-start = ((), (), s32[]{:S(2)}) async-start(), calls=%async_computation.3 | async-start | bytes 4595712 | tf_op jit(solution)/shard_map/all_gather | solution.py:191
  259.9 2.5 copy-start.3
Sparse Core Ops, SparseCore 0:
  13.6 79.0 all-gather.2
  131.6 28.1 reduce-scatter.1
  178.2 78.2 all-gather.4

commit v2 on v1

--- a/solution.py
+++ b/solution.py
@@ -1,12 +1,158 @@
+import functools
 import math
 
 import jax
 import jax.numpy as jnp
 from jax import lax
+from jax.experimental import pallas as pl
+from jax.experimental.pallas import tpu as pltpu
 from jax.sharding import PartitionSpec as P
 
 HD = 128
 GRID_W = 32
+SCALE = HD ** (-0.5)
+
+
+def forward_kernel(key_block, q_ref, kv_ref, out_ref, lse_ref):
+    q = q_ref[...]
+    rows = q.shape[0]
+    steps = kv_ref.shape[0] // key_block
+
+    def body(step, carry):
+        top, total, acc = carry
+        start = pl.multiple_of(step * key_block, key_block)
+        k = kv_ref[pl.ds(start, key_block), :HD]
+        v = kv_ref[pl.ds(start, key_block), HD:]
+        s = lax.dot_general(q, k, (((1,), (1,)), ((), ())), preferred_element_type=jnp.float32) * SCALE
+        new_top = jnp.maximum(top, jnp.max(s, axis=1, keepdims=True))
+        factor = jnp.exp(top - new_top)
+        w = jnp.exp(s - new_top)
+        total = total * factor + jnp.sum(w, axis=1, keepdims=True)
+        acc = acc * factor + jnp.dot(w.astype(jnp.bfloat16), v, preferred_element_type=jnp.float32)
+        return new_top, total, acc
+
+    start_state = (
+        jnp.full((rows, 1), -1e30, jnp.float32),
+        jnp.zeros((rows, 1), jnp.float32),
+        jnp.zeros((rows, HD), jnp.float32),
+    )
+    top, total, acc = lax.fori_loop(0, steps, body, start_state)
+    out_ref[...] = (acc / total).astype(out_ref.dtype)
+    lse_ref[...] = top + jnp.log(total)
+
+
+def attention_forward(q, kv_all, query_block=256, key_block=512):
+    rows = q.shape[0]
+    keys = kv_all.shape[0]
+    cost = pl.CostEstimate(
+        flops=4 * rows * keys * HD, transcendentals=rows * keys, bytes_accessed=2 * HD * (2 * rows + 2 * keys)
+    )
+    return pl.pallas_call(
+        functools.partial(forward_kernel, key_block),
+        grid=(rows // query_block,),
+        in_specs=[
+            pl.BlockSpec((query_block, HD), lambda i: (i, 0)),
+            pl.BlockSpec((keys, 2 * HD), lambda i: (0, 0)),
+        ],
+        out_specs=[
+            pl.BlockSpec((query_block, HD), lambda i: (i, 0)),
+            pl.BlockSpec((query_block, 1), lambda i: (i, 0)),
+        ],
+        out_shape=[
+            jax.ShapeDtypeStruct((rows, HD), jnp.bfloat16),
+            jax.ShapeDtypeStruct((rows, 1), jnp.float32),
+        ],
+        compiler_params=pltpu.CompilerParams(dimension_semantics=("arbitrary",)),
+        cost_estimate=cost,
+    )(q, kv_all)
+
+
+def query_grad_kernel(key_block, q_ref, g_ref, lse_ref, delta_ref, kv_ref, dq_ref):
+    q = q_ref[...]
+    g = g_ref[...]
+    lse = lse_ref[...]
+    delta = delta_ref[...]
+    steps = kv_ref.shape[0] // key_block
+
+    def body(step, acc):
+        start = pl.multiple_of(step * key_block, key_block)
+        k = kv_ref[pl.ds(start, key_block), :HD]
+        v = kv_ref[pl.ds(start, key_block), HD:]
+        s = lax.dot_general(q, k, (((1,), (1,)), ((), ())), preferred_element_type=jnp.float32) * SCALE
+        w = jnp.exp(s - lse)
+        gw = lax.dot_general(g, v, (((1,), (1,)), ((), ())), preferred_element_type=jnp.float32)
+        gs = (w * (gw - delta)).astype(jnp.bfloat16)
+        return acc + jnp.dot(gs, k, preferred_element_type=jnp.float32)
+
+    acc = lax.fori_loop(0, steps, body, jnp.zeros(dq_ref.shape, jnp.float32))
+    dq_ref[...] = acc * SCALE
+
+
+def attention_query_grad(q, g, lse_col, delta_col, kv_all, query_block=256, key_block=512):
+    rows = q.shape[0]
+    keys = kv_all.shape[0]
+    cost = pl.CostEstimate(
+        flops=6 * rows * keys * HD, transcendentals=rows * keys, bytes_accessed=2 * HD * (3 * rows + 2 * keys)
+    )
+    row_spec = pl.BlockSpec((query_block, HD), lambda i: (i, 0))
+    col_spec = pl.BlockSpec((query_block, 1), lambda i: (i, 0))
+    whole = pl.BlockSpec((keys, 2 * HD), lambda i: (0, 0))
+    return pl.pallas_call(
+        functools.partial(query_grad_kernel, key_block),
+        grid=(rows // query_block,),
+        in_specs=[row_spec, row_spec, col_spec, col_spec, whole],
+        out_specs=pl.BlockSpec((query_block, HD), lambda i: (i, 0)),
+        out_shape=jax.ShapeDtypeStruct((rows, HD), jnp.float32),
+        compiler_params=pltpu.CompilerParams(dimension_semantics=("arbitrary",)),
+        cost_estimate=cost,
+    )(q, g, lse_col, delta_col, kv_all)
+
+
+def key_grad_kernel(query_block, block_stride, k_ref, v_ref, qg_ref, lse_ref, delta_ref, dk_ref, dv_ref):
+    k = k_ref[...]
+    v = v_ref[...]
+    steps = lse_ref.shape[1] // query_block
+
+    def body(step, carry):
+        dk, dv = carry
+        start = pl.multiple_of(step * block_stride, 16)
+        column = pl.multiple_of(step * query_block, query_block)
+        q = qg_ref[pl.ds(start, query_block), :HD]
+        g = qg_ref[pl.ds(start, query_block), HD:]
+        lse = lse_ref[:, pl.ds(column, query_block)]
+        delta = delta_ref[:, pl.ds(column, query_block)]
+        s = lax.dot_general(k, q, (((1,), (1,)), ((), ())), preferred_element_type=jnp.float32) * SCALE
+        w = jnp.exp(s - lse)
+        gw = lax.dot_general(v, g, (((1,), (1,)), ((), ())), preferred_element_type=jnp.float32)
+        gs = (w * (gw - delta)).astype(jnp.bfloat16)
+        dk = dk + jnp.dot(gs, q, preferred_element_type=jnp.float32)
+        dv = dv + jnp.dot(w.astype(jnp.bfloat16), g, preferred_element_type=jnp.float32)
+        return dk, dv
+
+    zero = jnp.zeros(dk_ref.shape, jnp.float32)
+    dk, dv = lax.fori_loop(0, steps, body, (zero, zero))
+    dk_ref[...] = dk * SCALE
+    dv_ref[...] = dv
+
+
+def attention_key_grad(k, v, qg_all, lse_row, delta_row, query_block, block_stride, key_rows=256):
+    rows = k.shape[0]
+    queries = lse_row.shape[1]
+    cost = pl.CostEstimate(
+        flops=8 * rows * queries * HD, transcendentals=rows * queries, bytes_accessed=2 * HD * (2 * rows + 2 * queries)
+    )
+    row_spec = pl.BlockSpec((key_rows, HD), lambda i: (i, 0))
+    whole = pl.BlockSpec(qg_all.shape, lambda i: (0, 0))
+    stat = pl.BlockSpec((1, queries), lambda i: (0, 0))
+    return pl.pallas_call(
+        functools.partial(key_grad_kernel, query_block, block_stride),
+        grid=(rows // key_rows,),
+        in_specs=[row_spec, row_spec, whole, stat, stat],
+        out_specs=[row_spec, row_spec],
+        out_shape=[jax.ShapeDtypeStruct((rows, HD), jnp.float32)] * 2,
+        compiler_params=pltpu.CompilerParams(dimension_semantics=("arbitrary",)),
+        cost_estimate=cost,
+    )(k, v, qg_all, lse_row, delta_row)
 
 
 def shifted(value, axis, steps):
@@ -97,33 +243,8 @@
     )
     plain_v = values[:, 0, :]
     pair_all = lax.all_gather(jnp.concatenate([rot_k, plain_v], axis=1), "seq", axis=0, tiled=True)
-    keys_all, values_all = pair_all[:, :HD], pair_all[:, HD:]
-    total_tokens = keys_all.shape[0]
-    key_block = math.gcd(total_tokens, 1024)
-    block_count = total_tokens // key_block
-
-    def forward_step(block_id, state):
-        running_top, running_total, running_sum = state
-        key_piece = lax.dynamic_slice_in_dim(keys_all, block_id * key_block, key_block, 0)
-        value_piece = lax.dynamic_slice_in_dim(values_all, block_id * key_block, key_block, 0)
-        scores = cross(rot_q, key_piece) * score_scale
-        new_top = jnp.maximum(running_top, jnp.max(scores, axis=1))
-        factor = jnp.exp(running_top - new_top)
-        weights = jnp.exp(scores - new_top[:, None])
-        running_total = running_total * factor + jnp.sum(weights, axis=1)
-        running_sum = running_sum * factor[:, None] + jnp.dot(
-            weights.astype(jnp.bfloat16), value_piece, preferred_element_type=jnp.float32
-        )
-        return (new_top, running_total, running_sum)
-
-    start_state = (
-        jnp.full((tok_local,), -1e30, jnp.float32),
-        jnp.zeros((tok_local,), jnp.float32),
-        jnp.zeros((tok_local, HD), jnp.float32),
-    )
-    row_top, row_total, summed = lax.fori_loop(0, block_count, forward_step, start_state)
-    attended = (summed / row_total[:, None]).astype(jnp.bfloat16)
-    log_total = row_top + jnp.log(row_total)
+    attended, log_col = attention_forward(rot_q, pair_all)
+    log_total = log_col[:, 0]
     span_rows = span_frames * slab_cells
     mixed = (
         lax.psum_scatter(
@@ -166,21 +287,7 @@
     )
     row_delta = jnp.sum(grad_out.astype(jnp.float32) * attended.astype(jnp.float32), axis=1)
 
-    def score_block(block_id):
-        key_piece = lax.dynamic_slice_in_dim(keys_all, block_id * key_block, key_block, 0)
-        value_piece = lax.dynamic_slice_in_dim(values_all, block_id * key_block, key_block, 0)
-        scores = cross(rot_q, key_piece) * score_scale
-        weights = jnp.exp(scores - log_total[:, None])
-        grad_w = cross(grad_out, value_piece)
-        grad_s = (weights * (grad_w - row_delta[:, None])).astype(jnp.bfloat16)
-        return (key_piece, weights, grad_s)
-
-    def query_step(block_id, grad_q):
-        key_piece, weights, grad_s = score_block(block_id)
-        return grad_q + jnp.dot(grad_s, key_piece, preferred_element_type=jnp.float32) * score_scale
-
-    grad_q = lax.fori_loop(0, block_count, query_step, jnp.zeros((tok_local, HD), jnp.float32))
-    fold_start = (jnp.zeros((tok_local, HD), jnp.float32), jnp.zeros((tok_local, HD), jnp.float32))
+    grad_q = attention_query_grad(rot_q, grad_out, log_col, row_delta[:, None], pair_all)
     stat_rows = split_exact(jnp.stack([log_total, row_delta]))
     stat_rows = stat_rows.reshape(-1, 2 * HD)
     stat_pad = (-stat_rows.shape[0]) % 16
@@ -191,33 +298,20 @@
     gathered = lax.all_gather(packed, "seq", axis=0, tiled=True).reshape(
         seq_count, block_rows, 2 * HD
     )
-    body_rows = gathered[:, :tok_local, :].reshape(seq_count * tok_local, 2 * HD)
-    piece_q = body_rows[:, :HD]
-    piece_grad = body_rows[:, HD:]
     stat_all = gathered[:, tok_local:, :].reshape(seq_count, -1)[:, : 6 * tok_local]
     stat_all = stat_all.reshape(seq_count, 3, 2, tok_local).astype(jnp.float32)
     stat_all = (stat_all[:, 0] + stat_all[:, 1]) + stat_all[:, 2]
     piece_log = stat_all[:, 0, :].reshape(-1)
     piece_delta = stat_all[:, 1, :].reshape(-1)
-    piece_count = piece_q.shape[0]
-    sub_rows = math.gcd(piece_count, 1024)
-
-    def sub_step(sub_id, inner_carry):
-        grad_k, grad_v = inner_carry
-        offset = sub_id * sub_rows
-        query_block = lax.dynamic_slice_in_dim(piece_q, offset, sub_rows, 0).astype(jnp.bfloat16)
-        grad_rows = lax.dynamic_slice_in_dim(piece_grad, offset, sub_rows, 0).astype(jnp.bfloat16)
-        log_block = lax.dynamic_slice_in_dim(piece_log, offset, sub_rows, 0)
-        delta_block = lax.dynamic_slice_in_dim(piece_delta, offset, sub_rows, 0)
-        scores = cross(query_block, rot_k) * score_scale
-        weights = jnp.exp(scores - log_block[:, None])
-        grad_w = cross(grad_rows, plain_v)
-        grad_s = (weights * (grad_w - delta_block[:, None])).astype(jnp.bfloat16)
-        grad_k = grad_k + inner(grad_s, query_block) * score_scale
-        grad_v = grad_v + inner(weights.astype(jnp.bfloat16), grad_rows)
-        return (grad_k, grad_v)
-
-    grad_k, grad_v = lax.fori_loop(0, piece_count // sub_rows, sub_step, fold_start)
+    grad_k, grad_v = attention_key_grad(
+        rot_k,
+        plain_v,
+        gathered.reshape(seq_count * block_rows, 2 * HD),
+        piece_log[None, :],
+        piece_delta[None, :],
+        tok_local,
+        block_rows,
+    )
     grad_queries = rotate(grad_q, cos_table, sin_table, -1.0).astype(jnp.bfloat16)[:, None, :]
     grad_keys = rotate(grad_k, cos_table, sin_table, -1.0).astype(jnp.bfloat16)[:, None, :]
     grad_values = grad_v.astype(jnp.bfloat16)[:, None, :]

time: 319 us -> 270 us (0.85)
  matrix products: 97.2 us -> 3.31 us
  Pallas kernels: 0 us -> 56.3 us
  local copies, waits for them, and re-layouts: 28.1 us -> 14.4 us
  waiting for transfers between devices: 151 us -> 160 us
  other arithmetic: 8.98 us -> 5.72 us
    dot_general x32 -> x0, matrix products: 61.4 us -> none  [the longest x16 32.1 us: inner(): lax.dot_general(left, right, (((0,), (0,)), ((), ())), preferred_element_...]
    pallas_call x0 -> x3, Pallas kernels: none -> 56.3 us  [the longest x1 20.1 us: attention_key_grad(): pl.pallas_call(functools.partial(key_grad_kernel, query_block, block_stri...]
    dot_general x25 -> x1, matrix products: 33.8 us -> 0.35 us  [cross(): lax.dot_general(left, right, (((1,), (1,)), ((), ())), preferred_element_...]
    all_gather x1, waiting for transfers between devices: 48.8 us -> 58.6 us  [on_device(): lax.all_gather(packed, 'seq', axis=0, tiled=True)]
    slice x3 -> x0, local copies, waits for them, and re-layouts: 8.68 us -> none  [the longest x1 3.99 us: on_device(): keys_all, values_all = (pair_all[:, :HD], pair_all[:, HD:])]
    unnamed x21 -> x29, local copies, waits for them, and re-layouts: 9.56 us -> 1.64 us
    reduce_sum x8 -> x0, other arithmetic: 3.21 us -> none  [forward_step(): running_total = running_total * factor + jnp.sum(weights, axis=1)]
  transfers between devices with their start and end apart: 4 -> 4, of which waited for: 3 -> 3; matrix products, arithmetic and copies ran while one was open for 22% -> 3% of each run, Pallas kernels for 0% -> 13%
where the time goes in v2:
time: 270 us
  waiting for transfers between devices  160 us (59%)
  Pallas kernels  56.3 us (21%)
  local copies, waits for them, and re-layouts  14.4 us (5%)
  between operations  14.2 us (5%)
  blocking collectives  13.4 us (5%)
  other arithmetic  5.72 us (2%)
  matrix products  3.31 us (1%)
    all_gather x1, waiting for transfers between devices, on_device(): lax.all_gather(jnp.concatenate([rot_k, plain_v], axis=1), 'seq', axis=0,...  74.2 us
    all_gather x1, waiting for transfers between devices, on_device(): lax.all_gather(packed, 'seq', axis=0, tiled=True)  58.6 us
    reduce_scatter x1, waiting for transfers between devices, on_device(): lax.psum_scatter(jnp.dot(attended, head_weight[0], preferred_element_type...  27.4 us
    pallas_call x1, Pallas kernels, attention_key_grad(): pl.pallas_call(functools.partial(key_grad_kernel, query_block, block_stri...  20.1 us
    pallas_call x1, Pallas kernels, attention_forward(): pl.pallas_call(functools.partial(forward_kernel, key_block), grid=(rows /...  18.5 us
    pallas_call x1, Pallas kernels, attention_query_grad(): pl.pallas_call(functools.partial(query_grad_kernel, key_block), grid=(row...  17.6 us
    all_gather x1, blocking collectives, on_device(): lax.all_gather(grad_mixed, 'tm', axis=0, tiled=True)  13.4 us
  transfers between devices with their start and end apart: 4, of which 3 were waited for; matrix products, arithmetic and copies ran while one was open for 3% of the time, Pallas kernels for 13%

profile of v2, /device:TPU:2, one launch (start us, length us, event | category | flops | bytes accessed | tf_op | source)
XLA Modules:
  0.0 269.6 jit_solution(2145672541263645627)
XLA Ops:
  7.2 0.0 all-gather.3.cloned.1.call-start
  7.3 0.7 tile.4
  7.9 0.1 tile.10
  8.0 1.0 copy.33
  9.0 0.1 reshape.576
  9.2 0.2 fusion.34
  9.4 1.0 copy.29
  10.4 0.1 reshape.575
  10.6 0.2 fusion.35
  10.8 0.1 multiply_bitcast_fusion.2
  10.9 0.1 multiply_bitcast_fusion.1
  11.0 0.5 subtract_convert_fusion.2
  11.5 0.1 copy.36
  11.7 0.1 convert_element_type.108
  11.8 0.1 copy.37.k_ref
  11.9 0.8 pad_maximum_fusion
  12.7 0.0 reduce-scatter.2.cloned.1.call-start
  12.7 1.9 collective-permute-start
  14.7 0.1 copy.32
  14.8 0.1 convert_element_type.105
  14.9 0.8 copy.40.q_ref
  15.7 0.7 gather_fusion
  16.3 0.7 gather_fusion.1
  17.0 0.7 gather_fusion.2
  17.7 74.2 %all-gather.3.cloned.1.call-done.kv_ref = bf16[8192,256]{1,0:T(8,128)(2,1)} async-done(((bf16[512,256]{1,0:T(8,128)(2,1)}), bf16[8192,256]{1,0:T(8,128)(2,1)}) %all-gather.3.cloned.1.call-update) | async-done | bytes 4194320 | tf_op jit(solution)/shard_map/all_gather | solution.py:245
  91.9 18.5 %shard_map.112 = (bf16[512,128]{1,0:T(8,128)(2,1)}, f32[512,1]{1,0:T(8,128)}) custom-call(bf16[512,128]{1,0:T(8,128)(2,1)} %copy.40.q_ref, bf16[8192,256]{1,0:T(8,128)(2,1)} %all-gather.3.cloned.1.call-done.kv_ref), custom_call_target="tpu_custom_call" | custom-call | flops 2147483648 | bytes 4456448 | tf_op jit(solution)/shard_map/pallas_call | solution.py:50
  110.5 1.9 convolution_convert_fusion
  112.4 0.0 reduce-scatter.2.cloned.1.call-update
  112.4 0.0 all-gather.5.cloned.1.call-start
  112.5 0.1 constant_dynamic-slice_fusion
  112.5 0.3 convolution_multiply_fusion.2
  112.9 0.3 convolution_multiply_fusion.1
  113.2 0.1 reduce.1
  113.3 27.4 %reduce-scatter.2.cloned.1.call-done = bf16[64,384]{1,0:T(8,128)(2,1)} async-done(((bf16[512,384]{1,0:T(8,128)(2,1)}), bf16[64,384]{1,0:T(8,128)(2,1)}) %reduce-scatter.2.cloned.1.call-update) | async-done | bytes 49168 | tf_op jit(solution)/shard_map/reduce_scatter | solution.py:250
  140.8 1.0 multiply_reduce_fusion.2
  141.8 0.1 rsqrt.15
  141.8 0.8 convert_element_type.110
  142.7 0.4 multiply_reduce_fusion.1
  143.1 0.1 subtract_convert_fusion.4
  143.2 13.4 %all_gather.10 = bf16[512,384]{1,0:T(8,128)(2,1)S(1)} all-gather(bf16[64,384]{1,0:T(8,128)(2,1)S(1)} %bitcast.83), channel_id=1, replica_groups=mesh['seq'=16,'tm'=8,'dp'=2] {'tm'}, dimensions={0}, use_global_device_ids=true | all-gather | bytes 442368 | tf_op jit(solution)/shard_map/all_gather | solution.py:285
  156.6 0.4 multiply_reduce_fusion
  157.0 0.8 fusion.12
  157.8 0.0 all-gather.5.cloned.1.call-update
  157.8 0.9 copy.41.delta_ref
  158.7 17.6 %shard_map.113 = f32[512,128]{1,0:T(8,128)} custom-call(bf16[512,128]{1,0:T(8,128)(2,1)} %copy.40.q_ref, bf16[512,128]{1,0:T(8,128)(2,1)} %copy-done.6, f32[512,1]{1,0:T(8,128)} %get-tuple-element.8.lse_ref, f32[512,1]{1,0:T(8,128)} %copy.41.delta_ref, bf16[8192,256]{1,0:T(8,128)(2,1)} %all-gather.3.cloned.1.call-done.kv_ref), custom_call_target="tpu_custom_call" | custom-call | flops 3221225472 | bytes 4587520 | tf_op jit(solution)/shard_map/pallas_call | solution.py:100
  176.3 1.1 copy.42
  177.4 0.1 reshape.571
  177.5 0.2 fusion.33
  177.8 58.6 %all-gather.5.cloned.1.call-done.qg_ref = bf16[8448,256]{1,0:T(8,128)(2,1)} async-done(((bf16[528,256]{1,0:T(8,128)(2,1)}), bf16[8448,256]{1,0:T(8,128)(2,1)}) %all-gather.5.cloned.1.call-update) | async-done | bytes 4325392 | tf_op jit(solution)/shard_map/all_gather | solution.py:298
  236.3 0.9 slice.100
  237.3 0.2 reshape.577
  237.6 0.7 fusion.36
  238.2 20.1 %shard_map.114 = (f32[512,128]{1,0:T(8,128)}, f32[512,128]{1,0:T(8,128)}) custom-call(bf16[512,128]{1,0:T(8,128)(2,1)} %copy-done.4, bf16[512,128]{1,0:T(8,128)(2,1)} %bitcast.84, bf16[8448,256]{1,0:T(8,128)(2,1)} %all-gather.5.cloned.1.call-done.qg_ref, f32[1,8192]{1,0:T(1,128)} %bitcast.88, f32[1,8192]{1,0:T(1,128)} %bitcast.87), custom_call_target="tpu_custom_call" | custom-call | flops 4294967296 | bytes 4456448 | tf_op jit(solution)/shard_map/pallas_call | solution.py:147
  258.4 1.1 copy.48
  259.5 0.1 reshape.574
  259.6 0.2 fusion.32
  259.8 0.6 subtract_convert_fusion
  260.4 0.1 copy.51
  260.6 0.1 convert_element_type.119
  260.6 0.8 copy.53
  261.4 0.1 copy.45
  261.6 0.1 convert_element_type.115
  261.6 0.8 copy.52
  262.4 0.7 convert_bitcast_fusion
  (53 shorter events, 0.4 us)
Async XLA Ops:
  7.2 103.3 %copy-start = (bf16[1,128,384]{2,1,0:T(8,128)(2,1)S(1)}, bf16[1,128,384]{2,1,0:T(8,128)(2,1)}, u32[]{:S(2)}) copy-start(bf16[1,128,384]{2,1,0:T(8,128)(2,1)} %param.13) | copy-start | bytes 294916
  7.2 84.7 %all-gather.3.cloned.1.call-start = ((), (), s32[]{:S(2)}) async-start(), calls=%async_computation.1 | async-start | bytes 4456448 | tf_op jit(solution)/shard_map/all_gather | solution.py:245
  10.4 1.5 copy-start.10
  10.6 2.2 copy-start.11
  11.0 4.7 %copy-start.1 = (s32[16]{0:T(128)S(1)}, s32[16]{0:T(128)}, u32[]{:S(2)}) copy-start(s32[16]{0:T(128)} %param.16) | copy-start | bytes 196
  11.9 98.6 %copy-start.4 = (bf16[512,128]{1,0:T(8,128)(2,1)}, bf16[512,128]{1,0:T(8,128)(2,1)S(1)}, u32[]{:S(2)}) copy-start(bf16[512,128]{1,0:T(8,128)(2,1)S(1)} %copy.37.k_ref) | copy-start | bytes 393220
  12.7 128.1 %reduce-scatter.2.cloned.1.call-start = ((), (), s32[]{:S(2)}) async-start(), calls=%async_computation.2 | async-start | bytes 442368 | tf_op jit(solution)/shard_map/reduce_scatter | solution.py:250
  12.7 100.1 %collective-permute-start = (bf16[2,32,768]{2,1,0:T(8,128)(2,1)S(1)}, bf16[2,32,768]{2,1,0:T(8,128)(2,1)S(1)}, u32[]{:S(2)}, u32[]{:S(2)}) collective-permute-start(bf16[2,32,768]{2,1,0:T(8,128)(2,1)S(1)} %copy-done.11), channel_id=1, source_target_pairs={{2,0},{4,2},{6,4},{8,6},{10,8},{12,10},{14,12},{3,1},{5,3},{7,5},{... | collective-permute-start | bytes 294920 | tf_op jit(solution)/shard_map/ppermute | solution.py:161
  17.7 94.8 %copy-start.2 = (bf16[3,384,768]{2,1,0:T(8,128)(2,1)S(1)}, bf16[3,384,768]{2,1,0:T(8,128)(2,1)}, u32[]{:S(2)}) copy-start(bf16[3,384,768]{2,1,0:T(8,128)(2,1)} %param.15) | copy-start | bytes 5308420
  110.4 2.8 %copy-start.9 = (f32[512,1]{1,0:T(8,128)S(1)}, f32[512,1]{1,0:T(8,128)}, u32[]{:S(2)}) copy-start(f32[512,1]{1,0:T(8,128)} %get-tuple-element.8.lse_ref) | copy-start | bytes 6148
  110.4 32.2 %copy-start.12 = (f32[384]{0:T(512)S(1)}, f32[384]{0:T(512)}, u32[]{:S(2)}) copy-start(f32[384]{0:T(512)} %param.14) | copy-start | bytes 4612
  112.4 123.9 %all-gather.5.cloned.1.call-start = ((), (), s32[]{:S(2)}) async-start(), calls=%async_computation.3 | async-start | bytes 4595712 | tf_op jit(solution)/shard_map/all_gather | solution.py:298
  112.9 43.7 %copy-start.3 = (bf16[512,128]{1,0:T(8,128)(2,1)S(1)}, bf16[512,128]{1,0:T(8,128)(2,1)}, u32[]{:S(2)}) copy-start(bf16[512,128]{1,0:T(8,128)(2,1)} %get-tuple-element.7) | copy-start | bytes 393220
  113.2 43.8 %copy-start.5 = (bf16[512,128]{1,0:T(8,128)(2,1)S(1)}, bf16[512,128]{1,0:T(8,128)(2,1)}, u32[]{:S(2)}) copy-start(bf16[512,128]{1,0:T(8,128)(2,1)} %copy.40.q_ref) | copy-start | bytes 393220
  140.8 2.3 copy-start.7
  156.9 1.7 copy-start.6
  259.6 2.8 %copy-start.8 = (f32[512,128]{1,0:T(8,128)S(1)}, f32[512,128]{1,0:T(8,128)}, u32[]{:S(2)}) copy-start(f32[512,128]{1,0:T(8,128)} %get-tuple-element.10) | copy-start | bytes 786436
Sparse Core Ops, SparseCore 0:
  12.8 79.0 all-gather.2
  112.5 28.1 reduce-scatter.1
  157.9 78.3 all-gather.4

commit v3 on v2

--- a/solution.py
+++ b/solution.py
@@ -246,17 +246,15 @@
     attended, log_col = attention_forward(rot_q, pair_all)
     log_total = log_col[:, 0]
     span_rows = span_frames * slab_cells
-    mixed = (
-        lax.psum_scatter(
-            jnp.dot(attended, head_weight[0], preferred_element_type=jnp.float32).astype(
-                jnp.bfloat16
-            ),
-            "tm",
-            scatter_dimension=0,
-            tiled=True,
-        )
-        .astype(jnp.float32)
-        .reshape(span_frames, slab_cells, channels)
+    head_count = lax.axis_size("tm")
+    projected = jnp.dot(attended, head_weight[0], preferred_element_type=jnp.float32).astype(
+        jnp.bfloat16
+    )
+    exchanged = lax.all_to_all(
+        projected.reshape(head_count, span_frames * slab_cells, channels), "tm", 0, 0, tiled=False
+    )
+    mixed = jnp.sum(exchanged.astype(jnp.float32), axis=0).reshape(
+        span_frames, slab_cells, channels
     )
     inverse = lax.rsqrt(jnp.mean(mixed * mixed, axis=2, keepdims=True) + 1e-06)
     normed = mixed * inverse * norm_gain

time: 270 us -> 247 us (0.915)
  waiting for transfers between devices: 160 us -> 134 us
  starting transfers between devices: 2.04 us -> 6.89 us
    reduce_scatter x1 -> x0, waiting for transfers between devices: 27.4 us -> none  [on_device(): lax.psum_scatter(jnp.dot(attended, head_weight[0], preferred_element_type...]
    all_to_all x0 -> x1, waiting for transfers between devices: none -> 6.65 us  [on_device(): lax.all_to_all(projected.reshape(head_count, span_frames * slab_cells, ch...]
    all_gather x1, waiting for transfers between devices: 58.6 us -> 53.6 us  [on_device(): lax.all_gather(packed, 'seq', axis=0, tiled=True)]
    all_to_all x0 -> x1, starting transfers between devices: none -> 4.93 us  [on_device(): lax.all_to_all(projected.reshape(head_count, span_frames * slab_cells, ch...]
  transfers between devices with their start and end apart: 4 -> 4, of which waited for: 3 -> 3; matrix products, arithmetic and copies ran while one was open for 3% -> 3% of each run, Pallas kernels for 13% -> 15%
where the time goes in v3:
time: 247 us; the launch traced here: 246 us
  waiting for transfers between devices  134 us (54%)
  Pallas kernels  56.4 us (23%)
  between operations  14.5 us (6%)
  local copies, waits for them, and re-layouts  14.4 us (6%)
  blocking collectives  12.4 us (5%)
  starting transfers between devices  6.89 us (3%)
  other arithmetic  4.08 us (2%)
  matrix products  3.33 us (1%)
    all_gather x1, waiting for transfers between devices, on_device(): lax.all_gather(jnp.concatenate([rot_k, plain_v], axis=1), 'seq', axis=0,...  74.1 us
    all_gather x1, waiting for transfers between devices, on_device(): lax.all_gather(packed, 'seq', axis=0, tiled=True)  53.6 us
    pallas_call x1, Pallas kernels, attention_key_grad(): pl.pallas_call(functools.partial(key_grad_kernel, query_block, block_stri...  20.1 us
    pallas_call x1, Pallas kernels, attention_forward(): pl.pallas_call(functools.partial(forward_kernel, key_block), grid=(rows /...  18.5 us
    pallas_call x1, Pallas kernels, attention_query_grad(): pl.pallas_call(functools.partial(query_grad_kernel, key_block), grid=(row...  17.7 us
    all_gather x1, blocking collectives, on_device(): lax.all_gather(grad_mixed, 'tm', axis=0, tiled=True)  12.4 us
    all_to_all x1, waiting for transfers between devices, on_device(): lax.all_to_all(projected.reshape(head_count, span_frames * slab_cells, ch...  6.65 us
  transfers between devices with their start and end apart: 4, of which 3 were waited for; matrix products, arithmetic and copies ran while one was open for 3% of the time, Pallas kernels for 15%

profile of v3, /device:TPU:2, one launch (start us, length us, event | category | flops | bytes accessed | tf_op | source)
XLA Modules:
  0.0 246.3 jit_solution(8559511347808288895)
XLA Ops:
  7.2 0.0 copy-start
  7.2 0.0 all-gather.3.cloned.1.call-start
  7.3 0.7 tile.4
  7.9 0.1 tile.10
  8.0 1.0 copy.33
  9.0 0.1 reshape.580
  9.2 0.2 fusion.34
  9.4 1.0 copy.29
  10.4 0.1 reshape.579
  10.6 0.2 fusion.35
  10.8 0.1 multiply_bitcast_fusion.2
  10.9 0.1 multiply_bitcast_fusion.1
  11.0 0.5 subtract_convert_fusion.2
  11.5 0.1 copy.36
  11.7 0.1 convert_element_type.108
  11.7 0.1 copy.37.k_ref
  11.9 0.7 pad_maximum_fusion
  12.6 0.0 all-gather.3.cloned.1.call-update
  12.7 1.9 collective-permute-start
  14.6 0.1 copy.32
  14.7 0.1 convert_element_type.105
  14.8 0.8 copy.40.q_ref
  15.6 0.7 gather_fusion
  16.3 0.7 gather_fusion.1
  17.0 0.7 gather_fusion.2
  17.6 0.1 constant_dynamic-slice_fusion
  17.7 74.1 %all-gather.3.cloned.1.call-done.kv_ref = bf16[8192,256]{1,0:T(8,128)(2,1)} async-done(((bf16[512,256]{1,0:T(8,128)(2,1)}), bf16[8192,256]{1,0:T(8,128)(2,1)}) %all-gather.3.cloned.1.call-update) | async-done | bytes 4194320 | tf_op jit(solution)/shard_map/all_gather | solution.py:245
  91.9 18.5 %shard_map.112 = (bf16[512,128]{1,0:T(8,128)(2,1)}, f32[512,1]{1,0:T(8,128)}) custom-call(bf16[512,128]{1,0:T(8,128)(2,1)} %copy.40.q_ref, bf16[8192,256]{1,0:T(8,128)(2,1)} %all-gather.3.cloned.1.call-done.kv_ref), custom_call_target="tpu_custom_call" | custom-call | flops 2147483648 | bytes 4456448 | tf_op jit(solution)/shard_map/pallas_call | solution.py:50
  110.4 1.9 convolution_convert_fusion
  112.4 4.9 %all-to-all-start = ((bf16[8,64,384]{2,1,0:T(8,128)(2,1)}), bf16[8,64,384]{2,1,0:T(8,128)(2,1)S(1)}, u32[]{:S(2)}, u32[]{:S(2)}) async-start(bf16[8,64,384]{2,1,0:T(8,128)(2,1)} %bitcast.5), calls=%async_computation | async-start | bytes 786432 | tf_op jit(solution)/shard_map/all_to_all | solution.py:253
  117.3 0.3 convolution_multiply_fusion.2
  117.6 0.3 convolution_multiply_fusion.1
  117.9 0.1 reduce.1
  118.1 6.6 %all-to-all-done = bf16[8,64,384]{2,1,0:T(8,128)(2,1)S(1)} async-done(((bf16[8,64,384]{2,1,0:T(8,128)(2,1)}), bf16[8,64,384]{2,1,0:T(8,128)(2,1)S(1)}, u32[]{:S(2)}, u32[]{:S(2)}) %all-to-all-start) | async-done | bytes 393248 | tf_op jit(solution)/shard_map/all_to_all | solution.py:253
  124.7 0.1 convert_reduce_fusion
  124.8 0.1 multiply_reduce_fusion.2
  124.9 0.1 rsqrt.15
  125.0 0.4 multiply_reduce_fusion.1
  125.4 0.1 subtract_convert_fusion.4
  125.5 12.4 %all_gather.10 = bf16[512,384]{1,0:T(8,128)(2,1)S(1)} all-gather(bf16[64,384]{1,0:T(8,128)(2,1)S(1)} %bitcast.85), channel_id=1, replica_groups=mesh['seq'=16,'tm'=8,'dp'=2] {'tm'}, dimensions={0}, use_global_device_ids=true | all-gather | bytes 442368 | tf_op jit(solution)/shard_map/all_gather | solution.py:283
  137.9 0.4 multiply_reduce_fusion
  138.4 0.8 fusion.12
  139.1 0.0 all-gather.5.cloned.1.call-update
  139.1 0.9 copy.41.delta_ref
  140.0 17.7 %shard_map.113 = f32[512,128]{1,0:T(8,128)} custom-call(bf16[512,128]{1,0:T(8,128)(2,1)} %copy.40.q_ref, bf16[512,128]{1,0:T(8,128)(2,1)} %copy-done.6, f32[512,1]{1,0:T(8,128)} %get-tuple-element.8.lse_ref, f32[512,1]{1,0:T(8,128)} %copy.41.delta_ref, bf16[8192,256]{1,0:T(8,128)(2,1)} %all-gather.3.cloned.1.call-done.kv_ref), custom_call_target="tpu_custom_call" | custom-call | flops 3221225472 | bytes 4587520 | tf_op jit(solution)/shard_map/pallas_call | solution.py:100
  157.7 1.1 copy.42
  158.8 0.1 reshape.575
  158.9 0.2 fusion.33
  159.1 53.6 %all-gather.5.cloned.1.call-done.qg_ref = bf16[8448,256]{1,0:T(8,128)(2,1)} async-done(((bf16[528,256]{1,0:T(8,128)(2,1)}), bf16[8448,256]{1,0:T(8,128)(2,1)}) %all-gather.5.cloned.1.call-update) | async-done | bytes 4325392 | tf_op jit(solution)/shard_map/all_gather | solution.py:296
  212.7 0.9 slice.100
  213.7 0.2 reshape.581
  213.9 0.7 fusion.36
  214.6 20.1 %shard_map.114 = (f32[512,128]{1,0:T(8,128)}, f32[512,128]{1,0:T(8,128)}) custom-call(bf16[512,128]{1,0:T(8,128)(2,1)} %copy-done.4, bf16[512,128]{1,0:T(8,128)(2,1)} %bitcast.86, bf16[8448,256]{1,0:T(8,128)(2,1)} %all-gather.5.cloned.1.call-done.qg_ref, f32[1,8192]{1,0:T(1,128)} %bitcast.89, f32[1,8192]{1,0:T(1,128)} %bitcast.88), custom_call_target="tpu_custom_call" | custom-call | flops 4294967296 | bytes 4456448 | tf_op jit(solution)/shard_map/pallas_call | solution.py:147
  234.8 1.1 copy.48
  235.9 0.1 reshape.578
  236.0 0.2 fusion.32
  236.2 0.6 subtract_convert_fusion
  236.8 0.1 copy.51
  237.0 0.1 convert_element_type.119
  237.0 0.8 copy.53
  237.8 0.1 copy.45
  237.9 0.1 convert_element_type.115
  238.0 0.8 copy.52
  238.8 0.7 convert_bitcast_fusion
  (50 shorter events, 0.4 us)
Async XLA Ops:
  7.2 103.2 %copy-start = (bf16[1,128,384]{2,1,0:T(8,128)(2,1)S(1)}, bf16[1,128,384]{2,1,0:T(8,128)(2,1)}, u32[]{:S(2)}) copy-start(bf16[1,128,384]{2,1,0:T(8,128)(2,1)} %param.13) | copy-start | bytes 294916
  7.2 84.7 %all-gather.3.cloned.1.call-start = ((), (), s32[]{:S(2)}) async-start(), calls=%async_computation.1 | async-start | bytes 4456448 | tf_op jit(solution)/shard_map/all_gather | solution.py:245
  10.4 1.5 copy-start.9
  10.6 2.1 copy-start.10
  11.0 4.6 %copy-start.1 = (s32[16]{0:T(128)S(1)}, s32[16]{0:T(128)}, u32[]{:S(2)}) copy-start(s32[16]{0:T(128)} %param.16) | copy-start | bytes 196
  11.9 98.5 %copy-start.4 = (bf16[512,128]{1,0:T(8,128)(2,1)}, bf16[512,128]{1,0:T(8,128)(2,1)S(1)}, u32[]{:S(2)}) copy-start(bf16[512,128]{1,0:T(8,128)(2,1)S(1)} %copy.37.k_ref) | copy-start | bytes 393220
  12.7 104.9 %collective-permute-start = (bf16[2,32,768]{2,1,0:T(8,128)(2,1)S(1)}, bf16[2,32,768]{2,1,0:T(8,128)(2,1)S(1)}, u32[]{:S(2)}, u32[]{:S(2)}) collective-permute-start(bf16[2,32,768]{2,1,0:T(8,128)(2,1)S(1)} %copy-done.10), channel_id=1, source_target_pairs={{2,0},{4,2},{6,4},{8,6},{10,8},{12,10},{14,12},{3,1},{5,3},{7,5},{... | collective-permute-start | bytes 294920 | tf_op jit(solution)/shard_map/ppermute | solution.py:161
  17.7 99.6 %copy-start.2 = (bf16[3,384,768]{2,1,0:T(8,128)(2,1)S(1)}, bf16[3,384,768]{2,1,0:T(8,128)(2,1)}, u32[]{:S(2)}) copy-start(bf16[3,384,768]{2,1,0:T(8,128)(2,1)} %param.15) | copy-start | bytes 5308420
  110.4 7.5 %copy-start.8 = (f32[512,1]{1,0:T(8,128)S(1)}, f32[512,1]{1,0:T(8,128)}, u32[]{:S(2)}) copy-start(f32[512,1]{1,0:T(8,128)} %get-tuple-element.8.lse_ref) | copy-start | bytes 6148
  112.4 12.7 %copy-start.11 = (f32[384]{0:T(512)S(1)}, f32[384]{0:T(512)}, u32[]{:S(2)}) copy-start(f32[384]{0:T(512)} %param.14) | copy-start | bytes 4612
  112.4 12.4 %all-to-all-start = ((bf16[8,64,384]{2,1,0:T(8,128)(2,1)}), bf16[8,64,384]{2,1,0:T(8,128)(2,1)S(1)}, u32[]{:S(2)}, u32[]{:S(2)}) async-start(bf16[8,64,384]{2,1,0:T(8,128)(2,1)} %bitcast.5), calls=%async_computation | async-start | bytes 786432 | tf_op jit(solution)/shard_map/all_to_all | solution.py:253
  117.3 95.4 %all-gather.5.cloned.1.call-start = ((), (), s32[]{:S(2)}) async-start(), calls=%async_computation.2 | async-start | bytes 4595712 | tf_op jit(solution)/shard_map/all_gather | solution.py:296
  117.9 20.0 %copy-start.3 = (bf16[512,128]{1,0:T(8,128)(2,1)S(1)}, bf16[512,128]{1,0:T(8,128)(2,1)}, u32[]{:S(2)}) copy-start(bf16[512,128]{1,0:T(8,128)(2,1)} %get-tuple-element.7) | copy-start | bytes 393220
  118.1 20.3 %copy-start.5 = (bf16[512,128]{1,0:T(8,128)(2,1)S(1)}, bf16[512,128]{1,0:T(8,128)(2,1)}, u32[]{:S(2)}) copy-start(bf16[512,128]{1,0:T(8,128)(2,1)} %copy.40.q_ref) | copy-start | bytes 393220
  138.3 1.7 copy-start.6
  236.0 2.8 %copy-start.7 = (f32[512,128]{1,0:T(8,128)S(1)}, f32[512,128]{1,0:T(8,128)}, u32[]{:S(2)}) copy-start(f32[512,128]{1,0:T(8,128)} %get-tuple-element.10) | copy-start | bytes 786436
Sparse Core Ops, SparseCore 0:
  12.8 79.0 all-gather.2
  139.3 73.4 all-gather.4

commit v4 on v3

--- a/solution.py
+++ b/solution.py
@@ -36,12 +36,12 @@
         jnp.zeros((rows, 1), jnp.float32),
         jnp.zeros((rows, HD), jnp.float32),
     )
-    top, total, acc = lax.fori_loop(0, steps, body, start_state)
+    top, total, acc = lax.fori_loop(0, steps, body, start_state, unroll=2)
     out_ref[...] = (acc / total).astype(out_ref.dtype)
     lse_ref[...] = top + jnp.log(total)
 
 
-def attention_forward(q, kv_all, query_block=256, key_block=512):
+def attention_forward(q, kv_all, query_block=512, key_block=2048):
     rows = q.shape[0]
     keys = kv_all.shape[0]
     cost = pl.CostEstimate(
@@ -84,11 +84,11 @@
         gs = (w * (gw - delta)).astype(jnp.bfloat16)
         return acc + jnp.dot(gs, k, preferred_element_type=jnp.float32)
 
-    acc = lax.fori_loop(0, steps, body, jnp.zeros(dq_ref.shape, jnp.float32))
+    acc = lax.fori_loop(0, steps, body, jnp.zeros(dq_ref.shape, jnp.float32), unroll=2)
     dq_ref[...] = acc * SCALE
 
 
-def attention_query_grad(q, g, lse_col, delta_col, kv_all, query_block=256, key_block=512):
+def attention_query_grad(q, g, lse_col, delta_col, kv_all, query_block=512, key_block=1024):
     rows = q.shape[0]
     keys = kv_all.shape[0]
     cost = pl.CostEstimate(
@@ -130,12 +130,12 @@
         return dk, dv
 
     zero = jnp.zeros(dk_ref.shape, jnp.float32)
-    dk, dv = lax.fori_loop(0, steps, body, (zero, zero))
+    dk, dv = lax.fori_loop(0, steps, body, (zero, zero), unroll=2)
     dk_ref[...] = dk * SCALE
     dv_ref[...] = dv
 
 
-def attention_key_grad(k, v, qg_all, lse_row, delta_row, query_block, block_stride, key_rows=256):
+def attention_key_grad(k, v, qg_all, lse_row, delta_row, query_block, block_stride, key_rows=512):
     rows = k.shape[0]
     queries = lse_row.shape[1]
     cost = pl.CostEstimate(

time: 247 us -> 233 us (0.943)
  Pallas kernels: 56.4 us -> 36.3 us
  waiting for transfers between devices: 134 us -> 141 us
    pallas_call x1, Pallas kernels: 18.5 us -> 10.5 us  [attention_forward(): pl.pallas_call(functools.partial(forward_kernel, key_block), grid=(rows /...]
    all_gather x1, waiting for transfers between devices: 53.6 us -> 59.9 us  [on_device(): lax.all_gather(packed, 'seq', axis=0, tiled=True)]
    pallas_call x1, Pallas kernels: 17.7 us -> 11.6 us  [attention_query_grad(): pl.pallas_call(functools.partial(query_grad_kernel, key_block), grid=(row...]
    pallas_call x1, Pallas kernels: 20.1 us -> 14.2 us  [attention_key_grad(): pl.pallas_call(functools.partial(key_grad_kernel, query_block, block_stri...]
  transfers between devices with their start and end apart: 4 -> 4, of which waited for: 3 -> 3; matrix products, arithmetic and copies ran while one was open for 3% -> 3% of each run, Pallas kernels for 15% -> 10%
where the time goes in v4:
time: 233 us
  waiting for transfers between devices  141 us (61%)
  Pallas kernels  36.3 us (16%)
  between operations  14.5 us (6%)
  local copies, waits for them, and re-layouts  14.4 us (6%)
  blocking collectives  12.5 us (5%)
  starting transfers between devices  6.9 us (3%)
  other arithmetic  4.08 us (2%)
  matrix products  3.33 us (1%)
    all_gather x1, waiting for transfers between devices, on_device(): lax.all_gather(jnp.concatenate([rot_k, plain_v], axis=1), 'seq', axis=0,...  74.1 us
    all_gather x1, waiting for transfers between devices, on_device(): lax.all_gather(packed, 'seq', axis=0, tiled=True)  59.9 us
    pallas_call x1, Pallas kernels, attention_key_grad(): pl.pallas_call(functools.partial(key_grad_kernel, query_block, block_stri...  14.2 us
    all_gather x1, blocking collectives, on_device(): lax.all_gather(grad_mixed, 'tm', axis=0, tiled=True)  12.5 us
    pallas_call x1, Pallas kernels, attention_query_grad(): pl.pallas_call(functools.partial(query_grad_kernel, key_block), grid=(row...  11.6 us
    pallas_call x1, Pallas kernels, attention_forward(): pl.pallas_call(functools.partial(forward_kernel, key_block), grid=(rows /...  10.5 us
    all_to_all x1, waiting for transfers between devices, on_device(): lax.all_to_all(projected.reshape(head_count, span_frames * slab_cells, ch...  6.65 us
    all_to_all x1, starting transfers between devices, on_device(): lax.all_to_all(projected.reshape(head_count, span_frames * slab_cells, ch...  4.94 us
  transfers between devices with their start and end apart: 4, of which 3 were waited for; matrix products, arithmetic and copies ran while one was open for 3% of the time, Pallas kernels for 10%

profile of v4, /device:TPU:2, one launch (start us, length us, event | category | flops | bytes accessed | tf_op | source)
XLA Modules:
  0.0 232.7 jit_solution(3067474782960729902)
XLA Ops:
  7.2 0.0 copy-start
  7.2 0.0 all-gather.3.cloned.1.call-start
  7.3 0.7 tile.4
  7.9 0.1 tile.10
  8.0 1.0 copy.33
  9.0 0.1 reshape.580
  9.2 0.2 fusion.34
  9.4 1.0 copy.29
  10.4 0.1 reshape.579
  10.6 0.2 fusion.35
  10.8 0.1 multiply_bitcast_fusion.2
  10.9 0.1 multiply_bitcast_fusion.1
  11.0 0.5 subtract_convert_fusion.2
  11.5 0.1 copy.36
  11.7 0.1 convert_element_type.108
  11.7 0.1 copy.37.k_ref
  11.9 0.7 pad_maximum_fusion
  12.6 0.0 all-gather.3.cloned.1.call-update
  12.7 1.9 collective-permute-start
  14.6 0.1 copy.32
  14.7 0.1 convert_element_type.105
  14.8 0.8 copy.40.q_ref
  15.6 0.7 gather_fusion
  16.3 0.7 gather_fusion.1
  17.0 0.7 gather_fusion.2
  17.6 0.1 constant_dynamic-slice_fusion
  17.7 74.1 %all-gather.3.cloned.1.call-done.kv_ref = bf16[8192,256]{1,0:T(8,128)(2,1)} async-done(((bf16[512,256]{1,0:T(8,128)(2,1)}), bf16[8192,256]{1,0:T(8,128)(2,1)}) %all-gather.3.cloned.1.call-update) | async-done | bytes 4194320 | tf_op jit(solution)/shard_map/all_gather | solution.py:245
  91.9 10.5 %shard_map.112 = (bf16[512,128]{1,0:T(8,128)(2,1)}, f32[512,1]{1,0:T(8,128)}) custom-call(bf16[512,128]{1,0:T(8,128)(2,1)} %copy.40.q_ref, bf16[8192,256]{1,0:T(8,128)(2,1)} %all-gather.3.cloned.1.call-done.kv_ref), custom_call_target="tpu_custom_call" | custom-call | flops 2147483648 | bytes 4456448 | tf_op jit(solution)/shard_map/pallas_call | solution.py:50
  102.4 1.9 convolution_convert_fusion
  104.3 4.9 %all-to-all-start = ((bf16[8,64,384]{2,1,0:T(8,128)(2,1)}), bf16[8,64,384]{2,1,0:T(8,128)(2,1)S(1)}, u32[]{:S(2)}, u32[]{:S(2)}) async-start(bf16[8,64,384]{2,1,0:T(8,128)(2,1)} %bitcast.5), calls=%async_computation | async-start | bytes 786432 | tf_op jit(solution)/shard_map/all_to_all | solution.py:253
  109.3 0.3 convolution_multiply_fusion.2
  109.6 0.3 convolution_multiply_fusion.1
  109.9 0.1 reduce.1
  110.1 6.6 %all-to-all-done = bf16[8,64,384]{2,1,0:T(8,128)(2,1)S(1)} async-done(((bf16[8,64,384]{2,1,0:T(8,128)(2,1)}), bf16[8,64,384]{2,1,0:T(8,128)(2,1)S(1)}, u32[]{:S(2)}, u32[]{:S(2)}) %all-to-all-start) | async-done | bytes 393248 | tf_op jit(solution)/shard_map/all_to_all | solution.py:253
  116.7 0.1 convert_reduce_fusion
  116.8 0.1 multiply_reduce_fusion.2
  116.9 0.1 rsqrt.15
  117.0 0.4 multiply_reduce_fusion.1
  117.4 0.1 subtract_convert_fusion.4
  117.5 12.5 %all_gather.10 = bf16[512,384]{1,0:T(8,128)(2,1)S(1)} all-gather(bf16[64,384]{1,0:T(8,128)(2,1)S(1)} %bitcast.85), channel_id=1, replica_groups=mesh['seq'=16,'tm'=8,'dp'=2] {'tm'}, dimensions={0}, use_global_device_ids=true | all-gather | bytes 442368 | tf_op jit(solution)/shard_map/all_gather | solution.py:283
  130.1 0.4 multiply_reduce_fusion
  130.5 0.8 fusion.12
  131.3 0.0 all-gather.5.cloned.1.call-update
  131.3 0.9 copy.41.delta_ref
  132.2 11.6 %shard_map.113 = f32[512,128]{1,0:T(8,128)} custom-call(bf16[512,128]{1,0:T(8,128)(2,1)} %copy.40.q_ref, bf16[512,128]{1,0:T(8,128)(2,1)} %copy-done.6, f32[512,1]{1,0:T(8,128)} %get-tuple-element.8.lse_ref, f32[512,1]{1,0:T(8,128)} %copy.41.delta_ref, bf16[8192,256]{1,0:T(8,128)(2,1)} %all-gather.3.cloned.1.call-done.kv_ref), custom_call_target="tpu_custom_call" | custom-call | flops 3221225472 | bytes 4587520 | tf_op jit(solution)/shard_map/pallas_call | solution.py:100
  143.8 1.1 copy.42
  144.9 0.1 reshape.575
  145.0 0.2 fusion.33
  145.2 59.9 %all-gather.5.cloned.1.call-done.qg_ref = bf16[8448,256]{1,0:T(8,128)(2,1)} async-done(((bf16[528,256]{1,0:T(8,128)(2,1)}), bf16[8448,256]{1,0:T(8,128)(2,1)}) %all-gather.5.cloned.1.call-update) | async-done | bytes 4325392 | tf_op jit(solution)/shard_map/all_gather | solution.py:296
  205.1 0.9 slice.100
  206.1 0.2 reshape.581
  206.3 0.7 fusion.36
  207.0 14.2 %shard_map.114 = (f32[512,128]{1,0:T(8,128)}, f32[512,128]{1,0:T(8,128)}) custom-call(bf16[512,128]{1,0:T(8,128)(2,1)} %copy-done.4, bf16[512,128]{1,0:T(8,128)(2,1)} %bitcast.86, bf16[8448,256]{1,0:T(8,128)(2,1)} %all-gather.5.cloned.1.call-done.qg_ref, f32[1,8192]{1,0:T(1,128)} %bitcast.89, f32[1,8192]{1,0:T(1,128)} %bitcast.88), custom_call_target="tpu_custom_call" | custom-call | flops 4294967296 | bytes 4456448 | tf_op jit(solution)/shard_map/pallas_call | solution.py:147
  221.2 1.1 copy.48
  222.3 0.1 reshape.578
  222.4 0.2 fusion.32
  222.6 0.6 subtract_convert_fusion
  223.2 0.1 copy.51
  223.4 0.1 convert_element_type.119
  223.4 0.8 copy.53
  224.2 0.1 copy.45
  224.3 0.1 convert_element_type.115
  224.4 0.8 copy.52
  225.2 0.7 convert_bitcast_fusion
  (50 shorter events, 0.4 us)
Async XLA Ops:
  7.2 95.2 %copy-start = (bf16[1,128,384]{2,1,0:T(8,128)(2,1)S(1)}, bf16[1,128,384]{2,1,0:T(8,128)(2,1)}, u32[]{:S(2)}) copy-start(bf16[1,128,384]{2,1,0:T(8,128)(2,1)} %param.13) | copy-start | bytes 294916
  7.2 84.7 %all-gather.3.cloned.1.call-start = ((), (), s32[]{:S(2)}) async-start(), calls=%async_computation.1 | async-start | bytes 4456448 | tf_op jit(solution)/shard_map/all_gather | solution.py:245
  10.4 1.5 copy-start.9
  10.6 2.1 copy-start.10
  11.0 4.6 %copy-start.1 = (s32[16]{0:T(128)S(1)}, s32[16]{0:T(128)}, u32[]{:S(2)}) copy-start(s32[16]{0:T(128)} %param.16) | copy-start | bytes 196
  11.9 90.5 %copy-start.4 = (bf16[512,128]{1,0:T(8,128)(2,1)}, bf16[512,128]{1,0:T(8,128)(2,1)S(1)}, u32[]{:S(2)}) copy-start(bf16[512,128]{1,0:T(8,128)(2,1)S(1)} %copy.37.k_ref) | copy-start | bytes 393220
  12.7 96.9 %collective-permute-start = (bf16[2,32,768]{2,1,0:T(8,128)(2,1)S(1)}, bf16[2,32,768]{2,1,0:T(8,128)(2,1)S(1)}, u32[]{:S(2)}, u32[]{:S(2)}) collective-permute-start(bf16[2,32,768]{2,1,0:T(8,128)(2,1)S(1)} %copy-done.10), channel_id=1, source_target_pairs={{2,0},{4,2},{6,4},{8,6},{10,8},{12,10},{14,12},{3,1},{5,3},{7,5},{... | collective-permute-start | bytes 294920 | tf_op jit(solution)/shard_map/ppermute | solution.py:161
  17.7 91.5 %copy-start.2 = (bf16[3,384,768]{2,1,0:T(8,128)(2,1)S(1)}, bf16[3,384,768]{2,1,0:T(8,128)(2,1)}, u32[]{:S(2)}) copy-start(bf16[3,384,768]{2,1,0:T(8,128)(2,1)} %param.15) | copy-start | bytes 5308420
  102.4 7.5 %copy-start.8 = (f32[512,1]{1,0:T(8,128)S(1)}, f32[512,1]{1,0:T(8,128)}, u32[]{:S(2)}) copy-start(f32[512,1]{1,0:T(8,128)} %get-tuple-element.8.lse_ref) | copy-start | bytes 6148
  104.3 12.7 %copy-start.11 = (f32[384]{0:T(512)S(1)}, f32[384]{0:T(512)}, u32[]{:S(2)}) copy-start(f32[384]{0:T(512)} %param.14) | copy-start | bytes 4612
  104.3 12.4 %all-to-all-start = ((bf16[8,64,384]{2,1,0:T(8,128)(2,1)}), bf16[8,64,384]{2,1,0:T(8,128)(2,1)S(1)}, u32[]{:S(2)}, u32[]{:S(2)}) async-start(bf16[8,64,384]{2,1,0:T(8,128)(2,1)} %bitcast.5), calls=%async_computation | async-start | bytes 786432 | tf_op jit(solution)/shard_map/all_to_all | solution.py:253
  109.3 95.8 %all-gather.5.cloned.1.call-start = ((), (), s32[]{:S(2)}) async-start(), calls=%async_computation.2 | async-start | bytes 4595712 | tf_op jit(solution)/shard_map/all_gather | solution.py:296
  109.9 20.2 %copy-start.3 = (bf16[512,128]{1,0:T(8,128)(2,1)S(1)}, bf16[512,128]{1,0:T(8,128)(2,1)}, u32[]{:S(2)}) copy-start(bf16[512,128]{1,0:T(8,128)(2,1)} %get-tuple-element.7) | copy-start | bytes 393220
  110.1 20.4 %copy-start.5 = (bf16[512,128]{1,0:T(8,128)(2,1)S(1)}, bf16[512,128]{1,0:T(8,128)(2,1)}, u32[]{:S(2)}) copy-start(bf16[512,128]{1,0:T(8,128)(2,1)} %copy.40.q_ref) | copy-start | bytes 393220
  130.4 1.7 copy-start.6
  222.4 2.8 %copy-start.7 = (f32[512,128]{1,0:T(8,128)S(1)}, f32[512,128]{1,0:T(8,128)}, u32[]{:S(2)}) copy-start(f32[512,128]{1,0:T(8,128)} %get-tuple-element.10) | copy-start | bytes 786436
Sparse Core Ops, SparseCore 0:
  12.8 79.0 all-gather.2
  131.4 73.6 all-gather.4

commit v5 on v4

--- a/solution.py
+++ b/solution.py
@@ -11,6 +11,8 @@
 HD = 128
 GRID_W = 32
 SCALE = HD ** (-0.5)
+LOG2E = 1.4426950408889634
+LN2 = 0.6931471805599453
 
 
 def forward_kernel(key_block, q_ref, kv_ref, out_ref, lse_ref):
@@ -23,10 +25,10 @@
         start = pl.multiple_of(step * key_block, key_block)
         k = kv_ref[pl.ds(start, key_block), :HD]
         v = kv_ref[pl.ds(start, key_block), HD:]
-        s = lax.dot_general(q, k, (((1,), (1,)), ((), ())), preferred_element_type=jnp.float32) * SCALE
+        s = lax.dot_general(q, k, (((1,), (1,)), ((), ())), preferred_element_type=jnp.float32) * (SCALE * LOG2E)
         new_top = jnp.maximum(top, jnp.max(s, axis=1, keepdims=True))
-        factor = jnp.exp(top - new_top)
-        w = jnp.exp(s - new_top)
+        factor = jnp.exp2(top - new_top)
+        w = jnp.exp2(s - new_top)
         total = total * factor + jnp.sum(w, axis=1, keepdims=True)
         acc = acc * factor + jnp.dot(w.astype(jnp.bfloat16), v, preferred_element_type=jnp.float32)
         return new_top, total, acc
@@ -36,9 +38,9 @@
         jnp.zeros((rows, 1), jnp.float32),
         jnp.zeros((rows, HD), jnp.float32),
     )
-    top, total, acc = lax.fori_loop(0, steps, body, start_state, unroll=2)
+    top, total, acc = lax.fori_loop(0, steps, body, start_state, unroll=4)
     out_ref[...] = (acc / total).astype(out_ref.dtype)
-    lse_ref[...] = top + jnp.log(total)
+    lse_ref[...] = top * LN2 + jnp.log(total)
 
 
 def attention_forward(q, kv_all, query_block=512, key_block=2048):
@@ -70,7 +72,7 @@
 def query_grad_kernel(key_block, q_ref, g_ref, lse_ref, delta_ref, kv_ref, dq_ref):
     q = q_ref[...]
     g = g_ref[...]
-    lse = lse_ref[...]
+    lse = lse_ref[...] * LOG2E
     delta = delta_ref[...]
     steps = kv_ref.shape[0] // key_block
 
@@ -78,13 +80,13 @@
         start = pl.multiple_of(step * key_block, key_block)
         k = kv_ref[pl.ds(start, key_block), :HD]
         v = kv_ref[pl.ds(start, key_block), HD:]
-        s = lax.dot_general(q, k, (((1,), (1,)), ((), ())), preferred_element_type=jnp.float32) * SCALE
-        w = jnp.exp(s - lse)
+        s = lax.dot_general(q, k, (((1,), (1,)), ((), ())), preferred_element_type=jnp.float32) * (SCALE * LOG2E)
+        w = jnp.exp2(s - lse)
         gw = lax.dot_general(g, v, (((1,), (1,)), ((), ())), preferred_element_type=jnp.float32)
         gs = (w * (gw - delta)).astype(jnp.bfloat16)
         return acc + jnp.dot(gs, k, preferred_element_type=jnp.float32)
 
-    acc = lax.fori_loop(0, steps, body, jnp.zeros(dq_ref.shape, jnp.float32), unroll=2)
+    acc = lax.fori_loop(0, steps, body, jnp.zeros(dq_ref.shape, jnp.float32), unroll=4)
     dq_ref[...] = acc * SCALE
 
 
@@ -121,8 +123,8 @@
         g = qg_ref[pl.ds(start, query_block), HD:]
         lse = lse_ref[:, pl.ds(column, query_block)]
         delta = delta_ref[:, pl.ds(column, query_block)]
-        s = lax.dot_general(k, q, (((1,), (1,)), ((), ())), preferred_element_type=jnp.float32) * SCALE
-        w = jnp.exp(s - lse)
+        s = lax.dot_general(k, q, (((1,), (1,)), ((), ())), preferred_element_type=jnp.float32) * (SCALE * LOG2E)
+        w = jnp.exp2(s - lse * LOG2E)
         gw = lax.dot_general(v, g, (((1,), (1,)), ((), ())), preferred_element_type=jnp.float32)
         gs = (w * (gw - delta)).astype(jnp.bfloat16)
         dk = dk + jnp.dot(gs, q, preferred_element_type=jnp.float32)
@@ -130,7 +132,7 @@
         return dk, dv
 
     zero = jnp.zeros(dk_ref.shape, jnp.float32)
-    dk, dv = lax.fori_loop(0, steps, body, (zero, zero), unroll=2)
+    dk, dv = lax.fori_loop(0, steps, body, (zero, zero), unroll=4)
     dk_ref[...] = dk * SCALE
     dv_ref[...] = dv
 

time: 233 us -> 230 us (0.987)
  Pallas kernels: 36.3 us -> 32.7 us
  transfers between devices with their start and end apart: 4 -> 4, of which waited for: 3 -> 3; matrix products, arithmetic and copies ran while one was open for 3% -> 4% of each run, Pallas kernels for 10% -> 9%
where the time goes in v5:
time: 230 us
  waiting for transfers between devices  142 us (62%)
  Pallas kernels  32.7 us (14%)
  between operations  14.5 us (6%)
  local copies, waits for them, and re-layouts  14.4 us (6%)
  blocking collectives  12.5 us (5%)
  starting transfers between devices  6.91 us (3%)
  other arithmetic  4.08 us (2%)
  matrix products  3.33 us (1%)
    all_gather x1, waiting for transfers between devices, on_device(): lax.all_gather(jnp.concatenate([rot_k, plain_v], axis=1), 'seq', axis=0,...  74.1 us
    all_gather x1, waiting for transfers between devices, on_device(): lax.all_gather(packed, 'seq', axis=0, tiled=True)  60.8 us
    pallas_call x1, Pallas kernels, attention_key_grad(): pl.pallas_call(functools.partial(key_grad_kernel, query_block, block_stri...  12.9 us
    all_gather x1, blocking collectives, on_device(): lax.all_gather(grad_mixed, 'tm', axis=0, tiled=True)  12.5 us
    pallas_call x1, Pallas kernels, attention_query_grad(): pl.pallas_call(functools.partial(query_grad_kernel, key_block), grid=(row...  10.7 us
    pallas_call x1, Pallas kernels, attention_forward(): pl.pallas_call(functools.partial(forward_kernel, key_block), grid=(rows /...  9.05 us
    all_to_all x1, waiting for transfers between devices, on_device(): lax.all_to_all(projected.reshape(head_count, span_frames * slab_cells, ch...  6.65 us
    all_to_all x1, starting transfers between devices, on_device(): lax.all_to_all(projected.reshape(head_count, span_frames * slab_cells, ch...  4.95 us
  transfers between devices with their start and end apart: 4, of which 3 were waited for; matrix products, arithmetic and copies ran while one was open for 4% of the time, Pallas kernels for 9%

profile of v5, /device:TPU:2, one launch (start us, length us, event | category | flops | bytes accessed | tf_op | source)
XLA Modules:
  0.0 230.0 jit_solution(11598992722906717059)
XLA Ops:
  7.2 0.0 copy-start
  7.2 0.0 all-gather.3.cloned.1.call-start
  7.3 0.7 tile.4
  7.9 0.1 tile.10
  8.0 1.0 copy.33
  9.0 0.1 reshape.580
  9.2 0.2 fusion.34
  9.4 1.0 copy.29
  10.4 0.1 reshape.579
  10.6 0.2 fusion.35
  10.8 0.1 multiply_bitcast_fusion.2
  10.9 0.1 multiply_bitcast_fusion.1
  11.0 0.5 subtract_convert_fusion.2
  11.5 0.1 copy.36
  11.7 0.1 convert_element_type.108
  11.7 0.1 copy.37.k_ref
  11.9 0.7 pad_maximum_fusion
  12.6 0.0 all-gather.3.cloned.1.call-update
  12.7 1.9 collective-permute-start
  14.6 0.1 copy.32
  14.7 0.1 convert_element_type.105
  14.8 0.8 copy.40.q_ref
  15.6 0.7 gather_fusion
  16.3 0.7 gather_fusion.1
  17.0 0.7 gather_fusion.2
  17.6 0.1 constant_dynamic-slice_fusion
  17.7 74.1 %all-gather.3.cloned.1.call-done.kv_ref = bf16[8192,256]{1,0:T(8,128)(2,1)} async-done(((bf16[512,256]{1,0:T(8,128)(2,1)}), bf16[8192,256]{1,0:T(8,128)(2,1)}) %all-gather.3.cloned.1.call-update) | async-done | bytes 4194320 | tf_op jit(solution)/shard_map/all_gather | solution.py:247
  91.9 9.1 %shard_map.112 = (bf16[512,128]{1,0:T(8,128)(2,1)}, f32[512,1]{1,0:T(8,128)}) custom-call(bf16[512,128]{1,0:T(8,128)(2,1)} %copy.40.q_ref, bf16[8192,256]{1,0:T(8,128)(2,1)} %all-gather.3.cloned.1.call-done.kv_ref), custom_call_target="tpu_custom_call" | custom-call | flops 2147483648 | bytes 4456448 | tf_op jit(solution)/shard_map/pallas_call | solution.py:52
  100.9 1.9 convolution_convert_fusion
  102.9 4.9 %all-to-all-start = ((bf16[8,64,384]{2,1,0:T(8,128)(2,1)}), bf16[8,64,384]{2,1,0:T(8,128)(2,1)S(1)}, u32[]{:S(2)}, u32[]{:S(2)}) async-start(bf16[8,64,384]{2,1,0:T(8,128)(2,1)} %bitcast.5), calls=%async_computation | async-start | bytes 786432 | tf_op jit(solution)/shard_map/all_to_all | solution.py:255
  107.8 0.3 convolution_multiply_fusion.2
  108.1 0.3 convolution_multiply_fusion.1
  108.5 0.1 reduce.1
  108.6 6.6 %all-to-all-done = bf16[8,64,384]{2,1,0:T(8,128)(2,1)S(1)} async-done(((bf16[8,64,384]{2,1,0:T(8,128)(2,1)}), bf16[8,64,384]{2,1,0:T(8,128)(2,1)S(1)}, u32[]{:S(2)}, u32[]{:S(2)}) %all-to-all-start) | async-done | bytes 393248 | tf_op jit(solution)/shard_map/all_to_all | solution.py:255
  115.3 0.1 convert_reduce_fusion
  115.3 0.1 multiply_reduce_fusion.2
  115.5 0.1 rsqrt.15
  115.5 0.4 multiply_reduce_fusion.1
  116.0 0.1 subtract_convert_fusion.4
  116.1 12.5 %all_gather.10 = bf16[512,384]{1,0:T(8,128)(2,1)S(1)} all-gather(bf16[64,384]{1,0:T(8,128)(2,1)S(1)} %bitcast.85), channel_id=1, replica_groups=mesh['seq'=16,'tm'=8,'dp'=2] {'tm'}, dimensions={0}, use_global_device_ids=true | all-gather | bytes 442368 | tf_op jit(solution)/shard_map/all_gather | solution.py:285
  128.6 0.4 multiply_reduce_fusion
  129.1 0.8 fusion.12
  129.8 0.0 all-gather.5.cloned.1.call-update
  129.8 0.9 copy.41.delta_ref
  130.7 10.7 %shard_map.113 = f32[512,128]{1,0:T(8,128)} custom-call(bf16[512,128]{1,0:T(8,128)(2,1)} %copy.40.q_ref, bf16[512,128]{1,0:T(8,128)(2,1)} %copy-done.6, f32[512,1]{1,0:T(8,128)} %get-tuple-element.8.lse_ref, f32[512,1]{1,0:T(8,128)} %copy.41.delta_ref, bf16[8192,256]{1,0:T(8,128)(2,1)} %all-gather.3.cloned.1.call-done.kv_ref), custom_call_target="tpu_custom_call" | custom-call | flops 3221225472 | bytes 4587520 | tf_op jit(solution)/shard_map/pallas_call | solution.py:102
  141.5 1.1 copy.42
  142.5 0.1 reshape.575
  142.7 0.2 fusion.33
  142.9 60.8 %all-gather.5.cloned.1.call-done.qg_ref = bf16[8448,256]{1,0:T(8,128)(2,1)} async-done(((bf16[528,256]{1,0:T(8,128)(2,1)}), bf16[8448,256]{1,0:T(8,128)(2,1)}) %all-gather.5.cloned.1.call-update) | async-done | bytes 4325392 | tf_op jit(solution)/shard_map/all_gather | solution.py:298
  203.7 0.9 slice.100
  204.7 0.2 reshape.581
  204.9 0.7 fusion.36
  205.6 12.9 %shard_map.114 = (f32[512,128]{1,0:T(8,128)}, f32[512,128]{1,0:T(8,128)}) custom-call(bf16[512,128]{1,0:T(8,128)(2,1)} %copy-done.4, bf16[512,128]{1,0:T(8,128)(2,1)} %bitcast.86, bf16[8448,256]{1,0:T(8,128)(2,1)} %all-gather.5.cloned.1.call-done.qg_ref, f32[1,8192]{1,0:T(1,128)} %bitcast.89, f32[1,8192]{1,0:T(1,128)} %bitcast.88), custom_call_target="tpu_custom_call" | custom-call | flops 4294967296 | bytes 4456448 | tf_op jit(solution)/shard_map/pallas_call | solution.py:149
  218.5 1.1 copy.48
  219.6 0.1 reshape.578
  219.7 0.2 fusion.32
  220.0 0.6 subtract_convert_fusion
  220.5 0.1 copy.51
  220.7 0.1 convert_element_type.119
  220.8 0.8 copy.53
  221.5 0.1 copy.45
  221.7 0.1 convert_element_type.115
  221.7 0.8 copy.52
  222.5 0.7 convert_bitcast_fusion
  (50 shorter events, 0.4 us)
Async XLA Ops:
  7.2 93.8 %copy-start = (bf16[1,128,384]{2,1,0:T(8,128)(2,1)S(1)}, bf16[1,128,384]{2,1,0:T(8,128)(2,1)}, u32[]{:S(2)}) copy-start(bf16[1,128,384]{2,1,0:T(8,128)(2,1)} %param.13) | copy-start | bytes 294916
  7.2 84.7 %all-gather.3.cloned.1.call-start = ((), (), s32[]{:S(2)}) async-start(), calls=%async_computation.1 | async-start | bytes 4456448 | tf_op jit(solution)/shard_map/all_gather | solution.py:247
  10.4 1.5 copy-start.9
  10.6 2.1 copy-start.10
  11.0 4.6 %copy-start.1 = (s32[16]{0:T(128)S(1)}, s32[16]{0:T(128)}, u32[]{:S(2)}) copy-start(s32[16]{0:T(128)} %param.16) | copy-start | bytes 196
  11.9 89.0 %copy-start.4 = (bf16[512,128]{1,0:T(8,128)(2,1)}, bf16[512,128]{1,0:T(8,128)(2,1)S(1)}, u32[]{:S(2)}) copy-start(bf16[512,128]{1,0:T(8,128)(2,1)S(1)} %copy.37.k_ref) | copy-start | bytes 393220
  12.7 95.5 %collective-permute-start = (bf16[2,32,768]{2,1,0:T(8,128)(2,1)S(1)}, bf16[2,32,768]{2,1,0:T(8,128)(2,1)S(1)}, u32[]{:S(2)}, u32[]{:S(2)}) collective-permute-start(bf16[2,32,768]{2,1,0:T(8,128)(2,1)S(1)} %copy-done.10), channel_id=1, source_target_pairs={{2,0},{4,2},{6,4},{8,6},{10,8},{12,10},{14,12},{3,1},{5,3},{7,5},{... | collective-permute-start | bytes 294920 | tf_op jit(solution)/shard_map/ppermute | solution.py:163
  17.7 90.1 %copy-start.2 = (bf16[3,384,768]{2,1,0:T(8,128)(2,1)S(1)}, bf16[3,384,768]{2,1,0:T(8,128)(2,1)}, u32[]{:S(2)}) copy-start(bf16[3,384,768]{2,1,0:T(8,128)(2,1)} %param.15) | copy-start | bytes 5308420
  100.9 7.5 %copy-start.8 = (f32[512,1]{1,0:T(8,128)S(1)}, f32[512,1]{1,0:T(8,128)}, u32[]{:S(2)}) copy-start(f32[512,1]{1,0:T(8,128)} %get-tuple-element.8.lse_ref) | copy-start | bytes 6148
  102.9 12.7 %copy-start.11 = (f32[384]{0:T(512)S(1)}, f32[384]{0:T(512)}, u32[]{:S(2)}) copy-start(f32[384]{0:T(512)} %param.14) | copy-start | bytes 4612
  102.9 12.4 %all-to-all-start = ((bf16[8,64,384]{2,1,0:T(8,128)(2,1)}), bf16[8,64,384]{2,1,0:T(8,128)(2,1)S(1)}, u32[]{:S(2)}, u32[]{:S(2)}) async-start(bf16[8,64,384]{2,1,0:T(8,128)(2,1)} %bitcast.5), calls=%async_computation | async-start | bytes 786432 | tf_op jit(solution)/shard_map/all_to_all | solution.py:255
  107.8 95.8 %all-gather.5.cloned.1.call-start = ((), (), s32[]{:S(2)}) async-start(), calls=%async_computation.2 | async-start | bytes 4595712 | tf_op jit(solution)/shard_map/all_gather | solution.py:298
  108.5 20.2 %copy-start.3 = (bf16[512,128]{1,0:T(8,128)(2,1)S(1)}, bf16[512,128]{1,0:T(8,128)(2,1)}, u32[]{:S(2)}) copy-start(bf16[512,128]{1,0:T(8,128)(2,1)} %get-tuple-element.7) | copy-start | bytes 393220
  108.6 20.4 %copy-start.5 = (bf16[512,128]{1,0:T(8,128)(2,1)S(1)}, bf16[512,128]{1,0:T(8,128)(2,1)}, u32[]{:S(2)}) copy-start(bf16[512,128]{1,0:T(8,128)(2,1)} %copy.40.q_ref) | copy-start | bytes 393220
  129.0 1.7 copy-start.6
  219.7 2.8 %copy-start.7 = (f32[512,128]{1,0:T(8,128)S(1)}, f32[512,128]{1,0:T(8,128)}, u32[]{:S(2)}) copy-start(f32[512,128]{1,0:T(8,128)} %get-tuple-element.10) | copy-start | bytes 786436
Sparse Core Ops, SparseCore 0:
  12.8 79.0 all-gather.2
  130.0 73.6 all-gather.4

commit v6 on v5

--- a/solution.py
+++ b/solution.py
@@ -13,6 +13,16 @@
 SCALE = HD ** (-0.5)
 LOG2E = 1.4426950408889634
 LN2 = 0.6931471805599453
+
+
+def rotate_back_rows(x, cos_ref, sin_ref):
+    lanes = lax.broadcasted_iota(jnp.int32, x.shape, 1)
+    ahead = pltpu.roll(x, x.shape[1] - 1, 1)
+    behind = pltpu.roll(x, 1, 1)
+    ahead_lane = pltpu.roll(lanes, x.shape[1] - 1, 1)
+    partner_lane = jnp.where(lanes % 2 == 0, lanes + 1, lanes - 1)
+    partner = jnp.where(ahead_lane == partner_lane, ahead, behind)
+    return x * cos_ref[...] + partner * sin_ref[...]
 
 
 def forward_kernel(key_block, q_ref, kv_ref, out_ref, lse_ref):
@@ -69,7 +79,7 @@
     )(q, kv_all)
 
 
-def query_grad_kernel(key_block, q_ref, g_ref, lse_ref, delta_ref, kv_ref, dq_ref):
+def query_grad_kernel(key_block, q_ref, g_ref, lse_ref, delta_ref, kv_ref, cos_ref, sin_ref, dq_ref):
     q = q_ref[...]
     g = g_ref[...]
     lse = lse_ref[...] * LOG2E
@@ -87,10 +97,10 @@
         return acc + jnp.dot(gs, k, preferred_element_type=jnp.float32)
 
     acc = lax.fori_loop(0, steps, body, jnp.zeros(dq_ref.shape, jnp.float32), unroll=4)
-    dq_ref[...] = acc * SCALE
-
-
-def attention_query_grad(q, g, lse_col, delta_col, kv_all, query_block=512, key_block=1024):
+    dq_ref[...] = rotate_back_rows(acc * SCALE, cos_ref, sin_ref).astype(dq_ref.dtype)
+
+
+def attention_query_grad(q, g, lse_col, delta_col, kv_all, cos_wide, sin_wide, query_block=512, key_block=1024):
     rows = q.shape[0]
     keys = kv_all.shape[0]
     cost = pl.CostEstimate(
@@ -102,15 +112,15 @@
     return pl.pallas_call(
         functools.partial(query_grad_kernel, key_block),
         grid=(rows // query_block,),
-        in_specs=[row_spec, row_spec, col_spec, col_spec, whole],
+        in_specs=[row_spec, row_spec, col_spec, col_spec, whole, row_spec, row_spec],
         out_specs=pl.BlockSpec((query_block, HD), lambda i: (i, 0)),
-        out_shape=jax.ShapeDtypeStruct((rows, HD), jnp.float32),
+        out_shape=jax.ShapeDtypeStruct((rows, HD), jnp.bfloat16),
         compiler_params=pltpu.CompilerParams(dimension_semantics=("arbitrary",)),
         cost_estimate=cost,
-    )(q, g, lse_col, delta_col, kv_all)
-
-
-def key_grad_kernel(query_block, block_stride, k_ref, v_ref, qg_ref, lse_ref, delta_ref, dk_ref, dv_ref):
+    )(q, g, lse_col, delta_col, kv_all, cos_wide, sin_wide)
+
+
+def key_grad_kernel(query_block, block_stride, k_ref, v_ref, qg_ref, lse_ref, delta_ref, cos_ref, sin_ref, dk_ref, dv_ref):
     k = k_ref[...]
     v = v_ref[...]
     steps = lse_ref.shape[1] // query_block
@@ -133,11 +143,11 @@
 
     zero = jnp.zeros(dk_ref.shape, jnp.float32)
     dk, dv = lax.fori_loop(0, steps, body, (zero, zero), unroll=4)
-    dk_ref[...] = dk * SCALE
-    dv_ref[...] = dv
-
-
-def attention_key_grad(k, v, qg_all, lse_row, delta_row, query_block, block_stride, key_rows=512):
+    dk_ref[...] = rotate_back_rows(dk * SCALE, cos_ref, sin_ref).astype(dk_ref.dtype)
+    dv_ref[...] = dv.astype(dv_ref.dtype)
+
+
+def attention_key_grad(k, v, qg_all, lse_row, delta_row, cos_wide, sin_wide, query_block, block_stride, key_rows=512):
     rows = k.shape[0]
     queries = lse_row.shape[1]
     cost = pl.CostEstimate(
@@ -149,12 +159,12 @@
     return pl.pallas_call(
         functools.partial(key_grad_kernel, query_block, block_stride),
         grid=(rows // key_rows,),
-        in_specs=[row_spec, row_spec, whole, stat, stat],
+        in_specs=[row_spec, row_spec, whole, stat, stat, row_spec, row_spec],
         out_specs=[row_spec, row_spec],
-        out_shape=[jax.ShapeDtypeStruct((rows, HD), jnp.float32)] * 2,
+        out_shape=[jax.ShapeDtypeStruct((rows, HD), jnp.bfloat16)] * 2,
         compiler_params=pltpu.CompilerParams(dimension_semantics=("arbitrary",)),
         cost_estimate=cost,
-    )(k, v, qg_all, lse_row, delta_row)
+    )(k, v, qg_all, lse_row, delta_row, cos_wide, sin_wide)
 
 
 def shifted(value, axis, steps):
@@ -287,7 +297,11 @@
     )
     row_delta = jnp.sum(grad_out.astype(jnp.float32) * attended.astype(jnp.float32), axis=1)
 
-    grad_q = attention_query_grad(rot_q, grad_out, log_col, row_delta[:, None], pair_all)
+    cos_wide = jnp.stack([cos_table, cos_table], axis=-1).reshape(tok_local, HD)
+    sin_wide = jnp.stack([sin_table, -sin_table], axis=-1).reshape(tok_local, HD)
+    grad_q = attention_query_grad(
+        rot_q, grad_out, log_col, row_delta[:, None], pair_all, cos_wide, sin_wide
+    )
     stat_rows = split_exact(jnp.stack([log_total, row_delta]))
     stat_rows = stat_rows.reshape(-1, 2 * HD)
     stat_pad = (-stat_rows.shape[0]) % 16
@@ -309,12 +323,14 @@
         gathered.reshape(seq_count * block_rows, 2 * HD),
         piece_log[None, :],
         piece_delta[None, :],
+        cos_wide,
+        sin_wide,
         tok_local,
         block_rows,
     )
-    grad_queries = rotate(grad_q, cos_table, sin_table, -1.0).astype(jnp.bfloat16)[:, None, :]
-    grad_keys = rotate(grad_k, cos_table, sin_table, -1.0).astype(jnp.bfloat16)[:, None, :]
-    grad_values = grad_v.astype(jnp.bfloat16)[:, None, :]
+    grad_queries = grad_q[:, None, :]
+    grad_keys = grad_k[:, None, :]
+    grad_values = grad_v[:, None, :]
     return (grad_queries, grad_keys, grad_values)
 
 

time: 230 us -> 227 us (0.987)
  local copies, waits for them, and re-layouts: 14.4 us -> 12.1 us
where the time goes in v6:
time: 227 us
  waiting for transfers between devices  140 us (62%)
  Pallas kernels  33.1 us (15%)
  between operations  14.4 us (6%)
  blocking collectives  12.5 us (6%)
  local copies, waits for them, and re-layouts  12.1 us (5%)
  starting transfers between devices  6.9 us (3%)
  matrix products  4.87 us (2%)
  other arithmetic  3.32 us (1%)
    all_gather x1, waiting for transfers between devices, on_device(): lax.all_gather(jnp.concatenate([rot_k, plain_v], axis=1), 'seq', axis=0,...  74.1 us
    all_gather x1, waiting for transfers between devices, on_device(): lax.all_gather(packed, 'seq', axis=0, tiled=True)  59.4 us
    pallas_call x1, Pallas kernels, attention_key_grad(): pl.pallas_call(functools.partial(key_grad_kernel, query_block, block_stri...  13.1 us
    all_gather x1, blocking collectives, on_device(): lax.all_gather(grad_mixed, 'tm', axis=0, tiled=True)  12.5 us
    pallas_call x1, Pallas kernels, attention_query_grad(): pl.pallas_call(functools.partial(query_grad_kernel, key_block), grid=(row...  10.9 us
    pallas_call x1, Pallas kernels, attention_forward(): pl.pallas_call(functools.partial(forward_kernel, key_block), grid=(rows /...  9.05 us
    all_to_all x1, waiting for transfers between devices, on_device(): lax.all_to_all(projected.reshape(head_count, span_frames * slab_cells, ch...  6.01 us
    all_to_all x1, starting transfers between devices, on_device(): lax.all_to_all(projected.reshape(head_count, span_frames * slab_cells, ch...  4.94 us
  transfers between devices with their start and end apart: 4, of which 3 were waited for; matrix products, arithmetic and copies ran while one was open for 4% of the time, Pallas kernels for 9%

profile of v6, /device:TPU:2, one launch (start us, length us, event | category | flops | bytes accessed | tf_op | source)
XLA Modules:
  0.0 226.8 jit_solution(15760392632844732213)
XLA Ops:
  7.2 0.0 copy-start
  7.2 0.0 all-gather.3.cloned.1.call-start
  7.3 0.7 tile.4
  7.9 0.1 tile.10
  8.0 1.0 copy.33
  9.0 0.1 reshape.565
  9.2 0.2 fusion.36
  9.4 1.0 copy.29
  10.4 0.1 reshape.564
  10.6 0.2 fusion.35
  10.8 0.1 multiply_bitcast_fusion.2
  10.9 0.1 multiply_bitcast_fusion.1
  10.9 0.4 fusion.32
  11.4 0.0 copy-start.9
  11.4 0.5 subtract_convert_fusion
  11.9 0.0 copy-start.1
  11.9 0.1 subtract_convert_fusion.1
  12.0 0.1 copy.36
  12.1 0.1 convert_element_type.83
  12.2 0.1 copy.37.k_ref
  12.3 0.7 pad_maximum_fusion
  13.1 0.0 all-gather.3.cloned.1.call-update
  13.1 1.9 collective-permute-start
  15.1 0.1 copy.32
  15.2 0.1 convert_element_type.80
  15.3 0.8 copy.42.q_ref
  16.0 0.7 gather_fusion
  16.7 0.7 gather_fusion.1
  17.4 0.7 gather_fusion.2
  18.1 0.1 constant_dynamic-slice_fusion
  18.2 74.1 %all-gather.3.cloned.1.call-done.kv_ref = bf16[8192,256]{1,0:T(8,128)(2,1)} async-done(((bf16[512,256]{1,0:T(8,128)(2,1)}), bf16[8192,256]{1,0:T(8,128)(2,1)}) %all-gather.3.cloned.1.call-update) | async-done | bytes 4194320 | tf_op jit(solution)/shard_map/all_gather | solution.py:257
  92.3 9.1 %shard_map.112 = (bf16[512,128]{1,0:T(8,128)(2,1)}, f32[512,1]{1,0:T(8,128)}) custom-call(bf16[512,128]{1,0:T(8,128)(2,1)} %copy.42.q_ref, bf16[8192,256]{1,0:T(8,128)(2,1)} %all-gather.3.cloned.1.call-done.kv_ref), custom_call_target="tpu_custom_call" | custom-call | flops 2147483648 | bytes 4456448 | tf_op jit(solution)/shard_map/pallas_call | solution.py:62
  101.4 0.0 copy-done.4
  101.4 1.9 convolution_convert_fusion
  103.3 4.9 %all-to-all-start = ((bf16[8,64,384]{2,1,0:T(8,128)(2,1)}), bf16[8,64,384]{2,1,0:T(8,128)(2,1)S(1)}, u32[]{:S(2)}, u32[]{:S(2)}) async-start(bf16[8,64,384]{2,1,0:T(8,128)(2,1)} %bitcast.5), calls=%async_computation | async-start | bytes 786432 | tf_op jit(solution)/shard_map/all_to_all | solution.py:265
  108.3 0.3 convolution_multiply_fusion.2
  108.6 0.0 collective-permute-done
  108.6 1.0 convolution_multiply_fusion.1
  109.6 0.1 reduce.1
  109.7 0.0 copy-start.5
  109.7 6.0 %all-to-all-done = bf16[8,64,384]{2,1,0:T(8,128)(2,1)S(1)} async-done(((bf16[8,64,384]{2,1,0:T(8,128)(2,1)}), bf16[8,64,384]{2,1,0:T(8,128)(2,1)S(1)}, u32[]{:S(2)}, u32[]{:S(2)}) %all-to-all-start) | async-done | bytes 393248 | tf_op jit(solution)/shard_map/all_to_all | solution.py:265
  115.7 0.1 convert_reduce_fusion
  115.8 0.1 multiply_reduce_fusion.2
  115.9 0.1 rsqrt.15
  116.0 1.3 multiply_reduce_fusion.1
  117.3 0.1 subtract_convert_fusion.2
  117.4 12.5 %all_gather.10 = bf16[512,384]{1,0:T(8,128)(2,1)S(1)} all-gather(bf16[64,384]{1,0:T(8,128)(2,1)S(1)} %bitcast.82), channel_id=1, replica_groups=mesh['seq'=16,'tm'=8,'dp'=2] {'tm'}, dimensions={0}, use_global_device_ids=true | all-gather | bytes 442368 | tf_op jit(solution)/shard_map/all_gather | solution.py:295
  130.0 0.4 multiply_reduce_fusion
  130.3 0.0 copy-start.6
  130.4 0.8 fusion.12
  131.2 0.0 all-gather.5.cloned.1.call-update
  131.2 0.2 copy.40
  131.4 0.2 reshape.560
  131.6 0.9 copy.44.cos_ref
  132.5 0.2 copy.41
  132.7 0.2 reshape.561
  132.9 0.8 copy.45.sin_ref
  133.8 0.9 copy.43.delta_ref
  134.6 10.9 %shard_map.113 = bf16[512,128]{1,0:T(8,128)(2,1)} custom-call(bf16[512,128]{1,0:T(8,128)(2,1)} %copy.42.q_ref, bf16[512,128]{1,0:T(8,128)(2,1)} %copy-done.6, f32[512,1]{1,0:T(8,128)} %get-tuple-element.8.lse_ref, f32[512,1]{1,0:T(8,128)} %copy.43.delta_ref, bf16[8192,256]{1,0:T(8,128)(2,1)} %all-gather.3.cloned.1.call-done.kv_ref, ...), custom_call_target="tpu_custom_call" | custom-call | flops 3221225472 | bytes 4587520 | tf_op jit(solution)/shard_map/pallas_call | solution.py:112
  145.6 59.4 %all-gather.5.cloned.1.call-done.qg_ref = bf16[8448,256]{1,0:T(8,128)(2,1)} async-done(((bf16[528,256]{1,0:T(8,128)(2,1)}), bf16[8448,256]{1,0:T(8,128)(2,1)}) %all-gather.5.cloned.1.call-update) | async-done | bytes 4325392 | tf_op jit(solution)/shard_map/all_gather | solution.py:312
  205.0 0.9 slice.82
  206.0 0.2 reshape.566
  206.2 0.7 fusion.37
  206.9 13.1 %shard_map.114 = (bf16[512,128]{1,0:T(8,128)(2,1)}, bf16[512,128]{1,0:T(8,128)(2,1)}) custom-call(bf16[512,128]{1,0:T(8,128)(2,1)} %copy-done.4, bf16[512,128]{1,0:T(8,128)(2,1)} %bitcast.83, bf16[8448,256]{1,0:T(8,128)(2,1)} %all-gather.5.cloned.1.call-done.qg_ref, f32[1,8192]{1,0:T(1,128)} %bitcast.86, f32[1,8192]{1,0:T(1,128)} %bitcast.85, ...), custom_call_target="tpu_custom_call" | custom-call | flops 4294967296 | bytes 4456448 | tf_op jit(solution)/shard_map/pallas_call | solution.py:159
  (42 shorter events, 0.4 us)
Async XLA Ops:
  7.2 94.2 %copy-start = (bf16[1,128,384]{2,1,0:T(8,128)(2,1)S(1)}, bf16[1,128,384]{2,1,0:T(8,128)(2,1)}, u32[]{:S(2)}) copy-start(bf16[1,128,384]{2,1,0:T(8,128)(2,1)} %param.13) | copy-start | bytes 294916
  7.2 85.1 %all-gather.3.cloned.1.call-start = ((), (), s32[]{:S(2)}) async-start(), calls=%async_computation.1 | async-start | bytes 4456448 | tf_op jit(solution)/shard_map/all_gather | solution.py:257
  10.9 1.5 copy-start.8
  11.4 1.7 copy-start.9
  11.9 4.2 %copy-start.1 = (s32[16]{0:T(128)S(1)}, s32[16]{0:T(128)}, u32[]{:S(2)}) copy-start(s32[16]{0:T(128)} %param.16) | copy-start | bytes 196
  12.3 89.0 %copy-start.4 = (bf16[512,128]{1,0:T(8,128)(2,1)}, bf16[512,128]{1,0:T(8,128)(2,1)S(1)}, u32[]{:S(2)}) copy-start(bf16[512,128]{1,0:T(8,128)(2,1)S(1)} %copy.37.k_ref) | copy-start | bytes 393220
  13.1 95.5 %collective-permute-start = (bf16[2,32,768]{2,1,0:T(8,128)(2,1)S(1)}, bf16[2,32,768]{2,1,0:T(8,128)(2,1)S(1)}, u32[]{:S(2)}, u32[]{:S(2)}) collective-permute-start(bf16[2,32,768]{2,1,0:T(8,128)(2,1)S(1)} %copy-done.9), channel_id=1, source_target_pairs={{2,0},{4,2},{6,4},{8,6},{10,8},{12,10},{14,12},{3,1},{5,3},{7,5},{... | collective-permute-start | bytes 294920 | tf_op jit(solution)/shard_map/ppermute | solution.py:173
  18.2 90.1 %copy-start.2 = (bf16[3,384,768]{2,1,0:T(8,128)(2,1)S(1)}, bf16[3,384,768]{2,1,0:T(8,128)(2,1)}, u32[]{:S(2)}) copy-start(bf16[3,384,768]{2,1,0:T(8,128)(2,1)} %param.15) | copy-start | bytes 5308420
  101.4 8.2 %copy-start.7 = (f32[512,1]{1,0:T(8,128)S(1)}, f32[512,1]{1,0:T(8,128)}, u32[]{:S(2)}) copy-start(f32[512,1]{1,0:T(8,128)} %get-tuple-element.8.lse_ref) | copy-start | bytes 6148
  103.3 12.7 %copy-start.10 = (f32[384]{0:T(512)S(1)}, f32[384]{0:T(512)}, u32[]{:S(2)}) copy-start(f32[384]{0:T(512)} %param.14) | copy-start | bytes 4612
  103.3 12.4 %all-to-all-start = ((bf16[8,64,384]{2,1,0:T(8,128)(2,1)}), bf16[8,64,384]{2,1,0:T(8,128)(2,1)S(1)}, u32[]{:S(2)}, u32[]{:S(2)}) async-start(bf16[8,64,384]{2,1,0:T(8,128)(2,1)} %bitcast.5), calls=%async_computation | async-start | bytes 786432 | tf_op jit(solution)/shard_map/all_to_all | solution.py:265
  108.3 96.7 %all-gather.5.cloned.1.call-start = ((), (), s32[]{:S(2)}) async-start(), calls=%async_computation.2 | async-start | bytes 4595712 | tf_op jit(solution)/shard_map/all_gather | solution.py:312
  109.5 20.4 %copy-start.3 = (bf16[512,128]{1,0:T(8,128)(2,1)S(1)}, bf16[512,128]{1,0:T(8,128)(2,1)}, u32[]{:S(2)}) copy-start(bf16[512,128]{1,0:T(8,128)(2,1)} %get-tuple-element.7) | copy-start | bytes 393220
  109.7 20.7 %copy-start.5 = (bf16[512,128]{1,0:T(8,128)(2,1)S(1)}, bf16[512,128]{1,0:T(8,128)(2,1)}, u32[]{:S(2)}) copy-start(bf16[512,128]{1,0:T(8,128)(2,1)} %copy.42.q_ref) | copy-start | bytes 393220
  130.3 2.4 %copy-start.6 = (bf16[512,128]{1,0:T(8,128)(2,1)}, bf16[512,128]{1,0:T(8,128)(2,1)S(1)}, u32[]{:S(2)}) copy-start(bf16[512,128]{1,0:T(8,128)(2,1)S(1)} %get-tuple-element.40.g_ref) | copy-start | bytes 393220
Sparse Core Ops, SparseCore 0:
  13.2 79.0 all-gather.2
  131.3 73.6 all-gather.4

commit v7 on v6

--- a/solution.py
+++ b/solution.py
@@ -23,6 +23,28 @@
     partner_lane = jnp.where(lanes % 2 == 0, lanes + 1, lanes - 1)
     partner = jnp.where(ahead_lane == partner_lane, ahead, behind)
     return x * cos_ref[...] + partner * sin_ref[...]
+
+
+def prepare_kernel(q_ref, k_ref, v_ref, cos_ref, sin_ref, rq_ref, kv_ref):
+    rq_ref[...] = rotate_back_rows(q_ref[...].astype(jnp.float32), cos_ref, sin_ref).astype(
+        rq_ref.dtype
+    )
+    kv_ref[:, :HD] = rotate_back_rows(k_ref[...].astype(jnp.float32), cos_ref, sin_ref).astype(
+        kv_ref.dtype
+    )
+    kv_ref[:, HD:] = v_ref[...]
+
+
+def prepare(q, k, v, cos_wide, sin_forward):
+    rows = q.shape[0]
+    return pl.pallas_call(
+        prepare_kernel,
+        out_shape=[
+            jax.ShapeDtypeStruct((rows, HD), jnp.bfloat16),
+            jax.ShapeDtypeStruct((rows, 2 * HD), jnp.bfloat16),
+        ],
+        cost_estimate=pl.CostEstimate(flops=8 * rows * HD, transcendentals=0, bytes_accessed=14 * rows * HD),
+    )(q, k, v, cos_wide, sin_forward)
 
 
 def forward_kernel(key_block, q_ref, kv_ref, out_ref, lse_ref):
@@ -194,6 +216,30 @@
     return (jnp.cos(angles), jnp.sin(angles))
 
 
+def wide_tables(frame_pos, cell_ids):
+    pair_count = HD // 2
+    part_side = pair_count // 3
+    part_time = pair_count - 2 * part_side
+    freq = jnp.repeat(
+        jnp.concatenate(
+            [frequencies(part_time), frequencies(part_side), frequencies(part_side)]
+        ),
+        2,
+    )
+    pair = jnp.arange(HD, dtype=jnp.int32)[None, :] // 2
+    grid_row = (cell_ids // GRID_W).astype(jnp.float32)[:, None]
+    grid_col = (cell_ids % GRID_W).astype(jnp.float32)[:, None]
+    position = jnp.where(
+        pair < part_time,
+        frame_pos.astype(jnp.float32)[:, None],
+        jnp.where(pair < part_time + part_side, grid_row, grid_col),
+    )
+    angles = position * freq[None, :]
+    even = jnp.arange(HD, dtype=jnp.int32)[None, :] % 2 == 0
+    sin_angles = jnp.sin(angles)
+    return (jnp.cos(angles), jnp.where(even, sin_angles, -sin_angles))
+
+
 def rotate(vectors, cos_table, sin_table, direction):
     layout = vectors.shape
     paired = vectors.reshape(layout[:-1] + (layout[-1] // 2, 2))
@@ -246,15 +292,11 @@
     channels = head_weight.shape[2]
     frame_pos = jnp.arange(tok_local, dtype=jnp.int32) // slab_cells
     cell_ids = jnp.tile(token_cell, tok_local // slab_cells)
-    cos_table, sin_table = rope_tables(frame_pos, cell_ids)
-    rot_q = rotate(queries[:, 0, :].astype(jnp.float32), cos_table, sin_table, 1.0).astype(
-        jnp.bfloat16
-    )
-    rot_k = rotate(keys[:, 0, :].astype(jnp.float32), cos_table, sin_table, 1.0).astype(
-        jnp.bfloat16
-    )
+    cos_wide, sin_wide = wide_tables(frame_pos, cell_ids)
+    rot_q, pair = prepare(queries[:, 0, :], keys[:, 0, :], values[:, 0, :], cos_wide, -sin_wide)
+    pair_all = lax.all_gather(pair, "seq", axis=0, tiled=True)
+    rot_k = pair[:, :HD]
     plain_v = values[:, 0, :]
-    pair_all = lax.all_gather(jnp.concatenate([rot_k, plain_v], axis=1), "seq", axis=0, tiled=True)
     attended, log_col = attention_forward(rot_q, pair_all)
     log_total = log_col[:, 0]
     span_rows = span_frames * slab_cells
@@ -297,8 +339,6 @@
     )
     row_delta = jnp.sum(grad_out.astype(jnp.float32) * attended.astype(jnp.float32), axis=1)
 
-    cos_wide = jnp.stack([cos_table, cos_table], axis=-1).reshape(tok_local, HD)
-    sin_wide = jnp.stack([sin_table, -sin_table], axis=-1).reshape(tok_local, HD)
     grad_q = attention_query_grad(
         rot_q, grad_out, log_col, row_delta[:, None], pair_all, cos_wide, sin_wide
     )

time: 227 us -> 226 us (level)
  local copies, waits for them, and re-layouts: 12.1 us -> 6.47 us
  waiting for transfers between devices: 140 us -> 143 us
  Pallas kernels: 33.1 us -> 35.5 us
    convert_element_type x8 -> x0, local copies, waits for them, and re-layouts: 3.3 us -> none  [the longest x2 1.16 us: on_device(): queries[:, 0, :].astype(jnp.float32)]
  transfers between devices with their start and end apart: 4 -> 4, of which waited for: 3 -> 3; matrix products, arithmetic and copies ran while one was open for 4% -> 3% of each run, Pallas kernels for 9% -> 9%
where the time goes in v7:
time: 226 us
  waiting for transfers between devices  143 us (63%)
  Pallas kernels  35.5 us (16%)
  between operations  14.3 us (6%)
  blocking collectives  12.5 us (6%)
  starting transfers between devices  6.9 us (3%)
  local copies, waits for them, and re-layouts  6.47 us (3%)
  other arithmetic  3.66 us (2%)
  matrix products  3.33 us (1%)
    all_gather x1, waiting for transfers between devices, on_device(): pair_all = lax.all_gather(pair, 'seq', axis=0, tiled=True)  75.1 us
    all_gather x1, waiting for transfers between devices, on_device(): lax.all_gather(packed, 'seq', axis=0, tiled=True)  61.3 us
    pallas_call x1, Pallas kernels, attention_key_grad(): pl.pallas_call(functools.partial(key_grad_kernel, query_block, block_stri...  13.1 us
    all_gather x1, blocking collectives, on_device(): lax.all_gather(grad_mixed, 'tm', axis=0, tiled=True)  12.5 us
    pallas_call x1, Pallas kernels, attention_query_grad(): pl.pallas_call(functools.partial(query_grad_kernel, key_block), grid=(row...  11 us
    pallas_call x1, Pallas kernels, attention_forward(): pl.pallas_call(functools.partial(forward_kernel, key_block), grid=(rows /...  9.17 us
    all_to_all x1, waiting for transfers between devices, on_device(): lax.all_to_all(projected.reshape(head_count, span_frames * slab_cells, ch...  6.64 us
    all_to_all x1, starting transfers between devices, on_device(): lax.all_to_all(projected.reshape(head_count, span_frames * slab_cells, ch...  4.94 us
  transfers between devices with their start and end apart: 4, of which 3 were waited for; matrix products, arithmetic and copies ran while one was open for 3% of the time, Pallas kernels for 9%

profile of v7, /device:TPU:2, one launch (start us, length us, event | category | flops | bytes accessed | tf_op | source)
XLA Modules:
  0.0 225.7 jit_solution(10192455635079307049)
XLA Ops:
  7.2 0.0 copy-start
  7.2 0.0 copy-start.8
  7.2 0.0 copy-start.1
  7.2 0.0 all-gather.3.cloned.1.call-start
  7.3 0.1 pad_maximum_fusion.2
  7.4 0.1 broadcast_in_dim.80
  7.5 0.1 mul.122
  7.6 0.7 tile.4
  8.3 0.1 tile.10
  8.4 2.2 negate_select_fusion
  10.6 2.2 shard_map.112
  12.8 0.0 all-gather.3.cloned.1.call-update
  12.8 0.0 copy-done.8
  12.8 1.9 collective-permute-start
  14.8 0.0 copy-done.1
  14.8 0.7 gather_fusion
  15.4 0.7 gather_fusion.1
  16.1 0.7 gather_fusion.2
  16.8 0.1 constant_dynamic-slice_fusion
  16.9 75.1 %all-gather.3.cloned.1.call-done.kv_ref = bf16[8192,256]{1,0:T(8,128)(2,1)} async-done(((bf16[512,256]{1,0:T(8,128)(2,1)}), bf16[8192,256]{1,0:T(8,128)(2,1)}) %all-gather.3.cloned.1.call-update) | async-done | bytes 4194320 | tf_op jit(solution)/shard_map/all_gather | solution.py:297
  92.0 0.0 copy-start.2
  92.0 9.2 %shard_map.113 = (bf16[512,128]{1,0:T(8,128)(2,1)}, f32[512,1]{1,0:T(8,128)}) custom-call(bf16[512,128]{1,0:T(8,128)(2,1)} %get-tuple-element.9.q_ref, bf16[8192,256]{1,0:T(8,128)(2,1)} %all-gather.3.cloned.1.call-done.kv_ref), custom_call_target="tpu_custom_call" | custom-call | flops 2147483648 | bytes 4456448 | tf_op jit(solution)/shard_map/pallas_call | solution.py:84
  101.2 0.0 copy-start.6
  101.2 0.0 copy-done
  101.2 2.0 convolution_convert_fusion
  103.1 0.0 copy-start.9
  103.1 4.9 %all-to-all-start = ((bf16[8,64,384]{2,1,0:T(8,128)(2,1)}), bf16[8,64,384]{2,1,0:T(8,128)(2,1)S(1)}, u32[]{:S(2)}, u32[]{:S(2)}) async-start(bf16[8,64,384]{2,1,0:T(8,128)(2,1)} %bitcast.4), calls=%async_computation | async-start | bytes 786432 | tf_op jit(solution)/shard_map/all_to_all | solution.py:307
  108.1 0.0 all-gather.5.cloned.1.call-start
  108.1 0.0 copy-done.2
  108.1 0.3 convolution_multiply_fusion.2
  108.4 0.0 collective-permute-done
  108.4 0.3 convolution_multiply_fusion.1
  108.7 0.0 copy-start.4
  108.7 0.0 copy-done.6
  108.7 0.1 reduce.1
  108.9 0.0 copy-start.7
  108.9 6.6 %all-to-all-done = bf16[8,64,384]{2,1,0:T(8,128)(2,1)S(1)} async-done(((bf16[8,64,384]{2,1,0:T(8,128)(2,1)}), bf16[8,64,384]{2,1,0:T(8,128)(2,1)S(1)}, u32[]{:S(2)}, u32[]{:S(2)}) %all-to-all-start) | async-done | bytes 393248 | tf_op jit(solution)/shard_map/all_to_all | solution.py:307
  115.5 0.1 convert_reduce_fusion
  115.6 0.1 multiply_reduce_fusion.2
  115.7 0.1 rsqrt.15
  115.8 0.0 copy-done.9
  115.8 0.0 copy-start.3
  115.8 0.4 multiply_reduce_fusion.1
  116.2 0.1 subtract_convert_fusion
  116.3 12.5 %all_gather.10 = bf16[512,384]{1,0:T(8,128)(2,1)S(1)} all-gather(bf16[64,384]{1,0:T(8,128)(2,1)S(1)} %bitcast.66), channel_id=1, replica_groups=mesh['seq'=16,'tm'=8,'dp'=2] {'tm'}, dimensions={0}, use_global_device_ids=true | all-gather | bytes 442368 | tf_op jit(solution)/shard_map/all_gather | solution.py:337
  128.9 0.0 copy-done.4
  128.9 0.4 multiply_reduce_fusion
  129.2 0.0 copy-start.5
  129.3 0.0 copy-done.7
  129.3 0.8 fusion.12
  130.1 0.0 all-gather.5.cloned.1.call-update
  130.1 0.0 copy-done.3
  130.1 0.7 slice.52.k_ref
  130.8 0.9 copy.14.delta_ref
  131.6 0.0 copy-done.5
  131.6 11.0 %shard_map.114 = bf16[512,128]{1,0:T(8,128)(2,1)} custom-call(bf16[512,128]{1,0:T(8,128)(2,1)} %get-tuple-element.9.q_ref, bf16[512,128]{1,0:T(8,128)(2,1)} %copy-done.5, f32[512,1]{1,0:T(8,128)} %get-tuple-element.12.lse_ref, f32[512,1]{1,0:T(8,128)} %copy.14.delta_ref, bf16[8192,256]{1,0:T(8,128)(2,1)} %all-gather.3.cloned.1.call-done.kv_ref, ...), custom_call_target="tpu_custom_call" | custom-call | flops 3221225472 | bytes 4587520 | tf_op jit(solution)/shard_map/pallas_call | solution.py:134
  142.7 61.3 %all-gather.5.cloned.1.call-done.qg_ref = bf16[8448,256]{1,0:T(8,128)(2,1)} async-done(((bf16[528,256]{1,0:T(8,128)(2,1)}), bf16[8448,256]{1,0:T(8,128)(2,1)}) %all-gather.5.cloned.1.call-update) | async-done | bytes 4325392 | tf_op jit(solution)/shard_map/all_gather | solution.py:352
  203.9 0.9 slice.66
  204.9 0.2 reshape.346
  205.1 0.7 fusion.33
  205.8 13.1 %shard_map.115 = (bf16[512,128]{1,0:T(8,128)(2,1)}, bf16[512,128]{1,0:T(8,128)(2,1)}) custom-call(bf16[512,128]{1,0:T(8,128)(2,1)} %slice.52.k_ref, bf16[512,128]{1,0:T(8,128)(2,1)} %bitcast.70, bf16[8448,256]{1,0:T(8,128)(2,1)} %all-gather.5.cloned.1.call-done.qg_ref, f32[1,8192]{1,0:T(1,128)} %bitcast.72, f32[1,8192]{1,0:T(1,128)} %bitcast.71, ...), custom_call_target="tpu_custom_call" | custom-call | flops 4294967296 | bytes 4456448 | tf_op jit(solution)/shard_map/pallas_call | solution.py:181
  (23 shorter events, 0.3 us)
Async XLA Ops:
  7.2 94.0 %copy-start = (bf16[1,128,384]{2,1,0:T(8,128)(2,1)S(1)}, bf16[1,128,384]{2,1,0:T(8,128)(2,1)}, u32[]{:S(2)}) copy-start(bf16[1,128,384]{2,1,0:T(8,128)(2,1)} %param.13) | copy-start | bytes 294916
  7.2 5.6 %copy-start.8 = (bf16[2,32,768]{2,1,0:T(8,128)(2,1)S(1)}, bf16[2,32,768]{2,1,0:T(8,128)(2,1)}, u32[]{:S(2)}) copy-start(bf16[2,32,768]{2,1,0:T(8,128)(2,1)} %param.17) | copy-start | bytes 294916
  7.2 7.6 %copy-start.1 = (s32[16]{0:T(128)S(1)}, s32[16]{0:T(128)}, u32[]{:S(2)}) copy-start(s32[16]{0:T(128)} %param.16) | copy-start | bytes 196
  7.2 84.8 %all-gather.3.cloned.1.call-start = ((), (), s32[]{:S(2)}) async-start(), calls=%async_computation.1 | async-start | bytes 4456448 | tf_op jit(solution)/shard_map/all_gather | solution.py:297
  12.8 95.6 %collective-permute-start = (bf16[2,32,768]{2,1,0:T(8,128)(2,1)S(1)}, bf16[2,32,768]{2,1,0:T(8,128)(2,1)S(1)}, u32[]{:S(2)}, u32[]{:S(2)}) collective-permute-start(bf16[2,32,768]{2,1,0:T(8,128)(2,1)S(1)} %copy-done.8), channel_id=1, source_target_pairs={{2,0},{4,2},{6,4},{8,6},{10,8},{12,10},{14,12},{3,1},{5,3},{7,5},{... | collective-permute-start | bytes 294920 | tf_op jit(solution)/shard_map/ppermute | solution.py:195
  92.0 16.1 %copy-start.2 = (bf16[3,384,768]{2,1,0:T(8,128)(2,1)S(1)}, bf16[3,384,768]{2,1,0:T(8,128)(2,1)}, u32[]{:S(2)}) copy-start(bf16[3,384,768]{2,1,0:T(8,128)(2,1)} %param.15) | copy-start | bytes 5308420
  101.2 7.6 %copy-start.6 = (f32[512,1]{1,0:T(8,128)S(1)}, f32[512,1]{1,0:T(8,128)}, u32[]{:S(2)}) copy-start(f32[512,1]{1,0:T(8,128)} %get-tuple-element.12.lse_ref) | copy-start | bytes 6148
  103.1 12.7 %copy-start.9 = (f32[384]{0:T(512)S(1)}, f32[384]{0:T(512)}, u32[]{:S(2)}) copy-start(f32[384]{0:T(512)} %param.14) | copy-start | bytes 4612
  103.1 12.4 %all-to-all-start = ((bf16[8,64,384]{2,1,0:T(8,128)(2,1)}), bf16[8,64,384]{2,1,0:T(8,128)(2,1)S(1)}, u32[]{:S(2)}, u32[]{:S(2)}) async-start(bf16[8,64,384]{2,1,0:T(8,128)(2,1)} %bitcast.4), calls=%async_computation | async-start | bytes 786432 | tf_op jit(solution)/shard_map/all_to_all | solution.py:307
  108.1 95.9 %all-gather.5.cloned.1.call-start = ((), (), s32[]{:S(2)}) async-start(), calls=%async_computation.2 | async-start | bytes 4595712 | tf_op jit(solution)/shard_map/all_gather | solution.py:352
  108.7 20.2 %copy-start.4 = (bf16[512,128]{1,0:T(8,128)(2,1)S(1)}, bf16[512,128]{1,0:T(8,128)(2,1)}, u32[]{:S(2)}) copy-start(bf16[512,128]{1,0:T(8,128)(2,1)} %get-tuple-element.11) | copy-start | bytes 393220
  108.9 20.4 %copy-start.7 = (bf16[512,128]{1,0:T(8,128)(2,1)S(1)}, bf16[512,128]{1,0:T(8,128)(2,1)}, u32[]{:S(2)}) copy-start(bf16[512,128]{1,0:T(8,128)(2,1)} %get-tuple-element.9.q_ref) | copy-start | bytes 393220
  115.8 14.3 %copy-start.3 = (bf16[512,256]{1,0:T(8,128)(2,1)S(1)}, bf16[512,256]{1,0:T(8,128)(2,1)}, u32[]{:S(2)}) copy-start(bf16[512,256]{1,0:T(8,128)(2,1)} %get-tuple-element.10) | copy-start | bytes 786436
  129.2 2.4 %copy-start.5 = (bf16[512,128]{1,0:T(8,128)(2,1)}, bf16[512,128]{1,0:T(8,128)(2,1)S(1)}, u32[]{:S(2)}) copy-start(bf16[512,128]{1,0:T(8,128)(2,1)S(1)} %get-tuple-element.34.g_ref) | copy-start | bytes 393220
Sparse Core Ops, SparseCore 0:
  12.9 79.0 all-gather.2
  130.2 73.6 all-gather.4

commit v8 on v7

--- a/solution.py
+++ b/solution.py
@@ -295,6 +295,7 @@
     cos_wide, sin_wide = wide_tables(frame_pos, cell_ids)
     rot_q, pair = prepare(queries[:, 0, :], keys[:, 0, :], values[:, 0, :], cos_wide, -sin_wide)
     pair_all = lax.all_gather(pair, "seq", axis=0, tiled=True)
+    all_weights = lax.all_gather(head_weight[0], "tm", axis=0, tiled=False)
     rot_k = pair[:, :HD]
     plain_v = values[:, 0, :]
     attended, log_col = attention_forward(rot_q, pair_all)
@@ -334,9 +335,10 @@
         - inverse * inverse * inverse * mixed * jnp.mean(gained * mixed, axis=2, keepdims=True)
     ).astype(jnp.bfloat16)
     grad_mixed = grad_mixed.reshape(span_rows, channels)
-    grad_out = cross(lax.all_gather(grad_mixed, "tm", axis=0, tiled=True), head_weight[0]).astype(
-        jnp.bfloat16
-    )
+    grad_heads = jnp.einsum(
+        "re,hde->hrd", grad_mixed, all_weights, preferred_element_type=jnp.float32
+    ).astype(jnp.bfloat16)
+    grad_out = lax.all_to_all(grad_heads, "tm", 0, 0, tiled=False).reshape(tok_local, HD)
     row_delta = jnp.sum(grad_out.astype(jnp.float32) * attended.astype(jnp.float32), axis=1)
 
     grad_q = attention_query_grad(

time: 226 us -> 224 us (level)
  waiting for transfers between devices: 143 us -> 132 us
  starting transfers between devices: 6.9 us -> 11.7 us
  matrix products: 3.33 us -> 6.25 us
    all_gather x1, waiting for transfers between devices: 75.1 us -> 61.2 us  [on_device(): pair_all = lax.all_gather(pair, 'seq', axis=0, tiled=True)]
    all_to_all x0 -> x1, starting transfers between devices: none -> 4.73 us  [on_device(): lax.all_to_all(grad_heads, 'tm', 0, 0, tiled=False).reshape(tok_local, HD)]
    all_to_all x0 -> x1, waiting for transfers between devices: none -> 4.53 us  [on_device(): lax.all_to_all(grad_heads, 'tm', 0, 0, tiled=False).reshape(tok_local, HD)]
    dot_general x3, matrix products: 1.03 us -> 3.3 us  [on_device(): jnp.einsum('fco,io->fci', extended[offset:offset + span_frames], time_wei...]
  transfers between devices with their start and end apart: 4 -> 5, of which waited for: 3 -> 4; matrix products, arithmetic and copies ran while one was open for 3% -> 3% of each run, Pallas kernels for 9% -> 9%
where the time goes in v8:
time: 224 us; the launch traced here: 223 us
  waiting for transfers between devices  132 us (59%)
  Pallas kernels  35.4 us (16%)
  between operations  14.3 us (6%)
  blocking collectives  13.7 us (6%)
  starting transfers between devices  11.7 us (5%)
  local copies, waits for them, and re-layouts  6.47 us (3%)
  matrix products  6.25 us (3%)
  other arithmetic  3.8 us (2%)
    all_gather x1, waiting for transfers between devices, on_device(): pair_all = lax.all_gather(pair, 'seq', axis=0, tiled=True)  61.2 us
    all_gather x1, waiting for transfers between devices, on_device(): lax.all_gather(packed, 'seq', axis=0, tiled=True)  60.4 us
    all_gather x1, blocking collectives, on_device(): all_weights = lax.all_gather(head_weight[0], 'tm', axis=0, tiled=False)  13.7 us
    pallas_call x1, Pallas kernels, attention_key_grad(): pl.pallas_call(functools.partial(key_grad_kernel, query_block, block_stri...  13.1 us
    pallas_call x1, Pallas kernels, attention_query_grad(): pl.pallas_call(functools.partial(query_grad_kernel, key_block), grid=(row...  10.9 us
    pallas_call x1, Pallas kernels, attention_forward(): pl.pallas_call(functools.partial(forward_kernel, key_block), grid=(rows /...  9.17 us
    all_to_all x1, waiting for transfers between devices, on_device(): lax.all_to_all(projected.reshape(head_count, span_frames * slab_cells, ch...  5.54 us
    all_to_all x1, starting transfers between devices, on_device(): lax.all_to_all(projected.reshape(head_count, span_frames * slab_cells, ch...  5.01 us
  transfers between devices with their start and end apart: 5, of which 4 were waited for; matrix products, arithmetic and copies ran while one was open for 3% of the time, Pallas kernels for 9%

profile of v8, /device:TPU:2, one launch (start us, length us, event | category | flops | bytes accessed | tf_op | source)
XLA Modules:
  0.0 223.3 jit_solution(7862104349066166115)
XLA Ops:
  7.2 0.0 copy-start.8
  7.2 0.0 copy-start
  7.2 0.0 all-gather.3.cloned.1.call-start
  7.3 0.1 pad_maximum_fusion.2
  7.4 0.1 broadcast_in_dim.80
  7.4 0.1 mul.122
  7.6 0.7 tile.4
  8.2 0.1 tile.10
  8.3 0.0 copy-start.5
  8.3 2.2 negate_select_fusion
  10.6 2.2 shard_map.112
  12.8 0.0 all-gather.3.cloned.1.call-update
  12.8 0.0 copy-done.8
  12.8 1.9 collective-permute-start
  14.8 0.0 copy-done
  14.8 0.7 gather_fusion
  15.4 0.7 gather_fusion.1
  16.1 0.7 gather_fusion.2
  16.8 0.1 constant_dynamic-slice_fusion
  16.9 0.0 copy-done.5
  16.9 13.7 %all_gather.10 = bf16[8,128,384]{2,1,0:T(8,128)(2,1)S(1)} all-gather(bf16[1,128,384]{2,1,0:T(8,128)(2,1)S(1)} %copy-done.5), channel_id=1, replica_groups=mesh['seq'=16,'tm'=8,'dp'=2] {'tm'}, dimensions={0}, use_global_device_ids=true | all-gather | bytes 884736 | tf_op jit(solution)/shard_map/all_gather | solution.py:298
  30.6 61.2 %all-gather.3.cloned.1.call-done.kv_ref = bf16[8192,256]{1,0:T(8,128)(2,1)} async-done(((bf16[512,256]{1,0:T(8,128)(2,1)}), bf16[8192,256]{1,0:T(8,128)(2,1)}) %all-gather.3.cloned.1.call-update) | async-done | bytes 4194320 | tf_op jit(solution)/shard_map/all_gather | solution.py:297
  91.8 0.0 copy-start.2
  91.8 9.2 %shard_map.113 = (bf16[512,128]{1,0:T(8,128)(2,1)}, f32[512,1]{1,0:T(8,128)}) custom-call(bf16[512,128]{1,0:T(8,128)(2,1)} %get-tuple-element.9.q_ref, bf16[8192,256]{1,0:T(8,128)(2,1)} %all-gather.3.cloned.1.call-done.kv_ref), custom_call_target="tpu_custom_call" | custom-call | flops 2147483648 | bytes 4456448 | tf_op jit(solution)/shard_map/pallas_call | solution.py:84
  101.0 0.0 copy-start.10
  101.0 1.9 convolution_convert_fusion
  102.9 5.0 %all-to-all-start = ((bf16[8,64,384]{2,1,0:T(8,128)(2,1)}), bf16[8,64,384]{2,1,0:T(8,128)(2,1)S(1)}, u32[]{:S(2)}, u32[]{:S(2)}) async-start(bf16[8,64,384]{2,1,0:T(8,128)(2,1)} %bitcast.4), calls=%async_computation | async-start | bytes 786432 | tf_op jit(solution)/shard_map/all_to_all | solution.py:308
  107.9 0.0 copy-done.2
  107.9 1.0 convolution_multiply_fusion.2
  108.8 0.0 collective-permute-done
  108.8 0.0 copy-start.9
  108.8 1.0 convolution_multiply_fusion.1
  109.8 0.0 copy-done.9
  109.8 0.0 copy-start.6
  109.8 5.5 %all-to-all-done = bf16[8,64,384]{2,1,0:T(8,128)(2,1)S(1)} async-done(((bf16[8,64,384]{2,1,0:T(8,128)(2,1)}), bf16[8,64,384]{2,1,0:T(8,128)(2,1)S(1)}, u32[]{:S(2)}, u32[]{:S(2)}) %all-to-all-start) | async-done | bytes 393248 | tf_op jit(solution)/shard_map/all_to_all | solution.py:308
  115.3 0.1 convert_reduce_fusion
  115.4 0.0 copy-start.4
  115.4 0.1 multiply_reduce_fusion.2
  115.5 0.1 rsqrt.15
  115.6 0.0 copy-done.10
  115.6 1.4 multiply_reduce_fusion.1
  117.0 0.0 copy-start.3
  117.1 0.1 subtract_convert_fusion
  117.2 1.0 fusion
  118.2 4.7 %all-to-all-start.1 = ((bf16[8,64,128]{2,1,0:T(8,128)(2,1)}), bf16[8,64,128]{2,1,0:T(8,128)(2,1)S(1)}, u32[]{:S(2)}, u32[]{:S(2)}) async-start(bf16[8,64,128]{2,1,0:T(8,128)(2,1)} %fusion), calls=%async_computation.1 | async-start | bytes 262144 | tf_op jit(solution)/shard_map/all_to_all | solution.py:341
  122.9 0.0 all-gather.5.cloned.1.call-start
  122.9 0.0 copy-done.6
  122.9 0.1 reduce.1
  123.1 4.5 %all-to-all-done.1 = bf16[8,64,128]{2,1,0:T(8,128)(2,1)S(1)} async-done(((bf16[8,64,128]{2,1,0:T(8,128)(2,1)}), bf16[8,64,128]{2,1,0:T(8,128)(2,1)S(1)}, u32[]{:S(2)}, u32[]{:S(2)}) %all-to-all-start.1) | async-done | bytes 131104 | tf_op jit(solution)/shard_map/all_to_all | solution.py:341
  127.6 0.0 copy-done.4
  127.6 0.2 multiply_reduce_fusion
  127.8 0.0 copy-done.7
  127.8 0.7 fusion.13
  128.6 0.0 all-gather.5.cloned.1.call-update
  128.6 0.0 copy-done.3
  128.6 0.7 slice.52.k_ref
  129.3 0.9 copy.13.delta_ref
  130.1 0.0 copy-done.1
  130.1 10.9 %shard_map.114 = bf16[512,128]{1,0:T(8,128)(2,1)} custom-call(bf16[512,128]{1,0:T(8,128)(2,1)} %get-tuple-element.9.q_ref, bf16[512,128]{1,0:T(8,128)(2,1)} %bitcast.67, f32[512,1]{1,0:T(8,128)} %get-tuple-element.12.lse_ref, f32[512,1]{1,0:T(8,128)} %copy.13.delta_ref, bf16[8192,256]{1,0:T(8,128)(2,1)} %all-gather.3.cloned.1.call-done.kv_ref, ...), custom_call_target="tpu_custom_call" | custom-call | flops 3221225472 | bytes 4587520 | tf_op jit(solution)/shard_map/pallas_call | solution.py:134
  141.1 60.4 %all-gather.5.cloned.1.call-done.qg_ref = bf16[8448,256]{1,0:T(8,128)(2,1)} async-done(((bf16[528,256]{1,0:T(8,128)(2,1)}), bf16[8448,256]{1,0:T(8,128)(2,1)}) %all-gather.5.cloned.1.call-update) | async-done | bytes 4325392 | tf_op jit(solution)/shard_map/all_gather | solution.py:354
  201.5 0.9 slice.66
  202.5 0.2 reshape.350
  202.7 0.7 fusion.33
  203.4 13.1 %shard_map.115 = (bf16[512,128]{1,0:T(8,128)(2,1)}, bf16[512,128]{1,0:T(8,128)(2,1)}) custom-call(bf16[512,128]{1,0:T(8,128)(2,1)} %slice.52.k_ref, bf16[512,128]{1,0:T(8,128)(2,1)} %bitcast.75, bf16[8448,256]{1,0:T(8,128)(2,1)} %all-gather.5.cloned.1.call-done.qg_ref, f32[1,8192]{1,0:T(1,128)} %bitcast.77, f32[1,8192]{1,0:T(1,128)} %bitcast.76, ...), custom_call_target="tpu_custom_call" | custom-call | flops 4294967296 | bytes 4456448 | tf_op jit(solution)/shard_map/pallas_call | solution.py:181
  (25 shorter events, 0.3 us)
Async XLA Ops:
  7.2 5.6 %copy-start.8 = (bf16[2,32,768]{2,1,0:T(8,128)(2,1)S(1)}, bf16[2,32,768]{2,1,0:T(8,128)(2,1)}, u32[]{:S(2)}) copy-start(bf16[2,32,768]{2,1,0:T(8,128)(2,1)} %param.17) | copy-start | bytes 294916
  7.2 7.6 %copy-start = (s32[16]{0:T(128)S(1)}, s32[16]{0:T(128)}, u32[]{:S(2)}) copy-start(s32[16]{0:T(128)} %param.16) | copy-start | bytes 196
  7.2 84.6 %all-gather.3.cloned.1.call-start = ((), (), s32[]{:S(2)}) async-start(), calls=%async_computation.2 | async-start | bytes 4456448 | tf_op jit(solution)/shard_map/all_gather | solution.py:297
  8.3 8.6 %copy-start.5 = (bf16[1,128,384]{2,1,0:T(8,128)(2,1)S(1)}, bf16[1,128,384]{2,1,0:T(8,128)(2,1)}, u32[]{:S(2)}) copy-start(bf16[1,128,384]{2,1,0:T(8,128)(2,1)} %param.13) | copy-start | bytes 294916
  12.8 96.0 %collective-permute-start = (bf16[2,32,768]{2,1,0:T(8,128)(2,1)S(1)}, bf16[2,32,768]{2,1,0:T(8,128)(2,1)S(1)}, u32[]{:S(2)}, u32[]{:S(2)}) collective-permute-start(bf16[2,32,768]{2,1,0:T(8,128)(2,1)S(1)} %copy-done.8), channel_id=1, source_target_pairs={{2,0},{4,2},{6,4},{8,6},{10,8},{12,10},{14,12},{3,1},{5,3},{7,5},{... | collective-permute-start | bytes 294920 | tf_op jit(solution)/shard_map/ppermute | solution.py:195
  91.8 16.1 %copy-start.2 = (bf16[3,384,768]{2,1,0:T(8,128)(2,1)S(1)}, bf16[3,384,768]{2,1,0:T(8,128)(2,1)}, u32[]{:S(2)}) copy-start(bf16[3,384,768]{2,1,0:T(8,128)(2,1)} %param.15) | copy-start | bytes 5308420
  101.0 14.7 %copy-start.10 = (f32[384]{0:T(512)S(1)}, f32[384]{0:T(512)}, u32[]{:S(2)}) copy-start(f32[384]{0:T(512)} %param.14) | copy-start | bytes 4612
  102.9 12.5 %all-to-all-start = ((bf16[8,64,384]{2,1,0:T(8,128)(2,1)}), bf16[8,64,384]{2,1,0:T(8,128)(2,1)S(1)}, u32[]{:S(2)}, u32[]{:S(2)}) async-start(bf16[8,64,384]{2,1,0:T(8,128)(2,1)} %bitcast.4), calls=%async_computation | async-start | bytes 786432 | tf_op jit(solution)/shard_map/all_to_all | solution.py:308
  108.8 1.0 copy-start.9
  109.8 13.1 %copy-start.6 = (f32[512,1]{1,0:T(8,128)S(1)}, f32[512,1]{1,0:T(8,128)}, u32[]{:S(2)}) copy-start(f32[512,1]{1,0:T(8,128)} %get-tuple-element.12.lse_ref) | copy-start | bytes 6148
  115.4 12.2 %copy-start.4 = (bf16[512,128]{1,0:T(8,128)(2,1)S(1)}, bf16[512,128]{1,0:T(8,128)(2,1)}, u32[]{:S(2)}) copy-start(bf16[512,128]{1,0:T(8,128)(2,1)} %get-tuple-element.11) | copy-start | bytes 393220
  115.6 12.2 %copy-start.7 = (bf16[512,128]{1,0:T(8,128)(2,1)S(1)}, bf16[512,128]{1,0:T(8,128)(2,1)}, u32[]{:S(2)}) copy-start(bf16[512,128]{1,0:T(8,128)(2,1)} %get-tuple-element.9.q_ref) | copy-start | bytes 393220
  117.0 11.6 %copy-start.3 = (bf16[512,256]{1,0:T(8,128)(2,1)S(1)}, bf16[512,256]{1,0:T(8,128)(2,1)}, u32[]{:S(2)}) copy-start(bf16[512,256]{1,0:T(8,128)(2,1)} %get-tuple-element.10) | copy-start | bytes 786436
  118.2 9.4 %all-to-all-start.1 = ((bf16[8,64,128]{2,1,0:T(8,128)(2,1)}), bf16[8,64,128]{2,1,0:T(8,128)(2,1)S(1)}, u32[]{:S(2)}, u32[]{:S(2)}) async-start(bf16[8,64,128]{2,1,0:T(8,128)(2,1)} %fusion), calls=%async_computation.1 | async-start | bytes 262144 | tf_op jit(solution)/shard_map/all_to_all | solution.py:341
  122.9 78.6 %all-gather.5.cloned.1.call-start = ((), (), s32[]{:S(2)}) async-start(), calls=%async_computation.3 | async-start | bytes 4595712 | tf_op jit(solution)/shard_map/all_gather | solution.py:354
  127.6 2.5 %copy-start.1 = (bf16[8,64,128]{2,1,0:T(8,128)(2,1)}, bf16[8,64,128]{2,1,0:T(8,128)(2,1)S(1)}, u32[]{:S(2)}) copy-start(bf16[8,64,128]{2,1,0:T(8,128)(2,1)S(1)} %all-to-all-done.1) | copy-start | bytes 393220
Sparse Core Ops, SparseCore 0:
  12.9 78.8 all-gather.2
  128.7 72.7 all-gather.4

commit v9 on v8

--- a/solution.py
+++ b/solution.py
@@ -47,7 +47,7 @@
     )(q, k, v, cos_wide, sin_forward)
 
 
-def forward_kernel(key_block, q_ref, kv_ref, out_ref, lse_ref):
+def forward_kernel(key_block, q_ref, kv_ref, w_ref, out_ref, lse_ref, proj_ref):
     q = q_ref[...]
     rows = q.shape[0]
     steps = kv_ref.shape[0] // key_block
@@ -71,11 +71,15 @@
         jnp.zeros((rows, HD), jnp.float32),
     )
     top, total, acc = lax.fori_loop(0, steps, body, start_state, unroll=4)
-    out_ref[...] = (acc / total).astype(out_ref.dtype)
+    attended = (acc / total).astype(out_ref.dtype)
+    out_ref[...] = attended
+    proj_ref[...] = jnp.dot(attended, w_ref[...], preferred_element_type=jnp.float32).astype(
+        proj_ref.dtype
+    )
     lse_ref[...] = top * LN2 + jnp.log(total)
 
 
-def attention_forward(q, kv_all, query_block=512, key_block=2048):
+def attention_forward(q, kv_all, weight, query_block=512, key_block=2048):
     rows = q.shape[0]
     keys = kv_all.shape[0]
     cost = pl.CostEstimate(
@@ -87,18 +91,21 @@
         in_specs=[
             pl.BlockSpec((query_block, HD), lambda i: (i, 0)),
             pl.BlockSpec((keys, 2 * HD), lambda i: (0, 0)),
+            pl.BlockSpec(weight.shape, lambda i: (0, 0)),
         ],
         out_specs=[
             pl.BlockSpec((query_block, HD), lambda i: (i, 0)),
             pl.BlockSpec((query_block, 1), lambda i: (i, 0)),
+            pl.BlockSpec((query_block, weight.shape[1]), lambda i: (i, 0)),
         ],
         out_shape=[
             jax.ShapeDtypeStruct((rows, HD), jnp.bfloat16),
             jax.ShapeDtypeStruct((rows, 1), jnp.float32),
+            jax.ShapeDtypeStruct((rows, weight.shape[1]), jnp.bfloat16),
         ],
         compiler_params=pltpu.CompilerParams(dimension_semantics=("arbitrary",)),
         cost_estimate=cost,
-    )(q, kv_all)
+    )(q, kv_all, weight)
 
 
 def query_grad_kernel(key_block, q_ref, g_ref, lse_ref, delta_ref, kv_ref, cos_ref, sin_ref, dq_ref):
@@ -298,13 +305,10 @@
     all_weights = lax.all_gather(head_weight[0], "tm", axis=0, tiled=False)
     rot_k = pair[:, :HD]
     plain_v = values[:, 0, :]
-    attended, log_col = attention_forward(rot_q, pair_all)
+    attended, log_col, projected = attention_forward(rot_q, pair_all, head_weight[0])
     log_total = log_col[:, 0]
     span_rows = span_frames * slab_cells
     head_count = lax.axis_size("tm")
-    projected = jnp.dot(attended, head_weight[0], preferred_element_type=jnp.float32).astype(
-        jnp.bfloat16
-    )
     exchanged = lax.all_to_all(
         projected.reshape(head_count, span_frames * slab_cells, channels), "tm", 0, 0, tiled=False
     )

time: 224 us -> 221 us (0.987)
  matrix products: 6.25 us -> 2.04 us
    dot_general x3, matrix products: 3.3 us -> 1.02 us  [on_device(): jnp.einsum('fco,io->fci', extended[offset:offset + span_frames], time_wei...]
  transfers between devices with their start and end apart: 5 -> 5, of which waited for: 4 -> 4; matrix products, arithmetic and copies ran while one was open for 3% -> 2% of each run, Pallas kernels for 9% -> 9%
where the time goes in v9:
time: 221 us
  waiting for transfers between devices  132 us (60%)
  Pallas kernels  35.7 us (16%)
  between operations  14.3 us (6%)
  blocking collectives  13.7 us (6%)
  starting transfers between devices  11.9 us (5%)
  local copies, waits for them, and re-layouts  6.46 us (3%)
  other arithmetic  4.76 us (2%)
    all_gather x1, waiting for transfers between devices, on_device(): pair_all = lax.all_gather(pair, 'seq', axis=0, tiled=True)  61.2 us
    all_gather x1, waiting for transfers between devices, on_device(): lax.all_gather(packed, 'seq', axis=0, tiled=True)  60.4 us
    all_gather x1, blocking collectives, on_device(): all_weights = lax.all_gather(head_weight[0], 'tm', axis=0, tiled=False)  13.7 us
    pallas_call x1, Pallas kernels, attention_key_grad(): pl.pallas_call(functools.partial(key_grad_kernel, query_block, block_stri...  13.1 us
    pallas_call x1, Pallas kernels, attention_query_grad(): pl.pallas_call(functools.partial(query_grad_kernel, key_block), grid=(row...  11 us
    pallas_call x1, Pallas kernels, attention_forward(): pl.pallas_call(functools.partial(forward_kernel, key_block), grid=(rows /...  9.47 us
    all_to_all x1, waiting for transfers between devices, on_device(): lax.all_to_all(projected.reshape(head_count, span_frames * slab_cells, ch...  6.82 us
    all_to_all x1, starting transfers between devices, on_device(): lax.all_to_all(projected.reshape(head_count, span_frames * slab_cells, ch...  5.15 us
  transfers between devices with their start and end apart: 5, of which 4 were waited for; matrix products, arithmetic and copies ran while one was open for 2% of the time, Pallas kernels for 9%

profile of v9, /device:TPU:2, one launch (start us, length us, event | category | flops | bytes accessed | tf_op | source)
XLA Modules:
  0.0 220.8 jit_solution(1998640881240065945)
XLA Ops:
  7.2 0.0 copy-start.7
  7.2 0.0 copy-start
  7.2 0.0 all-gather.3.cloned.1.call-start
  7.3 0.1 pad_maximum_fusion.2
  7.4 0.1 broadcast_in_dim.80
  7.4 0.1 mul.122
  7.6 0.7 tile.4
  8.2 0.1 tile.10
  8.3 0.0 copy-start.6
  8.3 2.2 %negate_select_fusion = (f32[512,128]{1,0:T(8,128)}, f32[512,128]{1,0:T(8,128)}, f32[512,128]{1,0:T(8,128)}) fusion(f32[128]{0:T(128)S(1)} %mul.122, f32[512]{0:T(512)S(1)} %get-tuple-element.29, f32[512]{0:T(512)S(1)} %get-tuple-element.28, f32[512]{0:T(512)S(1)} %get-tuple-element.35, pred[128]{0:T(512)(128)(4,1)S(1)} %get-tuple-element.36, ...), kind=kLoop, calls=%fused_computation.22 | loop fusion | flops 393216 | bytes 793472 | tf_op jit(solution)/shard_map/jit(_where)/select_n | solution.py:247
  10.6 2.2 shard_map.112
  12.8 0.0 all-gather.3.cloned.1.call-update
  12.8 0.0 copy-done.7
  12.8 1.9 collective-permute-start
  14.8 0.0 copy-done
  14.8 0.7 gather_fusion
  15.4 0.7 gather_fusion.1
  16.1 0.7 gather_fusion.2
  16.8 0.1 constant_dynamic-slice_fusion
  16.9 0.0 copy-done.6
  16.9 13.7 %all_gather.10 = bf16[8,128,384]{2,1,0:T(8,128)(2,1)S(1)} all-gather(bf16[1,128,384]{2,1,0:T(8,128)(2,1)S(1)} %copy-done.6), channel_id=1, replica_groups=mesh['seq'=16,'tm'=8,'dp'=2] {'tm'}, dimensions={0}, use_global_device_ids=true | all-gather | bytes 884736 | tf_op jit(solution)/shard_map/all_gather | solution.py:305
  30.6 61.2 %all-gather.3.cloned.1.call-done.kv_ref = bf16[8192,256]{1,0:T(8,128)(2,1)} async-done(((bf16[512,256]{1,0:T(8,128)(2,1)}), bf16[8192,256]{1,0:T(8,128)(2,1)}) %all-gather.3.cloned.1.call-update) | async-done | bytes 4194320 | tf_op jit(solution)/shard_map/all_gather | solution.py:304
  91.8 0.0 copy-start.2
  91.8 9.5 %shard_map.113 = (bf16[512,128]{1,0:T(8,128)(2,1)}, f32[512,1]{1,0:T(8,128)}, bf16[512,384]{1,0:T(8,128)(2,1)}) custom-call(bf16[512,128]{1,0:T(8,128)(2,1)} %get-tuple-element.10.q_ref, bf16[8192,256]{1,0:T(8,128)(2,1)} %all-gather.3.cloned.1.call-done.kv_ref, bf16[128,384]{1,0:T(8,128)(2,1)} %bitcast.74), custom_call_target="tpu_custom_call" | custom-call | flops 2147483648 | bytes 4456448 | tf_op jit(solution)/shard_map/pallas_call | solution.py:88
  101.2 0.0 copy-start.8
  101.3 5.2 %all-to-all-start = ((bf16[8,64,384]{2,1,0:T(8,128)(2,1)}), bf16[8,64,384]{2,1,0:T(8,128)(2,1)S(1)}, u32[]{:S(2)}, u32[]{:S(2)}) async-start(bf16[8,64,384]{2,1,0:T(8,128)(2,1)} %bitcast.68), calls=%async_computation | async-start | bytes 786432 | tf_op jit(solution)/shard_map/all_to_all | solution.py:312
  106.4 0.0 copy-done.2
  106.4 0.3 convolution_multiply_fusion.2
  106.7 0.0 collective-permute-done
  106.7 0.3 convolution_multiply_fusion.1
  107.0 6.8 %all-to-all-done = bf16[8,64,384]{2,1,0:T(8,128)(2,1)S(1)} async-done(((bf16[8,64,384]{2,1,0:T(8,128)(2,1)}), bf16[8,64,384]{2,1,0:T(8,128)(2,1)S(1)}, u32[]{:S(2)}, u32[]{:S(2)}) %all-to-all-start) | async-done | bytes 393248 | tf_op jit(solution)/shard_map/all_to_all | solution.py:312
  113.9 0.1 convert_reduce_fusion
  113.9 0.0 copy-start.4
  113.9 0.1 multiply_reduce_fusion.2
  114.1 0.1 rsqrt.15
  114.1 0.0 copy-done.8
  114.1 0.0 copy-start.5
  114.2 0.4 multiply_reduce_fusion.1
  114.6 0.0 copy-start.3
  114.6 0.1 subtract_convert_fusion
  114.7 1.0 fusion
  115.7 4.8 %all-to-all-start.1 = ((bf16[8,64,128]{2,1,0:T(8,128)(2,1)}), bf16[8,64,128]{2,1,0:T(8,128)(2,1)S(1)}, u32[]{:S(2)}, u32[]{:S(2)}) async-start(bf16[8,64,128]{2,1,0:T(8,128)(2,1)} %fusion), calls=%async_computation.1 | async-start | bytes 262144 | tf_op jit(solution)/shard_map/all_to_all | solution.py:345
  120.4 0.0 all-gather.5.cloned.1.call-start
  120.5 1.1 reduce.1
  121.5 3.6 %all-to-all-done.1 = bf16[8,64,128]{2,1,0:T(8,128)(2,1)S(1)} async-done(((bf16[8,64,128]{2,1,0:T(8,128)(2,1)}), bf16[8,64,128]{2,1,0:T(8,128)(2,1)S(1)}, u32[]{:S(2)}, u32[]{:S(2)}) %all-to-all-start.1) | async-done | bytes 131104 | tf_op jit(solution)/shard_map/all_to_all | solution.py:345
  125.1 0.0 copy-start.1
  125.1 0.0 copy-done.4
  125.1 0.2 multiply_reduce_fusion
  125.3 0.0 copy-done.5
  125.4 0.8 fusion.13
  126.1 0.0 all-gather.5.cloned.1.call-update
  126.1 0.0 copy-done.3
  126.1 0.7 slice.52.k_ref
  126.8 0.9 copy.13.delta_ref
  127.7 0.0 copy-done.1
  127.7 11.0 %shard_map.114 = bf16[512,128]{1,0:T(8,128)(2,1)} custom-call(bf16[512,128]{1,0:T(8,128)(2,1)} %get-tuple-element.10.q_ref, bf16[512,128]{1,0:T(8,128)(2,1)} %bitcast.64, f32[512,1]{1,0:T(8,128)} %get-tuple-element.13.lse_ref, f32[512,1]{1,0:T(8,128)} %copy.13.delta_ref, bf16[8192,256]{1,0:T(8,128)(2,1)} %all-gather.3.cloned.1.call-done.kv_ref, ...), custom_call_target="tpu_custom_call" | custom-call | flops 3221225472 | bytes 4587520 | tf_op jit(solution)/shard_map/pallas_call | solution.py:141
  138.6 60.4 %all-gather.5.cloned.1.call-done.qg_ref = bf16[8448,256]{1,0:T(8,128)(2,1)} async-done(((bf16[528,256]{1,0:T(8,128)(2,1)}), bf16[8448,256]{1,0:T(8,128)(2,1)}) %all-gather.5.cloned.1.call-update) | async-done | bytes 4325392 | tf_op jit(solution)/shard_map/all_gather | solution.py:358
  199.0 0.9 slice.66
  200.0 0.2 reshape.350
  200.3 0.7 fusion.32
  200.9 13.1 %shard_map.115 = (bf16[512,128]{1,0:T(8,128)(2,1)}, bf16[512,128]{1,0:T(8,128)(2,1)}) custom-call(bf16[512,128]{1,0:T(8,128)(2,1)} %slice.52.k_ref, bf16[512,128]{1,0:T(8,128)(2,1)} %bitcast.73, bf16[8448,256]{1,0:T(8,128)(2,1)} %all-gather.5.cloned.1.call-done.qg_ref, f32[1,8192]{1,0:T(1,128)} %bitcast.76, f32[1,8192]{1,0:T(1,128)} %bitcast.75, ...), custom_call_target="tpu_custom_call" | custom-call | flops 4294967296 | bytes 4456448 | tf_op jit(solution)/shard_map/pallas_call | solution.py:188
  (23 shorter events, 0.3 us)
Async XLA Ops:
  7.2 5.6 %copy-start.7 = (bf16[2,32,768]{2,1,0:T(8,128)(2,1)S(1)}, bf16[2,32,768]{2,1,0:T(8,128)(2,1)}, u32[]{:S(2)}) copy-start(bf16[2,32,768]{2,1,0:T(8,128)(2,1)} %param.17) | copy-start | bytes 294916
  7.2 7.6 %copy-start = (s32[16]{0:T(128)S(1)}, s32[16]{0:T(128)}, u32[]{:S(2)}) copy-start(s32[16]{0:T(128)} %param.16) | copy-start | bytes 196
  7.2 84.6 %all-gather.3.cloned.1.call-start = ((), (), s32[]{:S(2)}) async-start(), calls=%async_computation.2 | async-start | bytes 4456448 | tf_op jit(solution)/shard_map/all_gather | solution.py:304
  8.3 8.6 %copy-start.6 = (bf16[1,128,384]{2,1,0:T(8,128)(2,1)S(1)}, bf16[1,128,384]{2,1,0:T(8,128)(2,1)}, u32[]{:S(2)}) copy-start(bf16[1,128,384]{2,1,0:T(8,128)(2,1)} %param.13) | copy-start | bytes 294916
  12.8 93.9 %collective-permute-start = (bf16[2,32,768]{2,1,0:T(8,128)(2,1)S(1)}, bf16[2,32,768]{2,1,0:T(8,128)(2,1)S(1)}, u32[]{:S(2)}, u32[]{:S(2)}) collective-permute-start(bf16[2,32,768]{2,1,0:T(8,128)(2,1)S(1)} %copy-done.7), channel_id=1, source_target_pairs={{2,0},{4,2},{6,4},{8,6},{10,8},{12,10},{14,12},{3,1},{5,3},{7,5},{... | collective-permute-start | bytes 294920 | tf_op jit(solution)/shard_map/ppermute | solution.py:202
  91.8 14.6 %copy-start.2 = (bf16[3,384,768]{2,1,0:T(8,128)(2,1)S(1)}, bf16[3,384,768]{2,1,0:T(8,128)(2,1)}, u32[]{:S(2)}) copy-start(bf16[3,384,768]{2,1,0:T(8,128)(2,1)} %param.15) | copy-start | bytes 5308420
  101.2 12.9 %copy-start.8 = (f32[384]{0:T(512)S(1)}, f32[384]{0:T(512)}, u32[]{:S(2)}) copy-start(f32[384]{0:T(512)} %param.14) | copy-start | bytes 4612
  101.3 12.6 %all-to-all-start = ((bf16[8,64,384]{2,1,0:T(8,128)(2,1)}), bf16[8,64,384]{2,1,0:T(8,128)(2,1)S(1)}, u32[]{:S(2)}, u32[]{:S(2)}) async-start(bf16[8,64,384]{2,1,0:T(8,128)(2,1)} %bitcast.68), calls=%async_computation | async-start | bytes 786432 | tf_op jit(solution)/shard_map/all_to_all | solution.py:312
  113.9 11.2 %copy-start.4 = (bf16[512,128]{1,0:T(8,128)(2,1)S(1)}, bf16[512,128]{1,0:T(8,128)(2,1)}, u32[]{:S(2)}) copy-start(bf16[512,128]{1,0:T(8,128)(2,1)} %get-tuple-element.14) | copy-start | bytes 393220
  114.1 11.2 %copy-start.5 = (bf16[512,128]{1,0:T(8,128)(2,1)S(1)}, bf16[512,128]{1,0:T(8,128)(2,1)}, u32[]{:S(2)}) copy-start(bf16[512,128]{1,0:T(8,128)(2,1)} %get-tuple-element.10.q_ref) | copy-start | bytes 393220
  114.6 11.6 %copy-start.3 = (bf16[512,256]{1,0:T(8,128)(2,1)S(1)}, bf16[512,256]{1,0:T(8,128)(2,1)}, u32[]{:S(2)}) copy-start(bf16[512,256]{1,0:T(8,128)(2,1)} %get-tuple-element.11) | copy-start | bytes 786436
  115.7 9.4 %all-to-all-start.1 = ((bf16[8,64,128]{2,1,0:T(8,128)(2,1)}), bf16[8,64,128]{2,1,0:T(8,128)(2,1)S(1)}, u32[]{:S(2)}, u32[]{:S(2)}) async-start(bf16[8,64,128]{2,1,0:T(8,128)(2,1)} %fusion), calls=%async_computation.1 | async-start | bytes 262144 | tf_op jit(solution)/shard_map/all_to_all | solution.py:345
  120.4 78.6 %all-gather.5.cloned.1.call-start = ((), (), s32[]{:S(2)}) async-start(), calls=%async_computation.3 | async-start | bytes 4595712 | tf_op jit(solution)/shard_map/all_gather | solution.py:358
  125.1 2.5 %copy-start.1 = (bf16[8,64,128]{2,1,0:T(8,128)(2,1)}, bf16[8,64,128]{2,1,0:T(8,128)(2,1)S(1)}, u32[]{:S(2)}) copy-start(bf16[8,64,128]{2,1,0:T(8,128)(2,1)S(1)} %all-to-all-done.1) | copy-start | bytes 393220
Sparse Core Ops, SparseCore 0:
  12.9 78.8 all-gather.2
  126.3 72.7 all-gather.4

commit v10 on v9

--- a/solution.py
+++ b/solution.py
@@ -149,19 +149,29 @@
     )(q, g, lse_col, delta_col, kv_all, cos_wide, sin_wide)
 
 
-def key_grad_kernel(query_block, block_stride, k_ref, v_ref, qg_ref, lse_ref, delta_ref, cos_ref, sin_ref, dk_ref, dv_ref):
+def stat_row(tile, stat, halves):
+    parts = []
+    for half in range(halves):
+        row = stat * halves + half
+        step = 2 * halves
+        parts.append((tile[row : row + 1] + tile[step + row : step + row + 1]) + tile[2 * step + row : 2 * step + row + 1])
+    return jnp.concatenate(parts, axis=1)
+
+
+def key_grad_kernel(query_block, block_stride, blocks, k_ref, v_ref, qg_ref, cos_ref, sin_ref, dk_ref, dv_ref):
     k = k_ref[...]
     v = v_ref[...]
-    steps = lse_ref.shape[1] // query_block
+    steps = blocks
+    halves = query_block // (2 * HD)
 
     def body(step, carry):
         dk, dv = carry
         start = pl.multiple_of(step * block_stride, 16)
-        column = pl.multiple_of(step * query_block, query_block)
         q = qg_ref[pl.ds(start, query_block), :HD]
         g = qg_ref[pl.ds(start, query_block), HD:]
-        lse = lse_ref[:, pl.ds(column, query_block)]
-        delta = delta_ref[:, pl.ds(column, query_block)]
+        tile = qg_ref[pl.ds(start + query_block, 16), :].astype(jnp.float32)
+        lse = stat_row(tile, 0, halves)
+        delta = stat_row(tile, 1, halves)
         s = lax.dot_general(k, q, (((1,), (1,)), ((), ())), preferred_element_type=jnp.float32) * (SCALE * LOG2E)
         w = jnp.exp2(s - lse * LOG2E)
         gw = lax.dot_general(v, g, (((1,), (1,)), ((), ())), preferred_element_type=jnp.float32)
@@ -176,24 +186,24 @@
     dv_ref[...] = dv.astype(dv_ref.dtype)
 
 
-def attention_key_grad(k, v, qg_all, lse_row, delta_row, cos_wide, sin_wide, query_block, block_stride, key_rows=512):
+def attention_key_grad(k, v, qg_all, cos_wide, sin_wide, query_block, block_stride, key_rows=512):
     rows = k.shape[0]
-    queries = lse_row.shape[1]
+    blocks = qg_all.shape[0] // block_stride
+    queries = blocks * query_block
     cost = pl.CostEstimate(
         flops=8 * rows * queries * HD, transcendentals=rows * queries, bytes_accessed=2 * HD * (2 * rows + 2 * queries)
     )
     row_spec = pl.BlockSpec((key_rows, HD), lambda i: (i, 0))
     whole = pl.BlockSpec(qg_all.shape, lambda i: (0, 0))
-    stat = pl.BlockSpec((1, queries), lambda i: (0, 0))
     return pl.pallas_call(
-        functools.partial(key_grad_kernel, query_block, block_stride),
+        functools.partial(key_grad_kernel, query_block, block_stride, blocks),
         grid=(rows // key_rows,),
-        in_specs=[row_spec, row_spec, whole, stat, stat, row_spec, row_spec],
+        in_specs=[row_spec, row_spec, whole, row_spec, row_spec],
         out_specs=[row_spec, row_spec],
         out_shape=[jax.ShapeDtypeStruct((rows, HD), jnp.bfloat16)] * 2,
         compiler_params=pltpu.CompilerParams(dimension_semantics=("arbitrary",)),
         cost_estimate=cost,
-    )(k, v, qg_all, lse_row, delta_row, cos_wide, sin_wide)
+    )(k, v, qg_all, cos_wide, sin_wide)
 
 
 def shifted(value, axis, steps):
@@ -358,17 +368,10 @@
     gathered = lax.all_gather(packed, "seq", axis=0, tiled=True).reshape(
         seq_count, block_rows, 2 * HD
     )
-    stat_all = gathered[:, tok_local:, :].reshape(seq_count, -1)[:, : 6 * tok_local]
-    stat_all = stat_all.reshape(seq_count, 3, 2, tok_local).astype(jnp.float32)
-    stat_all = (stat_all[:, 0] + stat_all[:, 1]) + stat_all[:, 2]
-    piece_log = stat_all[:, 0, :].reshape(-1)
-    piece_delta = stat_all[:, 1, :].reshape(-1)
     grad_k, grad_v = attention_key_grad(
         rot_k,
         plain_v,
         gathered.reshape(seq_count * block_rows, 2 * HD),
-        piece_log[None, :],
-        piece_delta[None, :],
         cos_wide,
         sin_wide,
         tok_local,

time: 221 us -> 219 us (level)
  no operation moved by 1% of the time
where the time goes in v10:
time: 219 us
  waiting for transfers between devices  132 us (60%)
  Pallas kernels  35.6 us (16%)
  between operations  14.3 us (7%)
  blocking collectives  13.7 us (6%)
  starting transfers between devices  11.8 us (5%)
  other arithmetic  4.71 us (2%)
  local copies, waits for them, and re-layouts  4.66 us (2%)
    all_gather x1, waiting for transfers between devices, on_device(): pair_all = lax.all_gather(pair, 'seq', axis=0, tiled=True)  61.2 us
    all_gather x1, waiting for transfers between devices, on_device(): lax.all_gather(packed, 'seq', axis=0, tiled=True)  60.4 us
    all_gather x1, blocking collectives, on_device(): all_weights = lax.all_gather(head_weight[0], 'tm', axis=0, tiled=False)  13.7 us
    pallas_call x1, Pallas kernels, attention_key_grad(): pl.pallas_call(functools.partial(key_grad_kernel, query_block, block_stri...  13 us
    pallas_call x1, Pallas kernels, attention_query_grad(): pl.pallas_call(functools.partial(query_grad_kernel, key_block), grid=(row...  11 us
    pallas_call x1, Pallas kernels, attention_forward(): pl.pallas_call(functools.partial(forward_kernel, key_block), grid=(rows /...  9.46 us
    all_to_all x1, waiting for transfers between devices, on_device(): lax.all_to_all(projected.reshape(head_count, span_frames * slab_cells, ch...  6.82 us
    all_to_all x1, starting transfers between devices, on_device(): lax.all_to_all(projected.reshape(head_count, span_frames * slab_cells, ch...  5.16 us
  transfers between devices with their start and end apart: 5, of which 4 were waited for; matrix products, arithmetic and copies ran while one was open for 2% of the time, Pallas kernels for 9%

profile of v10, /device:TPU:2, one launch (start us, length us, event | category | flops | bytes accessed | tf_op | source)
XLA Modules:
  0.0 218.9 jit_solution(2882054605263735485)
XLA Ops:
  7.2 0.0 copy-start.7
  7.2 0.0 copy-start
  7.2 0.0 all-gather.3.cloned.1.call-start
  7.3 0.1 pad_maximum_fusion.2
  7.4 0.1 broadcast_in_dim.80
  7.4 0.1 mul.122
  7.6 0.7 tile.4
  8.2 0.1 tile.10
  8.3 0.0 copy-start.6
  8.3 2.2 %negate_select_fusion = (f32[512,128]{1,0:T(8,128)}, f32[512,128]{1,0:T(8,128)}, f32[512,128]{1,0:T(8,128)}) fusion(f32[128]{0:T(128)S(1)} %mul.122, f32[512]{0:T(512)S(1)} %get-tuple-element.27, f32[512]{0:T(512)S(1)} %get-tuple-element.26, f32[512]{0:T(512)S(1)} %get-tuple-element.33, pred[128]{0:T(512)(128)(4,1)S(1)} %get-tuple-element.34, ...), kind=kLoop, calls=%fused_computation.22 | loop fusion | flops 393216 | bytes 793472 | tf_op jit(solution)/shard_map/jit(_where)/select_n | solution.py:257
  10.6 2.2 %shard_map.112 = (bf16[512,128]{1,0:T(8,128)(2,1)}, bf16[512,256]{1,0:T(8,128)(2,1)}) custom-call(bf16[512,128]{1,0:T(8,128)(2,1)} %bitcast.61, bf16[512,128]{1,0:T(8,128)(2,1)} %bitcast.62, bf16[512,128]{1,0:T(8,128)(2,1)} %bitcast.63, f32[512,128]{1,0:T(8,128)} %get-tuple-element.19.cos_ref, f32[512,128]{1,0:T(8,128)} %get-tuple-element.18.sin_ref), custom_call_target="tpu_custom_call" | custom-call | flops 524288 | bytes 917504 | tf_op jit(solution)/shard_map/pallas_call | solution.py:40
  12.8 0.0 all-gather.3.cloned.1.call-update
  12.8 0.0 copy-done.7
  12.8 1.9 collective-permute-start
  14.8 0.0 copy-done
  14.8 0.7 gather_fusion
  15.5 0.7 gather_fusion.1
  16.1 0.7 gather_fusion.2
  16.8 0.1 constant_dynamic-slice_fusion
  16.9 0.0 copy-done.6
  16.9 13.7 %all_gather.10 = bf16[8,128,384]{2,1,0:T(8,128)(2,1)S(1)} all-gather(bf16[1,128,384]{2,1,0:T(8,128)(2,1)S(1)} %copy-done.6), channel_id=1, replica_groups=mesh['seq'=16,'tm'=8,'dp'=2] {'tm'}, dimensions={0}, use_global_device_ids=true | all-gather | bytes 884736 | tf_op jit(solution)/shard_map/all_gather | solution.py:315
  30.6 61.2 %all-gather.3.cloned.1.call-done.kv_ref = bf16[8192,256]{1,0:T(8,128)(2,1)} async-done(((bf16[512,256]{1,0:T(8,128)(2,1)}), bf16[8192,256]{1,0:T(8,128)(2,1)}) %all-gather.3.cloned.1.call-update) | async-done | bytes 4194320 | tf_op jit(solution)/shard_map/all_gather | solution.py:314
  91.8 0.0 copy-start.2
  91.8 9.5 %shard_map.113 = (bf16[512,128]{1,0:T(8,128)(2,1)}, f32[512,1]{1,0:T(8,128)}, bf16[512,384]{1,0:T(8,128)(2,1)}) custom-call(bf16[512,128]{1,0:T(8,128)(2,1)} %get-tuple-element.10.q_ref, bf16[8192,256]{1,0:T(8,128)(2,1)} %all-gather.3.cloned.1.call-done.kv_ref, bf16[128,384]{1,0:T(8,128)(2,1)} %bitcast.65), custom_call_target="tpu_custom_call" | custom-call | flops 2147483648 | bytes 4456448 | tf_op jit(solution)/shard_map/pallas_call | solution.py:88
  101.3 0.0 copy-start.8
  101.3 5.2 %all-to-all-start = ((bf16[8,64,384]{2,1,0:T(8,128)(2,1)}), bf16[8,64,384]{2,1,0:T(8,128)(2,1)S(1)}, u32[]{:S(2)}, u32[]{:S(2)}) async-start(bf16[8,64,384]{2,1,0:T(8,128)(2,1)} %bitcast.59), calls=%async_computation | async-start | bytes 786432 | tf_op jit(solution)/shard_map/all_to_all | solution.py:322
  106.4 0.0 copy-done.2
  106.4 0.3 convolution_multiply_fusion.2
  106.7 0.0 collective-permute-done
  106.7 0.3 convolution_multiply_fusion.1
  107.1 6.8 %all-to-all-done = bf16[8,64,384]{2,1,0:T(8,128)(2,1)S(1)} async-done(((bf16[8,64,384]{2,1,0:T(8,128)(2,1)}), bf16[8,64,384]{2,1,0:T(8,128)(2,1)S(1)}, u32[]{:S(2)}, u32[]{:S(2)}) %all-to-all-start) | async-done | bytes 393248 | tf_op jit(solution)/shard_map/all_to_all | solution.py:322
  113.9 0.1 convert_reduce_fusion
  113.9 0.0 copy-start.4
  113.9 0.1 multiply_reduce_fusion.2
  114.1 0.1 rsqrt.15
  114.2 0.0 copy-done.8
  114.2 0.0 copy-start.5
  114.2 0.4 multiply_reduce_fusion.1
  114.6 0.0 copy-start.3
  114.6 0.1 subtract_convert_fusion
  114.7 1.0 fusion
  115.7 4.7 %all-to-all-start.1 = ((bf16[8,64,128]{2,1,0:T(8,128)(2,1)}), bf16[8,64,128]{2,1,0:T(8,128)(2,1)S(1)}, u32[]{:S(2)}, u32[]{:S(2)}) async-start(bf16[8,64,128]{2,1,0:T(8,128)(2,1)} %fusion), calls=%async_computation.1 | async-start | bytes 262144 | tf_op jit(solution)/shard_map/all_to_all | solution.py:355
  120.5 0.0 all-gather.5.cloned.1.call-start
  120.5 1.1 reduce.1
  121.5 3.6 %all-to-all-done.1 = bf16[8,64,128]{2,1,0:T(8,128)(2,1)S(1)} async-done(((bf16[8,64,128]{2,1,0:T(8,128)(2,1)}), bf16[8,64,128]{2,1,0:T(8,128)(2,1)S(1)}, u32[]{:S(2)}, u32[]{:S(2)}) %all-to-all-start.1) | async-done | bytes 131104 | tf_op jit(solution)/shard_map/all_to_all | solution.py:355
  125.1 0.0 copy-start.1
  125.1 0.0 copy-done.4
  125.1 0.2 multiply_reduce_fusion
  125.3 0.0 copy-done.5
  125.4 0.7 fusion.13
  126.1 0.0 all-gather.5.cloned.1.call-update
  126.1 0.0 copy-done.3
  126.1 0.7 slice.31.k_ref
  126.8 0.9 copy.13.delta_ref
  127.6 0.0 copy-done.1
  127.7 11.0 %shard_map.114 = bf16[512,128]{1,0:T(8,128)(2,1)} custom-call(bf16[512,128]{1,0:T(8,128)(2,1)} %get-tuple-element.10.q_ref, bf16[512,128]{1,0:T(8,128)(2,1)} %bitcast.57, f32[512,1]{1,0:T(8,128)} %get-tuple-element.13.lse_ref, f32[512,1]{1,0:T(8,128)} %copy.13.delta_ref, bf16[8192,256]{1,0:T(8,128)(2,1)} %all-gather.3.cloned.1.call-done.kv_ref, ...), custom_call_target="tpu_custom_call" | custom-call | flops 3221225472 | bytes 4587520 | tf_op jit(solution)/shard_map/pallas_call | solution.py:141
  138.6 60.4 %all-gather.5.cloned.1.call-done.qg_ref = bf16[8448,256]{1,0:T(8,128)(2,1)} async-done(((bf16[528,256]{1,0:T(8,128)(2,1)}), bf16[8448,256]{1,0:T(8,128)(2,1)}) %all-gather.5.cloned.1.call-update) | async-done | bytes 4325392 | tf_op jit(solution)/shard_map/all_gather | solution.py:368
  199.0 13.0 %shard_map.115 = (bf16[512,128]{1,0:T(8,128)(2,1)}, bf16[512,128]{1,0:T(8,128)(2,1)}) custom-call(bf16[512,128]{1,0:T(8,128)(2,1)} %slice.31.k_ref, bf16[512,128]{1,0:T(8,128)(2,1)} %bitcast.64, bf16[8448,256]{1,0:T(8,128)(2,1)} %all-gather.5.cloned.1.call-done.qg_ref, f32[512,128]{1,0:T(8,128)} %get-tuple-element.19.cos_ref, ...), custom_call_target="tpu_custom_call" | custom-call | flops 4294967296 | bytes 4456448 | tf_op jit(solution)/shard_map/pallas_call | solution.py:198
  (20 shorter events, 0.2 us)
Async XLA Ops:
  7.2 5.6 %copy-start.7 = (bf16[2,32,768]{2,1,0:T(8,128)(2,1)S(1)}, bf16[2,32,768]{2,1,0:T(8,128)(2,1)}, u32[]{:S(2)}) copy-start(bf16[2,32,768]{2,1,0:T(8,128)(2,1)} %param.17) | copy-start | bytes 294916
  7.2 7.6 %copy-start = (s32[16]{0:T(128)S(1)}, s32[16]{0:T(128)}, u32[]{:S(2)}) copy-start(s32[16]{0:T(128)} %param.16) | copy-start | bytes 196
  7.2 84.6 %all-gather.3.cloned.1.call-start = ((), (), s32[]{:S(2)}) async-start(), calls=%async_computation.2 | async-start | bytes 4456448 | tf_op jit(solution)/shard_map/all_gather | solution.py:314
  8.3 8.6 %copy-start.6 = (bf16[1,128,384]{2,1,0:T(8,128)(2,1)S(1)}, bf16[1,128,384]{2,1,0:T(8,128)(2,1)}, u32[]{:S(2)}) copy-start(bf16[1,128,384]{2,1,0:T(8,128)(2,1)} %param.13) | copy-start | bytes 294916
  12.8 93.9 %collective-permute-start = (bf16[2,32,768]{2,1,0:T(8,128)(2,1)S(1)}, bf16[2,32,768]{2,1,0:T(8,128)(2,1)S(1)}, u32[]{:S(2)}, u32[]{:S(2)}) collective-permute-start(bf16[2,32,768]{2,1,0:T(8,128)(2,1)S(1)} %copy-done.7), channel_id=1, source_target_pairs={{2,0},{4,2},{6,4},{8,6},{10,8},{12,10},{14,12},{3,1},{5,3},{7,5},{... | collective-permute-start | bytes 294920 | tf_op jit(solution)/shard_map/ppermute | solution.py:212
  91.8 14.6 %copy-start.2 = (bf16[3,384,768]{2,1,0:T(8,128)(2,1)S(1)}, bf16[3,384,768]{2,1,0:T(8,128)(2,1)}, u32[]{:S(2)}) copy-start(bf16[3,384,768]{2,1,0:T(8,128)(2,1)} %param.15) | copy-start | bytes 5308420
  101.3 12.9 %copy-start.8 = (f32[384]{0:T(512)S(1)}, f32[384]{0:T(512)}, u32[]{:S(2)}) copy-start(f32[384]{0:T(512)} %param.14) | copy-start | bytes 4612
  101.3 12.6 %all-to-all-start = ((bf16[8,64,384]{2,1,0:T(8,128)(2,1)}), bf16[8,64,384]{2,1,0:T(8,128)(2,1)S(1)}, u32[]{:S(2)}, u32[]{:S(2)}) async-start(bf16[8,64,384]{2,1,0:T(8,128)(2,1)} %bitcast.59), calls=%async_computation | async-start | bytes 786432 | tf_op jit(solution)/shard_map/all_to_all | solution.py:322
  113.9 11.2 %copy-start.4 = (bf16[512,128]{1,0:T(8,128)(2,1)S(1)}, bf16[512,128]{1,0:T(8,128)(2,1)}, u32[]{:S(2)}) copy-start(bf16[512,128]{1,0:T(8,128)(2,1)} %get-tuple-element.14) | copy-start | bytes 393220
  114.2 11.2 %copy-start.5 = (bf16[512,128]{1,0:T(8,128)(2,1)S(1)}, bf16[512,128]{1,0:T(8,128)(2,1)}, u32[]{:S(2)}) copy-start(bf16[512,128]{1,0:T(8,128)(2,1)} %get-tuple-element.10.q_ref) | copy-start | bytes 393220
  114.6 11.6 %copy-start.3 = (bf16[512,256]{1,0:T(8,128)(2,1)S(1)}, bf16[512,256]{1,0:T(8,128)(2,1)}, u32[]{:S(2)}) copy-start(bf16[512,256]{1,0:T(8,128)(2,1)} %get-tuple-element.11) | copy-start | bytes 786436
  115.7 9.4 %all-to-all-start.1 = ((bf16[8,64,128]{2,1,0:T(8,128)(2,1)}), bf16[8,64,128]{2,1,0:T(8,128)(2,1)S(1)}, u32[]{:S(2)}, u32[]{:S(2)}) async-start(bf16[8,64,128]{2,1,0:T(8,128)(2,1)} %fusion), calls=%async_computation.1 | async-start | bytes 262144 | tf_op jit(solution)/shard_map/all_to_all | solution.py:355
  120.5 78.6 %all-gather.5.cloned.1.call-start = ((), (), s32[]{:S(2)}) async-start(), calls=%async_computation.3 | async-start | bytes 4595712 | tf_op jit(solution)/shard_map/all_gather | solution.py:368
  125.1 2.5 %copy-start.1 = (bf16[8,64,128]{2,1,0:T(8,128)(2,1)}, bf16[8,64,128]{2,1,0:T(8,128)(2,1)S(1)}, u32[]{:S(2)}) copy-start(bf16[8,64,128]{2,1,0:T(8,128)(2,1)S(1)} %all-to-all-done.1) | copy-start | bytes 393220
Sparse Core Ops, SparseCore 0:
  12.9 78.8 all-gather.2
  126.2 72.7 all-gather.4

commit v11 on v10

--- a/solution.py
+++ b/solution.py
@@ -246,15 +246,20 @@
     pair = jnp.arange(HD, dtype=jnp.int32)[None, :] // 2
     grid_row = (cell_ids // GRID_W).astype(jnp.float32)[:, None]
     grid_col = (cell_ids % GRID_W).astype(jnp.float32)[:, None]
-    position = jnp.where(
-        pair < part_time,
-        frame_pos.astype(jnp.float32)[:, None],
-        jnp.where(pair < part_time + part_side, grid_row, grid_col),
-    )
-    angles = position * freq[None, :]
+    cell_angles = jnp.where(pair < part_time + part_side, grid_row, grid_col) * freq[None, :]
+    frame_angles = frame_pos.astype(jnp.float32)[:, None] * freq[None, :]
+    frames = frame_angles.shape[0]
+    cells = cell_angles.shape[0]
+    time_lane = (pair < part_time)[None]
     even = jnp.arange(HD, dtype=jnp.int32)[None, :] % 2 == 0
-    sin_angles = jnp.sin(angles)
-    return (jnp.cos(angles), jnp.where(even, sin_angles, -sin_angles))
+
+    def spread(table_fn):
+        by_frame = table_fn(frame_angles)[:, None, :]
+        by_cell = table_fn(cell_angles)[None, :, :]
+        return jnp.where(time_lane, by_frame, by_cell).reshape(frames * cells, HD)
+
+    sin_wide = spread(jnp.sin)
+    return (spread(jnp.cos), jnp.where(even, sin_wide, -sin_wide))
 
 
 def rotate(vectors, cos_table, sin_table, direction):
@@ -309,7 +314,9 @@
     channels = head_weight.shape[2]
     frame_pos = jnp.arange(tok_local, dtype=jnp.int32) // slab_cells
     cell_ids = jnp.tile(token_cell, tok_local // slab_cells)
-    cos_wide, sin_wide = wide_tables(frame_pos, cell_ids)
+    cos_wide, sin_wide = wide_tables(
+        jnp.arange(tok_local // slab_cells, dtype=jnp.int32), token_cell
+    )
     rot_q, pair = prepare(queries[:, 0, :], keys[:, 0, :], values[:, 0, :], cos_wide, -sin_wide)
     pair_all = lax.all_gather(pair, "seq", axis=0, tiled=True)
     all_weights = lax.all_gather(head_weight[0], "tm", axis=0, tiled=False)

time: 219 us -> 218 us (level)
  no operation moved by 1% of the time
where the time goes in v11:
time: 218 us
  waiting for transfers between devices  132 us (61%)
  Pallas kernels  35.7 us (16%)
  between operations  14.3 us (7%)
  blocking collectives  13.7 us (6%)
  starting transfers between devices  11.8 us (5%)
  other arithmetic  4.39 us (2%)
  local copies, waits for them, and re-layouts  3.93 us (2%)
    all_gather x1, waiting for transfers between devices, on_device(): pair_all = lax.all_gather(pair, 'seq', axis=0, tiled=True)  61.2 us
    all_gather x1, waiting for transfers between devices, on_device(): lax.all_gather(packed, 'seq', axis=0, tiled=True)  60.4 us
    all_gather x1, blocking collectives, on_device(): all_weights = lax.all_gather(head_weight[0], 'tm', axis=0, tiled=False)  13.7 us
    pallas_call x1, Pallas kernels, attention_key_grad(): pl.pallas_call(functools.partial(key_grad_kernel, query_block, block_stri...  13 us
    pallas_call x1, Pallas kernels, attention_query_grad(): pl.pallas_call(functools.partial(query_grad_kernel, key_block), grid=(row...  11 us
    pallas_call x1, Pallas kernels, attention_forward(): pl.pallas_call(functools.partial(forward_kernel, key_block), grid=(rows /...  9.48 us
    all_to_all x1, waiting for transfers between devices, on_device(): lax.all_to_all(projected.reshape(head_count, span_frames * slab_cells, ch...  6.82 us
    all_to_all x1, starting transfers between devices, on_device(): lax.all_to_all(projected.reshape(head_count, span_frames * slab_cells, ch...  5.14 us
  transfers between devices with their start and end apart: 5, of which 4 were waited for; matrix products, arithmetic and copies ran while one was open for 2% of the time, Pallas kernels for 9%

profile of v11, /device:TPU:2, one launch (start us, length us, event | category | flops | bytes accessed | tf_op | source)
XLA Modules:
  0.0 217.9 jit_solution(362192709474370043)
XLA Ops:
  7.2 0.0 copy-start.7
  7.2 0.0 copy-start
  7.2 0.0 all-gather.3.cloned.1.call-start
  7.3 0.1 pad_maximum_fusion.2
  7.4 0.1 broadcast_in_dim.112
  7.4 0.1 mul.150
  7.6 0.7 fusion.25
  8.3 0.1 multiply_sine_fusion
  8.4 0.1 fusion.18
  8.5 0.0 copy-start.6
  8.5 1.0 negate_select_fusion
  9.5 2.2 %shard_map.112 = (bf16[512,128]{1,0:T(8,128)(2,1)}, bf16[512,256]{1,0:T(8,128)(2,1)}) custom-call(bf16[512,128]{1,0:T(8,128)(2,1)} %bitcast.75, bf16[512,128]{1,0:T(8,128)(2,1)} %bitcast.76, bf16[512,128]{1,0:T(8,128)(2,1)} %bitcast.77, f32[512,128]{1,0:T(8,128)} %get-tuple-element.29.cos_ref, f32[512,128]{1,0:T(8,128)} %get-tuple-element.18.sin_ref), custom_call_target="tpu_custom_call" | custom-call | flops 524288 | bytes 917504 | tf_op jit(solution)/shard_map/pallas_call | solution.py:40
  11.7 0.0 all-gather.3.cloned.1.call-update
  11.8 0.0 copy-done.7
  11.8 1.9 collective-permute-start
  13.7 0.0 copy-done
  13.7 0.7 gather_fusion
  14.4 0.7 gather_fusion.1
  15.1 0.7 gather_fusion.2
  15.8 0.1 constant_dynamic-slice_fusion
  15.9 0.0 copy-done.6
  15.9 13.7 %all_gather.10 = bf16[8,128,384]{2,1,0:T(8,128)(2,1)S(1)} all-gather(bf16[1,128,384]{2,1,0:T(8,128)(2,1)S(1)} %copy-done.6), channel_id=1, replica_groups=mesh['seq'=16,'tm'=8,'dp'=2] {'tm'}, dimensions={0}, use_global_device_ids=true | all-gather | bytes 884736 | tf_op jit(solution)/shard_map/all_gather | solution.py:322
  29.6 61.2 %all-gather.3.cloned.1.call-done.kv_ref = bf16[8192,256]{1,0:T(8,128)(2,1)} async-done(((bf16[512,256]{1,0:T(8,128)(2,1)}), bf16[8192,256]{1,0:T(8,128)(2,1)}) %all-gather.3.cloned.1.call-update) | async-done | bytes 4194320 | tf_op jit(solution)/shard_map/all_gather | solution.py:321
  90.8 0.0 copy-start.2
  90.8 9.5 %shard_map.113 = (bf16[512,128]{1,0:T(8,128)(2,1)}, f32[512,1]{1,0:T(8,128)}, bf16[512,384]{1,0:T(8,128)(2,1)}) custom-call(bf16[512,128]{1,0:T(8,128)(2,1)} %get-tuple-element.10.q_ref, bf16[8192,256]{1,0:T(8,128)(2,1)} %all-gather.3.cloned.1.call-done.kv_ref, bf16[128,384]{1,0:T(8,128)(2,1)} %bitcast.79), custom_call_target="tpu_custom_call" | custom-call | flops 2147483648 | bytes 4456448 | tf_op jit(solution)/shard_map/pallas_call | solution.py:88
  100.2 0.0 copy-start.8
  100.2 5.1 %all-to-all-start = ((bf16[8,64,384]{2,1,0:T(8,128)(2,1)}), bf16[8,64,384]{2,1,0:T(8,128)(2,1)S(1)}, u32[]{:S(2)}, u32[]{:S(2)}) async-start(bf16[8,64,384]{2,1,0:T(8,128)(2,1)} %bitcast.73), calls=%async_computation | async-start | bytes 786432 | tf_op jit(solution)/shard_map/all_to_all | solution.py:329
  105.4 0.0 copy-done.2
  105.4 0.3 convolution_multiply_fusion.2
  105.7 0.0 collective-permute-done
  105.7 0.3 convolution_multiply_fusion.1
  106.0 6.8 %all-to-all-done = bf16[8,64,384]{2,1,0:T(8,128)(2,1)S(1)} async-done(((bf16[8,64,384]{2,1,0:T(8,128)(2,1)}), bf16[8,64,384]{2,1,0:T(8,128)(2,1)S(1)}, u32[]{:S(2)}, u32[]{:S(2)}) %all-to-all-start) | async-done | bytes 393248 | tf_op jit(solution)/shard_map/all_to_all | solution.py:329
  112.8 0.1 convert_reduce_fusion
  112.9 0.0 copy-start.4
  112.9 0.1 multiply_reduce_fusion.2
  113.0 0.1 rsqrt.15
  113.1 0.0 copy-done.8
  113.1 0.0 copy-start.5
  113.1 0.4 multiply_reduce_fusion.1
  113.5 0.0 copy-start.3
  113.6 0.1 subtract_convert_fusion
  113.7 1.0 fusion
  114.7 4.7 %all-to-all-start.1 = ((bf16[8,64,128]{2,1,0:T(8,128)(2,1)}), bf16[8,64,128]{2,1,0:T(8,128)(2,1)S(1)}, u32[]{:S(2)}, u32[]{:S(2)}) async-start(bf16[8,64,128]{2,1,0:T(8,128)(2,1)} %fusion), calls=%async_computation.1 | async-start | bytes 262144 | tf_op jit(solution)/shard_map/all_to_all | solution.py:362
  119.4 0.0 all-gather.5.cloned.1.call-start
  119.4 1.1 reduce.1
  120.5 3.6 %all-to-all-done.1 = bf16[8,64,128]{2,1,0:T(8,128)(2,1)S(1)} async-done(((bf16[8,64,128]{2,1,0:T(8,128)(2,1)}), bf16[8,64,128]{2,1,0:T(8,128)(2,1)S(1)}, u32[]{:S(2)}, u32[]{:S(2)}) %all-to-all-start.1) | async-done | bytes 131104 | tf_op jit(solution)/shard_map/all_to_all | solution.py:362
  124.1 0.0 copy-start.1
  124.1 0.0 copy-done.4
  124.1 0.2 multiply_reduce_fusion
  124.3 0.0 copy-done.5
  124.3 0.7 fusion.13
  125.1 0.0 all-gather.5.cloned.1.call-update
  125.1 0.0 copy-done.3
  125.1 0.7 slice.31.k_ref
  125.8 0.9 copy.13.delta_ref
  126.6 0.0 copy-done.1
  126.6 11.0 %shard_map.114 = bf16[512,128]{1,0:T(8,128)(2,1)} custom-call(bf16[512,128]{1,0:T(8,128)(2,1)} %get-tuple-element.10.q_ref, bf16[512,128]{1,0:T(8,128)(2,1)} %bitcast.71, f32[512,1]{1,0:T(8,128)} %get-tuple-element.13.lse_ref, f32[512,1]{1,0:T(8,128)} %copy.13.delta_ref, bf16[8192,256]{1,0:T(8,128)(2,1)} %all-gather.3.cloned.1.call-done.kv_ref, ...), custom_call_target="tpu_custom_call" | custom-call | flops 3221225472 | bytes 4587520 | tf_op jit(solution)/shard_map/pallas_call | solution.py:141
  137.6 60.4 %all-gather.5.cloned.1.call-done.qg_ref = bf16[8448,256]{1,0:T(8,128)(2,1)} async-done(((bf16[528,256]{1,0:T(8,128)(2,1)}), bf16[8448,256]{1,0:T(8,128)(2,1)}) %all-gather.5.cloned.1.call-update) | async-done | bytes 4325392 | tf_op jit(solution)/shard_map/all_gather | solution.py:375
  198.0 13.0 %shard_map.115 = (bf16[512,128]{1,0:T(8,128)(2,1)}, bf16[512,128]{1,0:T(8,128)(2,1)}) custom-call(bf16[512,128]{1,0:T(8,128)(2,1)} %slice.31.k_ref, bf16[512,128]{1,0:T(8,128)(2,1)} %bitcast.78, bf16[8448,256]{1,0:T(8,128)(2,1)} %all-gather.5.cloned.1.call-done.qg_ref, f32[512,128]{1,0:T(8,128)} %get-tuple-element.29.cos_ref, ...), custom_call_target="tpu_custom_call" | custom-call | flops 4294967296 | bytes 4456448 | tf_op jit(solution)/shard_map/pallas_call | solution.py:198
  (20 shorter events, 0.2 us)
Async XLA Ops:
  7.2 4.6 %copy-start.7 = (bf16[2,32,768]{2,1,0:T(8,128)(2,1)S(1)}, bf16[2,32,768]{2,1,0:T(8,128)(2,1)}, u32[]{:S(2)}) copy-start(bf16[2,32,768]{2,1,0:T(8,128)(2,1)} %param.17) | copy-start | bytes 294916
  7.2 6.6 %copy-start = (s32[16]{0:T(128)S(1)}, s32[16]{0:T(128)}, u32[]{:S(2)}) copy-start(s32[16]{0:T(128)} %param.16) | copy-start | bytes 196
  7.2 83.6 %all-gather.3.cloned.1.call-start = ((), (), s32[]{:S(2)}) async-start(), calls=%async_computation.2 | async-start | bytes 4456448 | tf_op jit(solution)/shard_map/all_gather | solution.py:321
  8.5 7.4 %copy-start.6 = (bf16[1,128,384]{2,1,0:T(8,128)(2,1)S(1)}, bf16[1,128,384]{2,1,0:T(8,128)(2,1)}, u32[]{:S(2)}) copy-start(bf16[1,128,384]{2,1,0:T(8,128)(2,1)} %param.13) | copy-start | bytes 294916
  11.8 93.9 %collective-permute-start = (bf16[2,32,768]{2,1,0:T(8,128)(2,1)S(1)}, bf16[2,32,768]{2,1,0:T(8,128)(2,1)S(1)}, u32[]{:S(2)}, u32[]{:S(2)}) collective-permute-start(bf16[2,32,768]{2,1,0:T(8,128)(2,1)S(1)} %copy-done.7), channel_id=1, source_target_pairs={{2,0},{4,2},{6,4},{8,6},{10,8},{12,10},{14,12},{3,1},{5,3},{7,5},{... | collective-permute-start | bytes 294920 | tf_op jit(solution)/shard_map/ppermute | solution.py:212
  90.8 14.6 %copy-start.2 = (bf16[3,384,768]{2,1,0:T(8,128)(2,1)S(1)}, bf16[3,384,768]{2,1,0:T(8,128)(2,1)}, u32[]{:S(2)}) copy-start(bf16[3,384,768]{2,1,0:T(8,128)(2,1)} %param.15) | copy-start | bytes 5308420
  100.2 12.9 %copy-start.8 = (f32[384]{0:T(512)S(1)}, f32[384]{0:T(512)}, u32[]{:S(2)}) copy-start(f32[384]{0:T(512)} %param.14) | copy-start | bytes 4612
  100.2 12.6 %all-to-all-start = ((bf16[8,64,384]{2,1,0:T(8,128)(2,1)}), bf16[8,64,384]{2,1,0:T(8,128)(2,1)S(1)}, u32[]{:S(2)}, u32[]{:S(2)}) async-start(bf16[8,64,384]{2,1,0:T(8,128)(2,1)} %bitcast.73), calls=%async_computation | async-start | bytes 786432 | tf_op jit(solution)/shard_map/all_to_all | solution.py:329
  112.9 11.2 %copy-start.4 = (bf16[512,128]{1,0:T(8,128)(2,1)S(1)}, bf16[512,128]{1,0:T(8,128)(2,1)}, u32[]{:S(2)}) copy-start(bf16[512,128]{1,0:T(8,128)(2,1)} %get-tuple-element.14) | copy-start | bytes 393220
  113.1 11.2 %copy-start.5 = (bf16[512,128]{1,0:T(8,128)(2,1)S(1)}, bf16[512,128]{1,0:T(8,128)(2,1)}, u32[]{:S(2)}) copy-start(bf16[512,128]{1,0:T(8,128)(2,1)} %get-tuple-element.10.q_ref) | copy-start | bytes 393220
  113.5 11.6 %copy-start.3 = (bf16[512,256]{1,0:T(8,128)(2,1)S(1)}, bf16[512,256]{1,0:T(8,128)(2,1)}, u32[]{:S(2)}) copy-start(bf16[512,256]{1,0:T(8,128)(2,1)} %get-tuple-element.11) | copy-start | bytes 786436
  114.7 9.4 %all-to-all-start.1 = ((bf16[8,64,128]{2,1,0:T(8,128)(2,1)}), bf16[8,64,128]{2,1,0:T(8,128)(2,1)S(1)}, u32[]{:S(2)}, u32[]{:S(2)}) async-start(bf16[8,64,128]{2,1,0:T(8,128)(2,1)} %fusion), calls=%async_computation.1 | async-start | bytes 262144 | tf_op jit(solution)/shard_map/all_to_all | solution.py:362
  119.4 78.6 %all-gather.5.cloned.1.call-start = ((), (), s32[]{:S(2)}) async-start(), calls=%async_computation.3 | async-start | bytes 4595712 | tf_op jit(solution)/shard_map/all_gather | solution.py:375
  124.1 2.5 %copy-start.1 = (bf16[8,64,128]{2,1,0:T(8,128)(2,1)}, bf16[8,64,128]{2,1,0:T(8,128)(2,1)S(1)}, u32[]{:S(2)}) copy-start(bf16[8,64,128]{2,1,0:T(8,128)(2,1)S(1)} %all-to-all-done.1) | copy-start | bytes 393220
Sparse Core Ops, SparseCore 0:
  11.9 78.8 all-gather.2
  125.2 72.7 all-gather.4

commit v12 on v11

--- a/solution.py
+++ b/solution.py
@@ -25,10 +25,13 @@
     return x * cos_ref[...] + partner * sin_ref[...]
 
 
-def prepare_kernel(q_ref, k_ref, v_ref, cos_ref, sin_ref, rq_ref, kv_ref):
+def rotate_kernel(q_ref, cos_ref, sin_ref, rq_ref):
     rq_ref[...] = rotate_back_rows(q_ref[...].astype(jnp.float32), cos_ref, sin_ref).astype(
         rq_ref.dtype
     )
+
+
+def pair_kernel(k_ref, v_ref, cos_ref, sin_ref, kv_ref):
     kv_ref[:, :HD] = rotate_back_rows(k_ref[...].astype(jnp.float32), cos_ref, sin_ref).astype(
         kv_ref.dtype
     )
@@ -37,14 +40,17 @@
 
 def prepare(q, k, v, cos_wide, sin_forward):
     rows = q.shape[0]
-    return pl.pallas_call(
-        prepare_kernel,
-        out_shape=[
-            jax.ShapeDtypeStruct((rows, HD), jnp.bfloat16),
-            jax.ShapeDtypeStruct((rows, 2 * HD), jnp.bfloat16),
-        ],
-        cost_estimate=pl.CostEstimate(flops=8 * rows * HD, transcendentals=0, bytes_accessed=14 * rows * HD),
-    )(q, k, v, cos_wide, sin_forward)
+    pair = pl.pallas_call(
+        pair_kernel,
+        out_shape=jax.ShapeDtypeStruct((rows, 2 * HD), jnp.bfloat16),
+        cost_estimate=pl.CostEstimate(flops=4 * rows * HD, transcendentals=0, bytes_accessed=16 * rows * HD),
+    )(k, v, cos_wide, sin_forward)
+    rot_q = pl.pallas_call(
+        rotate_kernel,
+        out_shape=jax.ShapeDtypeStruct((rows, HD), jnp.bfloat16),
+        cost_estimate=pl.CostEstimate(flops=4 * rows * HD, transcendentals=0, bytes_accessed=12 * rows * HD),
+    )(q, cos_wide, sin_forward)
+    return rot_q, pair
 
 
 def forward_kernel(key_block, q_ref, kv_ref, w_ref, out_ref, lse_ref, proj_ref):
@@ -181,7 +187,7 @@
         return dk, dv
 
     zero = jnp.zeros(dk_ref.shape, jnp.float32)
-    dk, dv = lax.fori_loop(0, steps, body, (zero, zero), unroll=4)
+    dk, dv = lax.fori_loop(0, steps, body, (zero, zero), unroll=8)
     dk_ref[...] = rotate_back_rows(dk * SCALE, cos_ref, sin_ref).astype(dk_ref.dtype)
     dv_ref[...] = dv.astype(dv_ref.dtype)
 

time: 218 us -> 218 us (level)
  transfers between devices with their start and end apart: 5 -> 5, of which waited for: 4 -> 4; matrix products, arithmetic and copies ran while one was open for 2% -> 3% of each run, Pallas kernels for 9% -> 10%
where the time goes in v12:
time: 218 us
  waiting for transfers between devices  130 us (60%)
  Pallas kernels  37 us (17%)
  between operations  14.3 us (7%)
  blocking collectives  13.7 us (6%)
  starting transfers between devices  11.4 us (5%)
  other arithmetic  4.4 us (2%)
  local copies, waits for them, and re-layouts  3.92 us (2%)
  matrix products  3.61 us (2%)
    all_gather x1, waiting for transfers between devices, on_device(): lax.all_gather(packed, 'seq', axis=0, tiled=True)  60.5 us
    all_gather x1, waiting for transfers between devices, on_device(): pair_all = lax.all_gather(pair, 'seq', axis=0, tiled=True)  59.5 us
    all_gather x1, blocking collectives, on_device(): all_weights = lax.all_gather(head_weight[0], 'tm', axis=0, tiled=False)  13.7 us
    pallas_call x1, Pallas kernels, attention_key_grad(): pl.pallas_call(functools.partial(key_grad_kernel, query_block, block_stri...  12.6 us
    pallas_call x1, Pallas kernels, attention_query_grad(): pl.pallas_call(functools.partial(query_grad_kernel, key_block), grid=(row...  10.9 us
    pallas_call x1, Pallas kernels, attention_forward(): pl.pallas_call(functools.partial(forward_kernel, key_block), grid=(rows /...  9.47 us
    all_to_all x1, waiting for transfers between devices, on_device(): lax.all_to_all(projected.reshape(head_count, span_frames * slab_cells, ch...  6.18 us
    all_to_all x1, starting transfers between devices, on_device(): lax.all_to_all(grad_heads, 'tm', 0, 0, tiled=False).reshape(tok_local, HD)  4.75 us
  transfers between devices with their start and end apart: 5, of which 4 were waited for; matrix products, arithmetic and copies ran while one was open for 3% of the time, Pallas kernels for 10%

profile of v12, /device:TPU:2, one launch (start us, length us, event | category | flops | bytes accessed | tf_op | source)
XLA Modules:
  0.0 218.0 jit_solution(9334384249393947420)
XLA Ops:
  7.2 0.0 copy-start.7
  7.2 0.0 copy-start
  7.2 0.0 all-gather.3.cloned.1.call-start
  7.3 0.1 pad_maximum_fusion.2
  7.4 0.1 broadcast_in_dim.112
  7.4 0.1 mul.150
  7.6 0.7 fusion.25
  8.3 0.1 multiply_sine_fusion
  8.4 0.1 fusion.18
  8.5 1.0 negate_select_fusion
  9.5 0.0 copy-start.6
  9.5 2.1 shard_map.113
  11.6 0.0 all-gather.3.cloned.1.call-update
  11.6 0.0 copy-done.7
  11.6 1.9 collective-permute-start
  13.6 1.9 shard_map.112.q_ref
  15.5 0.0 copy-done
  15.5 0.7 gather_fusion
  16.2 0.7 gather_fusion.1
  16.9 0.7 gather_fusion.2
  17.6 0.1 constant_dynamic-slice_fusion
  17.7 0.0 copy-done.6
  17.7 13.7 %all_gather.10 = bf16[8,128,384]{2,1,0:T(8,128)(2,1)S(1)} all-gather(bf16[1,128,384]{2,1,0:T(8,128)(2,1)S(1)} %copy-done.6), channel_id=1, replica_groups=mesh['seq'=16,'tm'=8,'dp'=2] {'tm'}, dimensions={0}, use_global_device_ids=true | all-gather | bytes 884736 | tf_op jit(solution)/shard_map/all_gather | solution.py:328
  31.3 59.5 %all-gather.3.cloned.1.call-done.kv_ref = bf16[8192,256]{1,0:T(8,128)(2,1)} async-done(((bf16[512,256]{1,0:T(8,128)(2,1)}), bf16[8192,256]{1,0:T(8,128)(2,1)}) %all-gather.3.cloned.1.call-update) | async-done | bytes 4194320 | tf_op jit(solution)/shard_map/all_gather | solution.py:327
  90.8 0.0 copy-start.3
  90.8 9.5 %shard_map.114 = (bf16[512,128]{1,0:T(8,128)(2,1)}, f32[512,1]{1,0:T(8,128)}, bf16[512,384]{1,0:T(8,128)(2,1)}) custom-call(bf16[512,128]{1,0:T(8,128)(2,1)} %shard_map.112.q_ref, bf16[8192,256]{1,0:T(8,128)(2,1)} %all-gather.3.cloned.1.call-done.kv_ref, bf16[128,384]{1,0:T(8,128)(2,1)} %bitcast.79), custom_call_target="tpu_custom_call" | custom-call | flops 2147483648 | bytes 4456448 | tf_op jit(solution)/shard_map/pallas_call | solution.py:94
  100.3 0.0 copy-start.8
  100.3 4.7 %all-to-all-start = ((bf16[8,64,384]{2,1,0:T(8,128)(2,1)}), bf16[8,64,384]{2,1,0:T(8,128)(2,1)S(1)}, u32[]{:S(2)}, u32[]{:S(2)}) async-start(bf16[8,64,384]{2,1,0:T(8,128)(2,1)} %bitcast.73), calls=%async_computation | async-start | bytes 786432 | tf_op jit(solution)/shard_map/all_to_all | solution.py:335
  105.0 0.0 copy-done.3
  105.0 0.3 convolution_multiply_fusion.2
  105.3 0.0 collective-permute-done
  105.3 1.0 convolution_multiply_fusion.1
  106.3 6.2 %all-to-all-done = bf16[8,64,384]{2,1,0:T(8,128)(2,1)S(1)} async-done(((bf16[8,64,384]{2,1,0:T(8,128)(2,1)}), bf16[8,64,384]{2,1,0:T(8,128)(2,1)S(1)}, u32[]{:S(2)}, u32[]{:S(2)}) %all-to-all-start) | async-done | bytes 393248 | tf_op jit(solution)/shard_map/all_to_all | solution.py:335
  112.4 0.1 convert_reduce_fusion
  112.5 0.0 copy-start.5
  112.5 0.1 multiply_reduce_fusion.2
  112.6 0.1 rsqrt.15
  112.7 0.0 copy-done.8
  112.7 0.0 copy-start.4
  112.7 1.3 multiply_reduce_fusion.1
  114.1 0.0 copy-start.1
  114.1 0.1 subtract_convert_fusion
  114.2 1.0 fusion
  115.2 4.7 %all-to-all-start.1 = ((bf16[8,64,128]{2,1,0:T(8,128)(2,1)}), bf16[8,64,128]{2,1,0:T(8,128)(2,1)S(1)}, u32[]{:S(2)}, u32[]{:S(2)}) async-start(bf16[8,64,128]{2,1,0:T(8,128)(2,1)} %fusion), calls=%async_computation.1 | async-start | bytes 262144 | tf_op jit(solution)/shard_map/all_to_all | solution.py:368
  120.0 0.0 all-gather.5.cloned.1.call-start
  120.0 1.1 reduce.1
  121.0 3.6 %all-to-all-done.1 = bf16[8,64,128]{2,1,0:T(8,128)(2,1)S(1)} async-done(((bf16[8,64,128]{2,1,0:T(8,128)(2,1)}), bf16[8,64,128]{2,1,0:T(8,128)(2,1)S(1)}, u32[]{:S(2)}, u32[]{:S(2)}) %all-to-all-start.1) | async-done | bytes 131104 | tf_op jit(solution)/shard_map/all_to_all | solution.py:368
  124.6 0.0 copy-start.2
  124.6 0.0 copy-done.5
  124.6 0.2 multiply_reduce_fusion
  124.9 0.0 copy-done.4
  124.9 0.8 fusion.13
  125.6 0.0 all-gather.5.cloned.1.call-update
  125.6 0.0 copy-done.1
  125.7 0.7 slice.38.k_ref
  126.3 0.9 copy.13.delta_ref
  127.2 0.0 copy-done.2
  127.2 10.9 %shard_map.115 = bf16[512,128]{1,0:T(8,128)(2,1)} custom-call(bf16[512,128]{1,0:T(8,128)(2,1)} %shard_map.112.q_ref, bf16[512,128]{1,0:T(8,128)(2,1)} %bitcast.71, f32[512,1]{1,0:T(8,128)} %get-tuple-element.9.lse_ref, f32[512,1]{1,0:T(8,128)} %copy.13.delta_ref, bf16[8192,256]{1,0:T(8,128)(2,1)} %all-gather.3.cloned.1.call-done.kv_ref, ...), custom_call_target="tpu_custom_call" | custom-call | flops 3221225472 | bytes 4587520 | tf_op jit(solution)/shard_map/pallas_call | solution.py:147
  138.1 60.5 %all-gather.5.cloned.1.call-done.qg_ref = bf16[8448,256]{1,0:T(8,128)(2,1)} async-done(((bf16[528,256]{1,0:T(8,128)(2,1)}), bf16[8448,256]{1,0:T(8,128)(2,1)}) %all-gather.5.cloned.1.call-update) | async-done | bytes 4325392 | tf_op jit(solution)/shard_map/all_gather | solution.py:381
  198.6 12.6 %shard_map.116 = (bf16[512,128]{1,0:T(8,128)(2,1)}, bf16[512,128]{1,0:T(8,128)(2,1)}) custom-call(bf16[512,128]{1,0:T(8,128)(2,1)} %slice.38.k_ref, bf16[512,128]{1,0:T(8,128)(2,1)} %bitcast.78, bf16[8448,256]{1,0:T(8,128)(2,1)} %all-gather.5.cloned.1.call-done.qg_ref, f32[512,128]{1,0:T(8,128)} %get-tuple-element.25.cos_ref, ...), custom_call_target="tpu_custom_call" | custom-call | flops 4294967296 | bytes 4456448 | tf_op jit(solution)/shard_map/pallas_call | solution.py:204
  (20 shorter events, 0.2 us)
Async XLA Ops:
  7.2 4.5 %copy-start.7 = (bf16[2,32,768]{2,1,0:T(8,128)(2,1)S(1)}, bf16[2,32,768]{2,1,0:T(8,128)(2,1)}, u32[]{:S(2)}) copy-start(bf16[2,32,768]{2,1,0:T(8,128)(2,1)} %param.17) | copy-start | bytes 294916
  7.2 8.3 %copy-start = (s32[16]{0:T(128)S(1)}, s32[16]{0:T(128)}, u32[]{:S(2)}) copy-start(s32[16]{0:T(128)} %param.16) | copy-start | bytes 196
  7.2 83.6 %all-gather.3.cloned.1.call-start = ((), (), s32[]{:S(2)}) async-start(), calls=%async_computation.2 | async-start | bytes 4456448 | tf_op jit(solution)/shard_map/all_gather | solution.py:327
  9.5 8.1 %copy-start.6 = (bf16[1,128,384]{2,1,0:T(8,128)(2,1)S(1)}, bf16[1,128,384]{2,1,0:T(8,128)(2,1)}, u32[]{:S(2)}) copy-start(bf16[1,128,384]{2,1,0:T(8,128)(2,1)} %param.13) | copy-start | bytes 294916
  11.6 93.7 %collective-permute-start = (bf16[2,32,768]{2,1,0:T(8,128)(2,1)S(1)}, bf16[2,32,768]{2,1,0:T(8,128)(2,1)S(1)}, u32[]{:S(2)}, u32[]{:S(2)}) collective-permute-start(bf16[2,32,768]{2,1,0:T(8,128)(2,1)S(1)} %copy-done.7), channel_id=1, source_target_pairs={{2,0},{4,2},{6,4},{8,6},{10,8},{12,10},{14,12},{3,1},{5,3},{7,5},{... | collective-permute-start | bytes 294920 | tf_op jit(solution)/shard_map/ppermute | solution.py:218
  90.8 14.2 %copy-start.3 = (bf16[3,384,768]{2,1,0:T(8,128)(2,1)S(1)}, bf16[3,384,768]{2,1,0:T(8,128)(2,1)}, u32[]{:S(2)}) copy-start(bf16[3,384,768]{2,1,0:T(8,128)(2,1)} %param.15) | copy-start | bytes 5308420
  100.3 12.4 %copy-start.8 = (f32[384]{0:T(512)S(1)}, f32[384]{0:T(512)}, u32[]{:S(2)}) copy-start(f32[384]{0:T(512)} %param.14) | copy-start | bytes 4612
  100.3 12.1 %all-to-all-start = ((bf16[8,64,384]{2,1,0:T(8,128)(2,1)}), bf16[8,64,384]{2,1,0:T(8,128)(2,1)S(1)}, u32[]{:S(2)}, u32[]{:S(2)}) async-start(bf16[8,64,384]{2,1,0:T(8,128)(2,1)} %bitcast.73), calls=%async_computation | async-start | bytes 786432 | tf_op jit(solution)/shard_map/all_to_all | solution.py:335
  112.5 12.1 %copy-start.5 = (bf16[512,128]{1,0:T(8,128)(2,1)S(1)}, bf16[512,128]{1,0:T(8,128)(2,1)}, u32[]{:S(2)}) copy-start(bf16[512,128]{1,0:T(8,128)(2,1)} %get-tuple-element.10) | copy-start | bytes 393220
  112.7 12.1 %copy-start.4 = (bf16[512,128]{1,0:T(8,128)(2,1)S(1)}, bf16[512,128]{1,0:T(8,128)(2,1)}, u32[]{:S(2)}) copy-start(bf16[512,128]{1,0:T(8,128)(2,1)} %shard_map.112.q_ref) | copy-start | bytes 393220
  114.1 11.6 %copy-start.1 = (bf16[512,256]{1,0:T(8,128)(2,1)S(1)}, bf16[512,256]{1,0:T(8,128)(2,1)}, u32[]{:S(2)}) copy-start(bf16[512,256]{1,0:T(8,128)(2,1)} %shard_map.113) | copy-start | bytes 786436
  115.2 9.4 %all-to-all-start.1 = ((bf16[8,64,128]{2,1,0:T(8,128)(2,1)}), bf16[8,64,128]{2,1,0:T(8,128)(2,1)S(1)}, u32[]{:S(2)}, u32[]{:S(2)}) async-start(bf16[8,64,128]{2,1,0:T(8,128)(2,1)} %fusion), calls=%async_computation.1 | async-start | bytes 262144 | tf_op jit(solution)/shard_map/all_to_all | solution.py:368
  120.0 78.6 %all-gather.5.cloned.1.call-start = ((), (), s32[]{:S(2)}) async-start(), calls=%async_computation.3 | async-start | bytes 4595712 | tf_op jit(solution)/shard_map/all_gather | solution.py:381
  124.6 2.5 %copy-start.2 = (bf16[8,64,128]{2,1,0:T(8,128)(2,1)}, bf16[8,64,128]{2,1,0:T(8,128)(2,1)S(1)}, u32[]{:S(2)}) copy-start(bf16[8,64,128]{2,1,0:T(8,128)(2,1)S(1)} %all-to-all-done.1) | copy-start | bytes 393220
Sparse Core Ops, SparseCore 0:
  11.8 79.0 all-gather.2
  125.8 72.7 all-gather.4

commit v13 on v12

--- a/solution.py
+++ b/solution.py
@@ -187,7 +187,7 @@
         return dk, dv
 
     zero = jnp.zeros(dk_ref.shape, jnp.float32)
-    dk, dv = lax.fori_loop(0, steps, body, (zero, zero), unroll=8)
+    dk, dv = lax.fori_loop(0, steps, body, (zero, zero), unroll=True)
     dk_ref[...] = rotate_back_rows(dk * SCALE, cos_ref, sin_ref).astype(dk_ref.dtype)
     dv_ref[...] = dv.astype(dv_ref.dtype)
 

time: 218 us -> 218 us (level)
  no operation moved by 1% of the time
where the time goes in v13:
time: 218 us
  waiting for transfers between devices  130 us (60%)
  Pallas kernels  36.5 us (17%)
  between operations  14.3 us (7%)
  blocking collectives  13.7 us (6%)
  starting transfers between devices  11.4 us (5%)
  other arithmetic  4.4 us (2%)
  local copies, waits for them, and re-layouts  3.92 us (2%)
  matrix products  3.61 us (2%)
    all_gather x1, waiting for transfers between devices, on_device(): lax.all_gather(packed, 'seq', axis=0, tiled=True)  60.5 us
    all_gather x1, waiting for transfers between devices, on_device(): pair_all = lax.all_gather(pair, 'seq', axis=0, tiled=True)  59.5 us
    all_gather x1, blocking collectives, on_device(): all_weights = lax.all_gather(head_weight[0], 'tm', axis=0, tiled=False)  13.7 us
    pallas_call x1, Pallas kernels, attention_key_grad(): pl.pallas_call(functools.partial(key_grad_kernel, query_block, block_stri...  12.1 us
    pallas_call x1, Pallas kernels, attention_query_grad(): pl.pallas_call(functools.partial(query_grad_kernel, key_block), grid=(row...  10.9 us
    pallas_call x1, Pallas kernels, attention_forward(): pl.pallas_call(functools.partial(forward_kernel, key_block), grid=(rows /...  9.47 us
    all_to_all x1, waiting for transfers between devices, on_device(): lax.all_to_all(projected.reshape(head_count, span_frames * slab_cells, ch...  6.18 us
    all_to_all x1, starting transfers between devices, on_device(): lax.all_to_all(grad_heads, 'tm', 0, 0, tiled=False).reshape(tok_local, HD)  4.75 us
  transfers between devices with their start and end apart: 5, of which 4 were waited for; matrix products, arithmetic and copies ran while one was open for 3% of the time, Pallas kernels for 10%

profile of v13, /device:TPU:2, one launch (start us, length us, event | category | flops | bytes accessed | tf_op | source)
XLA Modules:
  0.0 217.5 jit_solution(9459951700279984981)
XLA Ops:
  7.2 0.0 copy-start.7
  7.2 0.0 copy-start
  7.2 0.0 all-gather.3.cloned.1.call-start
  7.3 0.1 pad_maximum_fusion.2
  7.4 0.1 broadcast_in_dim.112
  7.4 0.1 mul.150
  7.6 0.7 fusion.25
  8.3 0.1 multiply_sine_fusion
  8.4 0.1 fusion.18
  8.5 1.0 negate_select_fusion
  9.5 0.0 copy-start.6
  9.5 2.1 shard_map.113
  11.6 0.0 all-gather.3.cloned.1.call-update
  11.6 0.0 copy-done.7
  11.6 1.9 collective-permute-start
  13.6 1.9 shard_map.112.q_ref
  15.5 0.0 copy-done
  15.5 0.7 gather_fusion
  16.2 0.7 gather_fusion.1
  16.9 0.7 gather_fusion.2
  17.6 0.1 constant_dynamic-slice_fusion
  17.7 0.0 copy-done.6
  17.7 13.7 %all_gather.10 = bf16[8,128,384]{2,1,0:T(8,128)(2,1)S(1)} all-gather(bf16[1,128,384]{2,1,0:T(8,128)(2,1)S(1)} %copy-done.6), channel_id=1, replica_groups=mesh['seq'=16,'tm'=8,'dp'=2] {'tm'}, dimensions={0}, use_global_device_ids=true | all-gather | bytes 884736 | tf_op jit(solution)/shard_map/all_gather | solution.py:328
  31.3 59.5 %all-gather.3.cloned.1.call-done.kv_ref = bf16[8192,256]{1,0:T(8,128)(2,1)} async-done(((bf16[512,256]{1,0:T(8,128)(2,1)}), bf16[8192,256]{1,0:T(8,128)(2,1)}) %all-gather.3.cloned.1.call-update) | async-done | bytes 4194320 | tf_op jit(solution)/shard_map/all_gather | solution.py:327
  90.8 0.0 copy-start.3
  90.8 9.5 %shard_map.114 = (bf16[512,128]{1,0:T(8,128)(2,1)}, f32[512,1]{1,0:T(8,128)}, bf16[512,384]{1,0:T(8,128)(2,1)}) custom-call(bf16[512,128]{1,0:T(8,128)(2,1)} %shard_map.112.q_ref, bf16[8192,256]{1,0:T(8,128)(2,1)} %all-gather.3.cloned.1.call-done.kv_ref, bf16[128,384]{1,0:T(8,128)(2,1)} %bitcast.79), custom_call_target="tpu_custom_call" | custom-call | flops 2147483648 | bytes 4456448 | tf_op jit(solution)/shard_map/pallas_call | solution.py:94
  100.3 0.0 copy-start.8
  100.3 4.7 %all-to-all-start = ((bf16[8,64,384]{2,1,0:T(8,128)(2,1)}), bf16[8,64,384]{2,1,0:T(8,128)(2,1)S(1)}, u32[]{:S(2)}, u32[]{:S(2)}) async-start(bf16[8,64,384]{2,1,0:T(8,128)(2,1)} %bitcast.73), calls=%async_computation | async-start | bytes 786432 | tf_op jit(solution)/shard_map/all_to_all | solution.py:335
  105.0 0.0 copy-done.3
  105.0 0.3 convolution_multiply_fusion.2
  105.3 0.0 collective-permute-done
  105.3 1.0 convolution_multiply_fusion.1
  106.3 6.2 %all-to-all-done = bf16[8,64,384]{2,1,0:T(8,128)(2,1)S(1)} async-done(((bf16[8,64,384]{2,1,0:T(8,128)(2,1)}), bf16[8,64,384]{2,1,0:T(8,128)(2,1)S(1)}, u32[]{:S(2)}, u32[]{:S(2)}) %all-to-all-start) | async-done | bytes 393248 | tf_op jit(solution)/shard_map/all_to_all | solution.py:335
  112.4 0.1 convert_reduce_fusion
  112.5 0.0 copy-start.5
  112.5 0.1 multiply_reduce_fusion.2
  112.6 0.1 rsqrt.15
  112.7 0.0 copy-done.8
  112.7 0.0 copy-start.4
  112.7 1.3 multiply_reduce_fusion.1
  114.1 0.0 copy-start.1
  114.1 0.1 subtract_convert_fusion
  114.2 1.0 fusion
  115.2 4.7 %all-to-all-start.1 = ((bf16[8,64,128]{2,1,0:T(8,128)(2,1)}), bf16[8,64,128]{2,1,0:T(8,128)(2,1)S(1)}, u32[]{:S(2)}, u32[]{:S(2)}) async-start(bf16[8,64,128]{2,1,0:T(8,128)(2,1)} %fusion), calls=%async_computation.1 | async-start | bytes 262144 | tf_op jit(solution)/shard_map/all_to_all | solution.py:368
  120.0 0.0 all-gather.5.cloned.1.call-start
  120.0 1.1 reduce.1
  121.0 3.6 %all-to-all-done.1 = bf16[8,64,128]{2,1,0:T(8,128)(2,1)S(1)} async-done(((bf16[8,64,128]{2,1,0:T(8,128)(2,1)}), bf16[8,64,128]{2,1,0:T(8,128)(2,1)S(1)}, u32[]{:S(2)}, u32[]{:S(2)}) %all-to-all-start.1) | async-done | bytes 131104 | tf_op jit(solution)/shard_map/all_to_all | solution.py:368
  124.6 0.0 copy-start.2
  124.6 0.0 copy-done.5
  124.6 0.2 multiply_reduce_fusion
  124.9 0.0 copy-done.4
  124.9 0.8 fusion.13
  125.6 0.0 all-gather.5.cloned.1.call-update
  125.6 0.0 copy-done.1
  125.7 0.7 slice.38.k_ref
  126.3 0.9 copy.13.delta_ref
  127.2 0.0 copy-done.2
  127.2 10.9 %shard_map.115 = bf16[512,128]{1,0:T(8,128)(2,1)} custom-call(bf16[512,128]{1,0:T(8,128)(2,1)} %shard_map.112.q_ref, bf16[512,128]{1,0:T(8,128)(2,1)} %bitcast.71, f32[512,1]{1,0:T(8,128)} %get-tuple-element.9.lse_ref, f32[512,1]{1,0:T(8,128)} %copy.13.delta_ref, bf16[8192,256]{1,0:T(8,128)(2,1)} %all-gather.3.cloned.1.call-done.kv_ref, ...), custom_call_target="tpu_custom_call" | custom-call | flops 3221225472 | bytes 4587520 | tf_op jit(solution)/shard_map/pallas_call | solution.py:147
  138.1 60.5 %all-gather.5.cloned.1.call-done.qg_ref = bf16[8448,256]{1,0:T(8,128)(2,1)} async-done(((bf16[528,256]{1,0:T(8,128)(2,1)}), bf16[8448,256]{1,0:T(8,128)(2,1)}) %all-gather.5.cloned.1.call-update) | async-done | bytes 4325392 | tf_op jit(solution)/shard_map/all_gather | solution.py:381
  198.6 12.1 %shard_map.116 = (bf16[512,128]{1,0:T(8,128)(2,1)}, bf16[512,128]{1,0:T(8,128)(2,1)}) custom-call(bf16[512,128]{1,0:T(8,128)(2,1)} %slice.38.k_ref, bf16[512,128]{1,0:T(8,128)(2,1)} %bitcast.78, bf16[8448,256]{1,0:T(8,128)(2,1)} %all-gather.5.cloned.1.call-done.qg_ref, f32[512,128]{1,0:T(8,128)} %get-tuple-element.25.cos_ref, ...), custom_call_target="tpu_custom_call" | custom-call | flops 4294967296 | bytes 4456448 | tf_op jit(solution)/shard_map/pallas_call | solution.py:204
  (20 shorter events, 0.2 us)
Async XLA Ops:
  7.2 4.5 %copy-start.7 = (bf16[2,32,768]{2,1,0:T(8,128)(2,1)S(1)}, bf16[2,32,768]{2,1,0:T(8,128)(2,1)}, u32[]{:S(2)}) copy-start(bf16[2,32,768]{2,1,0:T(8,128)(2,1)} %param.17) | copy-start | bytes 294916
  7.2 8.3 %copy-start = (s32[16]{0:T(128)S(1)}, s32[16]{0:T(128)}, u32[]{:S(2)}) copy-start(s32[16]{0:T(128)} %param.16) | copy-start | bytes 196
  7.2 83.6 %all-gather.3.cloned.1.call-start = ((), (), s32[]{:S(2)}) async-start(), calls=%async_computation.2 | async-start | bytes 4456448 | tf_op jit(solution)/shard_map/all_gather | solution.py:327
  9.5 8.1 %copy-start.6 = (bf16[1,128,384]{2,1,0:T(8,128)(2,1)S(1)}, bf16[1,128,384]{2,1,0:T(8,128)(2,1)}, u32[]{:S(2)}) copy-start(bf16[1,128,384]{2,1,0:T(8,128)(2,1)} %param.13) | copy-start | bytes 294916
  11.6 93.7 %collective-permute-start = (bf16[2,32,768]{2,1,0:T(8,128)(2,1)S(1)}, bf16[2,32,768]{2,1,0:T(8,128)(2,1)S(1)}, u32[]{:S(2)}, u32[]{:S(2)}) collective-permute-start(bf16[2,32,768]{2,1,0:T(8,128)(2,1)S(1)} %copy-done.7), channel_id=1, source_target_pairs={{2,0},{4,2},{6,4},{8,6},{10,8},{12,10},{14,12},{3,1},{5,3},{7,5},{... | collective-permute-start | bytes 294920 | tf_op jit(solution)/shard_map/ppermute | solution.py:218
  90.8 14.2 %copy-start.3 = (bf16[3,384,768]{2,1,0:T(8,128)(2,1)S(1)}, bf16[3,384,768]{2,1,0:T(8,128)(2,1)}, u32[]{:S(2)}) copy-start(bf16[3,384,768]{2,1,0:T(8,128)(2,1)} %param.15) | copy-start | bytes 5308420
  100.3 12.4 %copy-start.8 = (f32[384]{0:T(512)S(1)}, f32[384]{0:T(512)}, u32[]{:S(2)}) copy-start(f32[384]{0:T(512)} %param.14) | copy-start | bytes 4612
  100.3 12.1 %all-to-all-start = ((bf16[8,64,384]{2,1,0:T(8,128)(2,1)}), bf16[8,64,384]{2,1,0:T(8,128)(2,1)S(1)}, u32[]{:S(2)}, u32[]{:S(2)}) async-start(bf16[8,64,384]{2,1,0:T(8,128)(2,1)} %bitcast.73), calls=%async_computation | async-start | bytes 786432 | tf_op jit(solution)/shard_map/all_to_all | solution.py:335
  112.5 12.1 %copy-start.5 = (bf16[512,128]{1,0:T(8,128)(2,1)S(1)}, bf16[512,128]{1,0:T(8,128)(2,1)}, u32[]{:S(2)}) copy-start(bf16[512,128]{1,0:T(8,128)(2,1)} %get-tuple-element.10) | copy-start | bytes 393220
  112.7 12.1 %copy-start.4 = (bf16[512,128]{1,0:T(8,128)(2,1)S(1)}, bf16[512,128]{1,0:T(8,128)(2,1)}, u32[]{:S(2)}) copy-start(bf16[512,128]{1,0:T(8,128)(2,1)} %shard_map.112.q_ref) | copy-start | bytes 393220
  114.1 11.6 %copy-start.1 = (bf16[512,256]{1,0:T(8,128)(2,1)S(1)}, bf16[512,256]{1,0:T(8,128)(2,1)}, u32[]{:S(2)}) copy-start(bf16[512,256]{1,0:T(8,128)(2,1)} %shard_map.113) | copy-start | bytes 786436
  115.2 9.4 %all-to-all-start.1 = ((bf16[8,64,128]{2,1,0:T(8,128)(2,1)}), bf16[8,64,128]{2,1,0:T(8,128)(2,1)S(1)}, u32[]{:S(2)}, u32[]{:S(2)}) async-start(bf16[8,64,128]{2,1,0:T(8,128)(2,1)} %fusion), calls=%async_computation.1 | async-start | bytes 262144 | tf_op jit(solution)/shard_map/all_to_all | solution.py:368
  120.0 78.6 %all-gather.5.cloned.1.call-start = ((), (), s32[]{:S(2)}) async-start(), calls=%async_computation.3 | async-start | bytes 4595712 | tf_op jit(solution)/shard_map/all_gather | solution.py:381
  124.6 2.5 %copy-start.2 = (bf16[8,64,128]{2,1,0:T(8,128)(2,1)}, bf16[8,64,128]{2,1,0:T(8,128)(2,1)S(1)}, u32[]{:S(2)}) copy-start(bf16[8,64,128]{2,1,0:T(8,128)(2,1)S(1)} %all-to-all-done.1) | copy-start | bytes 393220
Sparse Core Ops, SparseCore 0:
  11.8 79.0 all-gather.2
  125.8 72.7 all-gather.4

commit v14 on v12

--- a/solution.py
+++ b/solution.py
@@ -71,12 +71,17 @@
         acc = acc * factor + jnp.dot(w.astype(jnp.bfloat16), v, preferred_element_type=jnp.float32)
         return new_top, total, acc
 
+    k = kv_ref[pl.ds(0, key_block), :HD]
+    v = kv_ref[pl.ds(0, key_block), HD:]
+    s = lax.dot_general(q, k, (((1,), (1,)), ((), ())), preferred_element_type=jnp.float32) * (SCALE * LOG2E)
+    top = jnp.max(s, axis=1, keepdims=True)
+    w = jnp.exp2(s - top)
     start_state = (
-        jnp.full((rows, 1), -1e30, jnp.float32),
-        jnp.zeros((rows, 1), jnp.float32),
-        jnp.zeros((rows, HD), jnp.float32),
-    )
-    top, total, acc = lax.fori_loop(0, steps, body, start_state, unroll=4)
+        top,
+        jnp.sum(w, axis=1, keepdims=True),
+        jnp.dot(w.astype(jnp.bfloat16), v, preferred_element_type=jnp.float32),
+    )
+    top, total, acc = lax.fori_loop(1, steps, body, start_state, unroll=True)
     attended = (acc / total).astype(out_ref.dtype)
     out_ref[...] = attended
     proj_ref[...] = jnp.dot(attended, w_ref[...], preferred_element_type=jnp.float32).astype(

time: 218 us -> 218 us (level)
  no operation moved by 1% of the time
where the time goes in v14:
time: 218 us
  waiting for transfers between devices  130 us (60%)
  Pallas kernels  36.8 us (17%)
  between operations  14.3 us (7%)
  blocking collectives  13.7 us (6%)
  starting transfers between devices  11.4 us (5%)
  other arithmetic  4.4 us (2%)
  local copies, waits for them, and re-layouts  3.92 us (2%)
  matrix products  3.62 us (2%)
    all_gather x1, waiting for transfers between devices, on_device(): lax.all_gather(packed, 'seq', axis=0, tiled=True)  60.5 us
    all_gather x1, waiting for transfers between devices, on_device(): pair_all = lax.all_gather(pair, 'seq', axis=0, tiled=True)  59.5 us
    all_gather x1, blocking collectives, on_device(): all_weights = lax.all_gather(head_weight[0], 'tm', axis=0, tiled=False)  13.7 us
    pallas_call x1, Pallas kernels, attention_key_grad(): pl.pallas_call(functools.partial(key_grad_kernel, query_block, block_stri...  12.6 us
    pallas_call x1, Pallas kernels, attention_query_grad(): pl.pallas_call(functools.partial(query_grad_kernel, key_block), grid=(row...  11 us
    pallas_call x1, Pallas kernels, attention_forward(): pl.pallas_call(functools.partial(forward_kernel, key_block), grid=(rows /...  9.25 us
    all_to_all x1, waiting for transfers between devices, on_device(): lax.all_to_all(projected.reshape(head_count, span_frames * slab_cells, ch...  6.17 us
    all_to_all x1, starting transfers between devices, on_device(): lax.all_to_all(grad_heads, 'tm', 0, 0, tiled=False).reshape(tok_local, HD)  4.74 us
  transfers between devices with their start and end apart: 5, of which 4 were waited for; matrix products, arithmetic and copies ran while one was open for 3% of the time, Pallas kernels for 10%

profile of v14, /device:TPU:2, one launch (start us, length us, event | category | flops | bytes accessed | tf_op | source)
XLA Modules:
  0.0 217.8 jit_solution(13886069836942401729)
XLA Ops:
  7.2 0.0 copy-start.7
  7.2 0.0 copy-start
  7.2 0.0 all-gather.3.cloned.1.call-start
  7.3 0.1 pad_maximum_fusion.2
  7.4 0.1 broadcast_in_dim.112
  7.4 0.1 mul.150
  7.6 0.7 fusion.25
  8.3 0.1 multiply_sine_fusion
  8.4 0.1 fusion.18
  8.5 1.0 negate_select_fusion
  9.5 0.0 copy-start.6
  9.5 2.1 shard_map.113
  11.6 0.0 all-gather.3.cloned.1.call-update
  11.6 0.0 copy-done.7
  11.6 1.9 collective-permute-start
  13.6 1.9 shard_map.112.q_ref
  15.5 0.0 copy-done
  15.5 0.7 gather_fusion
  16.2 0.7 gather_fusion.1
  16.9 0.7 gather_fusion.2
  17.6 0.1 constant_dynamic-slice_fusion
  17.7 0.0 copy-done.6
  17.7 13.7 %all_gather.10 = bf16[8,128,384]{2,1,0:T(8,128)(2,1)S(1)} all-gather(bf16[1,128,384]{2,1,0:T(8,128)(2,1)S(1)} %copy-done.6), channel_id=1, replica_groups=mesh['seq'=16,'tm'=8,'dp'=2] {'tm'}, dimensions={0}, use_global_device_ids=true | all-gather | bytes 884736 | tf_op jit(solution)/shard_map/all_gather | solution.py:333
  31.3 59.5 %all-gather.3.cloned.1.call-done.kv_ref = bf16[8192,256]{1,0:T(8,128)(2,1)} async-done(((bf16[512,256]{1,0:T(8,128)(2,1)}), bf16[8192,256]{1,0:T(8,128)(2,1)}) %all-gather.3.cloned.1.call-update) | async-done | bytes 4194320 | tf_op jit(solution)/shard_map/all_gather | solution.py:332
  90.8 0.0 copy-start.3
  90.8 9.3 %shard_map.114 = (bf16[512,128]{1,0:T(8,128)(2,1)}, f32[512,1]{1,0:T(8,128)}, bf16[512,384]{1,0:T(8,128)(2,1)}) custom-call(bf16[512,128]{1,0:T(8,128)(2,1)} %shard_map.112.q_ref, bf16[8192,256]{1,0:T(8,128)(2,1)} %all-gather.3.cloned.1.call-done.kv_ref, bf16[128,384]{1,0:T(8,128)(2,1)} %bitcast.79), custom_call_target="tpu_custom_call" | custom-call | flops 2147483648 | bytes 4456448 | tf_op jit(solution)/shard_map/pallas_call | solution.py:99
  100.1 0.0 copy-start.8
  100.1 4.7 %all-to-all-start = ((bf16[8,64,384]{2,1,0:T(8,128)(2,1)}), bf16[8,64,384]{2,1,0:T(8,128)(2,1)S(1)}, u32[]{:S(2)}, u32[]{:S(2)}) async-start(bf16[8,64,384]{2,1,0:T(8,128)(2,1)} %bitcast.73), calls=%async_computation | async-start | bytes 786432 | tf_op jit(solution)/shard_map/all_to_all | solution.py:340
  104.8 0.0 copy-done.3
  104.8 0.3 convolution_multiply_fusion.2
  105.1 0.0 collective-permute-done
  105.1 1.0 convolution_multiply_fusion.1
  106.0 6.2 %all-to-all-done = bf16[8,64,384]{2,1,0:T(8,128)(2,1)S(1)} async-done(((bf16[8,64,384]{2,1,0:T(8,128)(2,1)}), bf16[8,64,384]{2,1,0:T(8,128)(2,1)S(1)}, u32[]{:S(2)}, u32[]{:S(2)}) %all-to-all-start) | async-done | bytes 393248 | tf_op jit(solution)/shard_map/all_to_all | solution.py:340
  112.2 0.1 convert_reduce_fusion
  112.3 0.0 copy-start.5
  112.3 0.1 multiply_reduce_fusion.2
  112.4 0.1 rsqrt.15
  112.5 0.0 copy-done.8
  112.5 0.0 copy-start.4
  112.5 1.3 multiply_reduce_fusion.1
  113.8 0.0 copy-start.1
  113.9 0.1 subtract_convert_fusion
  114.0 1.0 fusion
  115.0 4.7 %all-to-all-start.1 = ((bf16[8,64,128]{2,1,0:T(8,128)(2,1)}), bf16[8,64,128]{2,1,0:T(8,128)(2,1)S(1)}, u32[]{:S(2)}, u32[]{:S(2)}) async-start(bf16[8,64,128]{2,1,0:T(8,128)(2,1)} %fusion), calls=%async_computation.1 | async-start | bytes 262144 | tf_op jit(solution)/shard_map/all_to_all | solution.py:373
  119.7 0.0 all-gather.5.cloned.1.call-start
  119.7 1.1 reduce.1
  120.8 3.6 %all-to-all-done.1 = bf16[8,64,128]{2,1,0:T(8,128)(2,1)S(1)} async-done(((bf16[8,64,128]{2,1,0:T(8,128)(2,1)}), bf16[8,64,128]{2,1,0:T(8,128)(2,1)S(1)}, u32[]{:S(2)}, u32[]{:S(2)}) %all-to-all-start.1) | async-done | bytes 131104 | tf_op jit(solution)/shard_map/all_to_all | solution.py:373
  124.4 0.0 copy-start.2
  124.4 0.0 copy-done.5
  124.4 0.2 multiply_reduce_fusion
  124.6 0.0 copy-done.4
  124.6 0.8 fusion.13
  125.4 0.0 all-gather.5.cloned.1.call-update
  125.4 0.0 copy-done.1
  125.4 0.7 slice.38.k_ref
  126.1 0.9 copy.13.delta_ref
  126.9 0.0 copy-done.2
  127.0 11.0 %shard_map.115 = bf16[512,128]{1,0:T(8,128)(2,1)} custom-call(bf16[512,128]{1,0:T(8,128)(2,1)} %shard_map.112.q_ref, bf16[512,128]{1,0:T(8,128)(2,1)} %bitcast.71, f32[512,1]{1,0:T(8,128)} %get-tuple-element.9.lse_ref, f32[512,1]{1,0:T(8,128)} %copy.13.delta_ref, bf16[8192,256]{1,0:T(8,128)(2,1)} %all-gather.3.cloned.1.call-done.kv_ref, ...), custom_call_target="tpu_custom_call" | custom-call | flops 3221225472 | bytes 4587520 | tf_op jit(solution)/shard_map/pallas_call | solution.py:152
  137.9 60.5 %all-gather.5.cloned.1.call-done.qg_ref = bf16[8448,256]{1,0:T(8,128)(2,1)} async-done(((bf16[528,256]{1,0:T(8,128)(2,1)}), bf16[8448,256]{1,0:T(8,128)(2,1)}) %all-gather.5.cloned.1.call-update) | async-done | bytes 4325392 | tf_op jit(solution)/shard_map/all_gather | solution.py:386
  198.4 12.6 %shard_map.116 = (bf16[512,128]{1,0:T(8,128)(2,1)}, bf16[512,128]{1,0:T(8,128)(2,1)}) custom-call(bf16[512,128]{1,0:T(8,128)(2,1)} %slice.38.k_ref, bf16[512,128]{1,0:T(8,128)(2,1)} %bitcast.78, bf16[8448,256]{1,0:T(8,128)(2,1)} %all-gather.5.cloned.1.call-done.qg_ref, f32[512,128]{1,0:T(8,128)} %get-tuple-element.25.cos_ref, ...), custom_call_target="tpu_custom_call" | custom-call | flops 4294967296 | bytes 4456448 | tf_op jit(solution)/shard_map/pallas_call | solution.py:209
  (20 shorter events, 0.2 us)
Async XLA Ops:
  7.2 4.5 %copy-start.7 = (bf16[2,32,768]{2,1,0:T(8,128)(2,1)S(1)}, bf16[2,32,768]{2,1,0:T(8,128)(2,1)}, u32[]{:S(2)}) copy-start(bf16[2,32,768]{2,1,0:T(8,128)(2,1)} %param.17) | copy-start | bytes 294916
  7.2 8.3 %copy-start = (s32[16]{0:T(128)S(1)}, s32[16]{0:T(128)}, u32[]{:S(2)}) copy-start(s32[16]{0:T(128)} %param.16) | copy-start | bytes 196
  7.2 83.6 %all-gather.3.cloned.1.call-start = ((), (), s32[]{:S(2)}) async-start(), calls=%async_computation.2 | async-start | bytes 4456448 | tf_op jit(solution)/shard_map/all_gather | solution.py:332
  9.5 8.1 %copy-start.6 = (bf16[1,128,384]{2,1,0:T(8,128)(2,1)S(1)}, bf16[1,128,384]{2,1,0:T(8,128)(2,1)}, u32[]{:S(2)}) copy-start(bf16[1,128,384]{2,1,0:T(8,128)(2,1)} %param.13) | copy-start | bytes 294916
  11.6 93.4 %collective-permute-start = (bf16[2,32,768]{2,1,0:T(8,128)(2,1)S(1)}, bf16[2,32,768]{2,1,0:T(8,128)(2,1)S(1)}, u32[]{:S(2)}, u32[]{:S(2)}) collective-permute-start(bf16[2,32,768]{2,1,0:T(8,128)(2,1)S(1)} %copy-done.7), channel_id=1, source_target_pairs={{2,0},{4,2},{6,4},{8,6},{10,8},{12,10},{14,12},{3,1},{5,3},{7,5},{... | collective-permute-start | bytes 294920 | tf_op jit(solution)/shard_map/ppermute | solution.py:223
  90.8 13.9 %copy-start.3 = (bf16[3,384,768]{2,1,0:T(8,128)(2,1)S(1)}, bf16[3,384,768]{2,1,0:T(8,128)(2,1)}, u32[]{:S(2)}) copy-start(bf16[3,384,768]{2,1,0:T(8,128)(2,1)} %param.15) | copy-start | bytes 5308420
  100.1 12.4 %copy-start.8 = (f32[384]{0:T(512)S(1)}, f32[384]{0:T(512)}, u32[]{:S(2)}) copy-start(f32[384]{0:T(512)} %param.14) | copy-start | bytes 4612
  100.1 12.1 %all-to-all-start = ((bf16[8,64,384]{2,1,0:T(8,128)(2,1)}), bf16[8,64,384]{2,1,0:T(8,128)(2,1)S(1)}, u32[]{:S(2)}, u32[]{:S(2)}) async-start(bf16[8,64,384]{2,1,0:T(8,128)(2,1)} %bitcast.73), calls=%async_computation | async-start | bytes 786432 | tf_op jit(solution)/shard_map/all_to_all | solution.py:340
  112.3 12.1 %copy-start.5 = (bf16[512,128]{1,0:T(8,128)(2,1)S(1)}, bf16[512,128]{1,0:T(8,128)(2,1)}, u32[]{:S(2)}) copy-start(bf16[512,128]{1,0:T(8,128)(2,1)} %get-tuple-element.10) | copy-start | bytes 393220
  112.5 12.1 %copy-start.4 = (bf16[512,128]{1,0:T(8,128)(2,1)S(1)}, bf16[512,128]{1,0:T(8,128)(2,1)}, u32[]{:S(2)}) copy-start(bf16[512,128]{1,0:T(8,128)(2,1)} %shard_map.112.q_ref) | copy-start | bytes 393220
  113.8 11.6 %copy-start.1 = (bf16[512,256]{1,0:T(8,128)(2,1)S(1)}, bf16[512,256]{1,0:T(8,128)(2,1)}, u32[]{:S(2)}) copy-start(bf16[512,256]{1,0:T(8,128)(2,1)} %shard_map.113) | copy-start | bytes 786436
  115.0 9.4 %all-to-all-start.1 = ((bf16[8,64,128]{2,1,0:T(8,128)(2,1)}), bf16[8,64,128]{2,1,0:T(8,128)(2,1)S(1)}, u32[]{:S(2)}, u32[]{:S(2)}) async-start(bf16[8,64,128]{2,1,0:T(8,128)(2,1)} %fusion), calls=%async_computation.1 | async-start | bytes 262144 | tf_op jit(solution)/shard_map/all_to_all | solution.py:373
  119.7 78.7 %all-gather.5.cloned.1.call-start = ((), (), s32[]{:S(2)}) async-start(), calls=%async_computation.3 | async-start | bytes 4595712 | tf_op jit(solution)/shard_map/all_gather | solution.py:386
  124.4 2.5 %copy-start.2 = (bf16[8,64,128]{2,1,0:T(8,128)(2,1)}, bf16[8,64,128]{2,1,0:T(8,128)(2,1)S(1)}, u32[]{:S(2)}) copy-start(bf16[8,64,128]{2,1,0:T(8,128)(2,1)S(1)} %all-to-all-done.1) | copy-start | bytes 393220
Sparse Core Ops, SparseCore 0:
  11.8 79.0 all-gather.2
  125.5 72.8 all-gather.4
